TPU v7x, 128 devices: a whole 4x4x4 slice. The times are simulated.
128 devices in a mesh: dom: 16 (over y, z), sub: 8 (over x, core).
Axes of the slice: x: 4, y: 4, z: 4, core: 2. Of those that a mesh axis runs over, the one named last changes fastest.
Arguments:
- history: bfloat16 [131072, 256], P(('dom', 'sub')), may hold values from -140 to 140
- tile_weight: bfloat16 [1024, 64, 128, 128], P(('dom', 'sub')), may hold values from 0 to 1.75, as said below
- tile_source: int32 [1024, 64], P(('dom', 'sub')), may hold values from 0 to 95
- tile_live: int32 [1024], P(('dom', 'sub')), may hold values from 8 to 64, as said below
- send_list: int32 [128, 16, 2], P(('dom', 'sub')), may hold values from 0 to 7
- degree: int32 [131072], P(('dom', 'sub')), may hold values from 16 to 64
- labels: int32 [131072], P(('dom', 'sub')), may hold values from 0 to 171
- neigh_weight: bfloat16 [256, 172], replicated, may hold values from -0.375 to 0.375
- self_weight: bfloat16 [256, 172], replicated, may hold values from -0.375 to 0.375
Outputs:
- grad_history: float32 [131072, 256], P(('dom', 'sub'))
- neigh_grad: float32 [256, 172], replicated
- self_grad: float32 [256, 172], replicated
Inputs may be any that keep to these rules, and one draw needn't show every extreme that they name: `tile_live`: every device owns a block with all 64 tiles live. `tile_weight`: nonzero entries lie within 0.25 and 1.75.
All inputs are finite; a program needn't handle non-finite values.
Results may differ from a plain program's by a relative error of at most 0.0055.
Values may be sent and summed in bfloat16 or wider, within the bound.
No kernel may reach another device: no remote copies, remote signals or barrier semaphores. Data moves between devices by JAX's collectives and lax.ppermute only.
A program may use at most 192 MiB of HBM per device.

v0:
```python
import functools

import jax
import jax.numpy as jnp
from jax import lax
from jax.experimental import pallas as pl
from jax.experimental.pallas import tpu as pltpu
from jax.sharding import PartitionSpec as P

LANES = 128


def _fused_kernel(
    src_ref,
    live_ref,
    w_ref,
    sources_ref,
    hist_ref,
    deg_ref,
    lab_ref,
    nw_ref,
    sw_ref,
    swt_ref,
    term_ref,
    grads_ref,
    selfterm_ref,
    *,
    classes,
):
    b = pl.program_id(0)
    rows = w_ref.shape[2]
    width = sources_ref.shape[2]
    padded = nw_ref.shape[1]

    @pl.when(b == 0)
    def _():
        term_ref[...] = jnp.zeros_like(term_ref)
        grads_ref[...] = jnp.zeros_like(grads_ref)

    live = live_ref[b]

    def forward(t, acc):
        s = src_ref[b, t]
        return acc + jnp.dot(w_ref[0, t], sources_ref[s], preferred_element_type=jnp.float32)

    acc = lax.fori_loop(0, live, forward, jnp.zeros((rows, width), jnp.float32))
    deg = deg_ref[0]
    aggregate = (acc / deg).astype(jnp.bfloat16)
    own = hist_ref[0]
    logits = jnp.dot(aggregate, nw_ref[...], preferred_element_type=jnp.float32) + jnp.dot(
        own, sw_ref[...], preferred_element_type=jnp.float32
    )
    col = lax.broadcasted_iota(jnp.int32, (rows, padded), 1)
    logits = jnp.where(col < classes, logits, -1e30)
    top = jnp.max(logits, axis=-1, keepdims=True)
    expd = jnp.exp(logits - top)
    predicted = expd / jnp.sum(expd, axis=-1, keepdims=True)
    onehot = (col == lab_ref[0]).astype(jnp.float32)
    residual = predicted - onehot
    delta = residual.astype(jnp.bfloat16)
    tn = (((0,), (0,)), ((), ()))
    grads_ref[0] += lax.dot_general(aggregate, delta, tn, preferred_element_type=jnp.float32)
    grads_ref[1] += lax.dot_general(own, delta, tn, preferred_element_type=jnp.float32)
    selfterm_ref[0] = jnp.dot(delta, swt_ref[...], preferred_element_type=jnp.float32)
    scaled = (residual / deg).astype(jnp.bfloat16)

    def backward(t, carry):
        s = src_ref[b, t]
        term_ref[s] += lax.dot_general(w_ref[0, t], scaled, tn, preferred_element_type=jnp.float32)
        return carry

    lax.fori_loop(0, live, backward, 0)


def _fused(tile_source, tile_live, tile_weight, sources, own_blocks, deg, lab, nw, sw, swt, classes):
    block_count, tile_slots, rows, _ = tile_weight.shape
    source_total, _, width = sources.shape
    padded = nw.shape[1]
    vmem = pltpu.MemorySpace.VMEM if hasattr(pltpu, "MemorySpace") else pltpu.VMEM
    grid_spec = pltpu.PrefetchScalarGridSpec(
        num_scalar_prefetch=2,
        grid=(block_count,),
        in_specs=[
            pl.BlockSpec((1, tile_slots, rows, rows), lambda b, *_: (b, 0, 0, 0)),
            pl.BlockSpec(memory_space=vmem),
            pl.BlockSpec((1, rows, width), lambda b, *_: (b, 0, 0)),
            pl.BlockSpec((1, rows, 1), lambda b, *_: (b, 0, 0)),
            pl.BlockSpec((1, rows, 1), lambda b, *_: (b, 0, 0)),
            pl.BlockSpec(memory_space=vmem),
            pl.BlockSpec(memory_space=vmem),
            pl.BlockSpec(memory_space=vmem),
        ],
        out_specs=[
            pl.BlockSpec(memory_space=vmem),
            pl.BlockSpec(memory_space=vmem),
            pl.BlockSpec((1, rows, width), lambda b, *_: (b, 0, 0)),
        ],
    )
    return pl.pallas_call(
        functools.partial(_fused_kernel, classes=classes),
        grid_spec=grid_spec,
        out_shape=[
            jax.ShapeDtypeStruct((source_total, rows, padded), jnp.float32),
            jax.ShapeDtypeStruct((2, width, padded), jnp.float32),
            jax.ShapeDtypeStruct((block_count, rows, width), jnp.float32),
        ],
        compiler_params=pltpu.CompilerParams(
            dimension_semantics=("arbitrary",), vmem_limit_bytes=56 * 1024 * 1024
        ),
    )(tile_source, tile_live, tile_weight, sources, own_blocks, deg, lab, nw, sw, swt)


def per_device(
    history,
    tile_weight,
    tile_source,
    tile_live,
    send_list,
    degree,
    labels,
    neigh_weight,
    self_weight,
):
    block_count = tile_weight.shape[0]
    block_rows = tile_weight.shape[2]
    width = history.shape[1]
    classes = neigh_weight.shape[1]
    dom_count = lax.axis_size("dom")
    sub_count = lax.axis_size("sub")
    devices_all = dom_count * sub_count
    nodes_all = history.shape[0] * devices_all
    padded = -(-classes // LANES) * LANES
    own_blocks = history.reshape(block_count, block_rows, width)
    partition = lax.all_gather(own_blocks, "sub", axis=0, tiled=True)
    part_blocks = partition.shape[0]
    own_ids = jnp.arange(block_count, dtype=jnp.int32)
    send_table = send_list[0][:, :, None] == own_ids[None, None, :]
    outgoing = jnp.einsum(
        "pks,sif->pkif",
        send_table.astype(jnp.bfloat16),
        own_blocks,
        preferred_element_type=jnp.float32,
    ).astype(jnp.bfloat16)
    boundary = lax.all_to_all(outgoing, "dom", split_axis=0, concat_axis=0, tiled=True)
    slot_count = boundary.shape[1]
    sources = jnp.concatenate(
        [partition, boundary.reshape(dom_count * slot_count, block_rows, width)], axis=0
    )
    degrees = degree.astype(jnp.float32).reshape(block_count, block_rows, 1)
    lab = labels.reshape(block_count, block_rows, 1)
    pad_cols = ((0, 0), (0, padded - classes))
    nw = jnp.pad(neigh_weight, pad_cols)
    sw = jnp.pad(self_weight, pad_cols)
    swt = jnp.pad(self_weight.T, ((0, padded - classes), (0, 0)))
    term, grads, selfterm = _fused(
        tile_source, tile_live, tile_weight, sources, own_blocks, degrees, lab, nw, sw, swt, classes
    )

    flat = grads[:, :, :classes].reshape(devices_all, -1)
    mine = lax.all_to_all(flat, ("dom", "sub"), 0, 0, tiled=True).sum(axis=0, keepdims=True)
    spread = jnp.broadcast_to(mine, (devices_all, mine.shape[1]))
    totals = lax.all_to_all(spread, ("dom", "sub"), 0, 0, tiled=True).reshape(2, width, classes)
    norm_factor = float(nodes_all) ** (-0.5)

    local = term[:part_blocks, :, :classes].astype(jnp.bfloat16)
    local = local.reshape(sub_count, block_count, block_rows, classes)
    local_grad = (
        lax.all_to_all(local, "sub", 0, 0, tiled=True).astype(jnp.float32).sum(axis=0)
    )
    halo = term[part_blocks:, :, :classes].astype(jnp.bfloat16)
    halo = halo.reshape(dom_count, slot_count, block_rows, classes)
    arrived = lax.all_to_all(halo, "dom", 0, 0, tiled=True).astype(jnp.float32)
    return_table = send_table.astype(jnp.float32)
    incoming = jnp.einsum("pks,pkic->sic", return_table, arrived, precision=lax.Precision.HIGHEST)
    backward_sum = (local_grad + incoming).reshape(-1, classes)
    neigh_float = neigh_weight.astype(jnp.float32)
    grad_history = jnp.dot(
        backward_sum, neigh_float.T, precision=lax.Precision.HIGHEST
    ) + selfterm.reshape(-1, width)
    return (grad_history, totals[0] * norm_factor, totals[1] * norm_factor)


def solution(mesh):
    placed = (
        P(("dom", "sub"), None),
        P(("dom", "sub"), None, None, None),
        P(("dom", "sub"), None),
        P(("dom", "sub")),
        P(("dom", "sub"), None, None),
        P(("dom", "sub")),
        P(("dom", "sub")),
        P(),
        P(),
    )
    return jax.shard_map(
        per_device,
        mesh=mesh,
        in_specs=placed,
        out_specs=(P(("dom", "sub"), None), P(), P()),
        check_vma=False,
    )
```

profile of v0, /device:TPU:1, one launch (start us, length us, event | category | flops | bytes accessed | tf_op | source)
XLA Modules:
  0.0 356.3 jit_solution(5759339594073356304)
XLA Ops:
  7.2 0.0 all-gather.2.cloned.1.call-start
  7.2 0.7 all-gather.2.cloned.1.call-update
  7.9 1.8 convolution_convert_fusion
  9.7 2.0 copy.27
  11.7 0.0 copy-start.2
  11.7 0.0 copy-start.4
  11.7 0.0 copy-start.7
  11.8 0.0 copy-start.6
  11.8 8.7 %all-to-all-start = ((bf16[16,2,128,256]{3,2,1,0:T(8,128)(2,1)}), bf16[16,2,128,256]{3,2,1,0:T(8,128)(2,1)S(1)}, u32[]{:S(2)}, u32[]{:S(2)}) async-start(bf16[16,2,128,256]{3,2,1,0:T(8,128)(2,1)} %copy.27), calls=%async_computation | async-start | bytes 4194304 | tf_op jit(solution)/shard_map/all_to_all | solution.py:144
  20.5 0.0 copy-done.2
  20.5 0.1 copy.28
  20.6 0.0 copy-done.4
  20.6 0.1 copy.29
  20.7 0.7 pad.13.swt_ref
  21.4 0.7 pad.11.nw_ref
  22.1 0.7 pad.12.sw_ref
  22.7 0.0 copy-done.7
  22.7 1.0 copy.30.deg_ref
  23.8 0.0 copy-done.6
  23.8 1.0 copy.31.lab_ref
  24.8 23.8 %all-to-all-done = bf16[16,2,128,256]{3,2,1,0:T(8,128)(2,1)S(1)} async-done(((bf16[16,2,128,256]{3,2,1,0:T(8,128)(2,1)}), bf16[16,2,128,256]{3,2,1,0:T(8,128)(2,1)S(1)}, u32[]{:S(2)}, u32[]{:S(2)}) %all-to-all-start) | async-done | bytes 2097184 | tf_op jit(solution)/shard_map/all_to_all | solution.py:144
  48.6 0.0 all-gather.2.cloned.1.call-done
  48.6 5.3 %pad_maximum_fusion.sources_ref = bf16[96,128,256]{2,1,0:T(8,128)(2,1)} fusion(bf16[32,128,256]{2,1,0:T(8,128)(2,1)S(1)} %bitcast.38, bf16[64,128,256]{2,1,0:T(8,128)(2,1)} %all-gather.2.cloned.1.call-done), kind=kLoop, calls=%fused_computation | loop fusion | flops 3145728 | bytes 12582912 | tf_op jit(solution)/shard_map/concatenate | solution.py:146
  54.0 136.1 %shard_map.112 = (f32[96,128,256]{2,1,0:T(8,128)}, f32[2,256,256]{2,1,0:T(8,128)}, f32[8,128,256]{2,1,0:T(8,128)}) custom-call(s32[8,64]{1,0:T(8,128)} %src_ref.1, s32[8]{0:T(128)} %live_ref.1, bf16[8,64,128,128]{3,2,1,0:T(8,128)(2,1)} %w_ref.1, bf16[96,128,256]{2,1,0:T(8,128)(2,1)} %pad_maximum_fusion.sources_ref, bf16[8,128,256]{2,1,0:T(8,128)(2,1)} %bitcast.41, ...), custom_call_target="tpu_custom_call" | custom-call | tf_op jit(solution)/shard_map/pallas_call | solution.py:99
  190.1 1.8 all_to_all.25
  191.9 66.6 %all_to_all.31 = f32[128,1,688]{2,1,0:T(1,128)S(1)} all-to-all(f32[128,1,688]{2,1,0:T(1,128)S(1)} %all_to_all.25), channel_id=1, replica_groups=mesh['dom'=16,'sub'=8] {'dom','sub'}, dimensions={0} | all-to-all | bytes 704512 | tf_op jit(solution)/shard_map/all_to_all | solution.py:160
  258.5 0.3 reduce_sum.19
  258.8 1.0 broadcast_in_dim.2
  259.8 4.6 %all-to-all-start.4 = ((f32[128,1,688]{2,1,0:T(1,128)}), f32[128,1,688]{2,1,0:T(1,128)S(1)}, u32[]{:S(2)}, u32[]{:S(2)}) async-start(f32[128,1,688]{2,1,0:T(1,128)} %broadcast_in_dim.2), calls=%async_computation.4 | async-start | bytes 786432 | tf_op jit(solution)/shard_map/all_to_all | solution.py:162
  264.4 5.5 %convert.4 = bf16[96,128,256]{2,1,0:T(8,128)(2,1)S(1)} convert(f32[96,128,256]{2,1,0:T(8,128)} %get-tuple-element.6) | non-fusion elementwise | flops 3145728 | bytes 18874368 | tf_op jit(solution)/shard_map/convert.1
  270.0 0.0 copy-start
  270.0 2.5 slice.26
  272.4 1.5 copy-done
  274.0 6.4 %copy.32 = bf16[8,8,128,172]{2,1,3,0:T(8,128)(2,1)} copy(bf16[8,8,128,172]{3,2,1,0:T(8,128)(2,1)} %bitcast.36) | data formatting | bytes 5636096 | tf_op jit(solution)/shard_map/reshape | solution.py:166
  280.4 0.0 all-to-all-done.4
  280.4 4.8 %all-to-all-start.1 = ((bf16[8,8,128,172]{2,1,3,0:T(8,128)(2,1)}), bf16[8,8,128,172]{2,1,3,0:T(8,128)(2,1)S(1)}, u32[]{:S(2)}, u32[]{:S(2)}) async-start(bf16[8,8,128,172]{2,1,3,0:T(8,128)(2,1)} %copy.32), calls=%async_computation.1 | async-start | bytes 5636096 | tf_op jit(solution)/shard_map/all_to_all | solution.py:168
  285.2 3.2 slice.27
  288.4 5.1 %copy.34 = bf16[16,2,128,172]{2,1,3,0:T(2,128)(2,1)} copy(bf16[16,2,128,172]{3,2,1,0:T(8,128)(2,1)} %bitcast.37) | data formatting | bytes 2818048 | tf_op jit(solution)/shard_map/reshape | solution.py:171
  293.5 25.7 %all-to-all-done.1 = bf16[8,8,128,172]{2,1,3,0:T(8,128)(2,1)S(1)} async-done(((bf16[8,8,128,172]{2,1,3,0:T(8,128)(2,1)}), bf16[8,8,128,172]{2,1,3,0:T(8,128)(2,1)S(1)}, u32[]{:S(2)}, u32[]{:S(2)}) %all-to-all-start.1) | async-done | bytes 2818080 | tf_op jit(solution)/shard_map/all_to_all | solution.py:168
  319.1 7.1 %all-to-all-start.2 = ((bf16[16,2,128,172]{2,1,3,0:T(2,128)(2,1)}), bf16[16,2,128,172]{2,1,3,0:T(2,128)(2,1)}, u32[]{:S(2)}, u32[]{:S(2)}) async-start(bf16[16,2,128,172]{2,1,3,0:T(2,128)(2,1)} %copy.34), calls=%async_computation.2 | async-start | bytes 2818048 | tf_op jit(solution)/shard_map/all_to_all | solution.py:172
  326.2 1.8 fusion.13
  328.1 0.0 copy-start.5
  328.1 1.1 mul.15
  329.1 0.8 copy.39
  329.9 1.1 mul.13
  331.0 0.8 copy.38
  331.8 0.4 convert_reduce_fusion
  332.2 0.0 copy-start.1
  332.2 0.0 copy-start.3
  332.2 13.2 %all-to-all-done.2 = bf16[16,2,128,172]{2,1,3,0:T(2,128)(2,1)} async-done(((bf16[16,2,128,172]{2,1,3,0:T(2,128)(2,1)}), bf16[16,2,128,172]{2,1,3,0:T(2,128)(2,1)}, u32[]{:S(2)}, u32[]{:S(2)}) %all-to-all-start.2) | async-done | bytes 1409056 | tf_op jit(solution)/shard_map/all_to_all | solution.py:172
  345.5 0.0 copy-done.5
  345.5 1.7 fusion.8
  347.2 0.1 copy.43
  347.4 0.0 copy-done.1
  347.4 0.0 copy-done.3
  347.4 2.0 convolution_add_fusion
  (2 shorter events, 0.1 us)
Async XLA Ops:
  7.2 41.5 %all-gather.2.cloned.1.call-start = ((), (), s32[]{:S(2)}) async-start(), calls=%async_computation.5 | async-start | bytes 4718592 | tf_op jit(solution)/shard_map/all_gather | solution.py:134
  11.7 8.7 %copy-start.2 = (bf16[256,172]{0,1:T(8,128)(2,1)S(1)}, bf16[256,172]{0,1:T(8,128)(2,1)}, u32[]{:S(2)}) copy-start(bf16[256,172]{0,1:T(8,128)(2,1)} %param.16) | copy-start | bytes 264196
  11.7 8.9 %copy-start.4 = (bf16[256,172]{0,1:T(8,128)(2,1)S(1)}, bf16[256,172]{0,1:T(8,128)(2,1)}, u32[]{:S(2)}) copy-start(bf16[256,172]{0,1:T(8,128)(2,1)} %param.17) | copy-start | bytes 264196
  11.7 11.0 %copy-start.7 = (s32[1024]{0:T(1024)S(1)}, s32[1024]{0:T(1024)}, u32[]{:S(2)}) copy-start(s32[1024]{0:T(1024)} %param.14) | copy-start | bytes 12292
  11.8 12.0 %copy-start.6 = (s32[1024]{0:T(1024)S(1)}, s32[1024]{0:T(1024)}, u32[]{:S(2)}) copy-start(s32[1024]{0:T(1024)} %param.15) | copy-start | bytes 12292
  11.8 36.9 %all-to-all-start = ((bf16[16,2,128,256]{3,2,1,0:T(8,128)(2,1)}), bf16[16,2,128,256]{3,2,1,0:T(8,128)(2,1)S(1)}, u32[]{:S(2)}, u32[]{:S(2)}) async-start(bf16[16,2,128,256]{3,2,1,0:T(8,128)(2,1)} %copy.27), calls=%async_computation | async-start | bytes 4194304 | tf_op jit(solution)/shard_map/all_to_all | solution.py:144
  259.8 20.6 %all-to-all-start.4 = ((f32[128,1,688]{2,1,0:T(1,128)}), f32[128,1,688]{2,1,0:T(1,128)S(1)}, u32[]{:S(2)}, u32[]{:S(2)}) async-start(f32[128,1,688]{2,1,0:T(1,128)} %broadcast_in_dim.2), calls=%async_computation.4 | async-start | bytes 786432 | tf_op jit(solution)/shard_map/all_to_all | solution.py:162
  270.0 4.0 %copy-start = (bf16[96,128,256]{2,1,0:T(8,128)(2,1)}, bf16[96,128,256]{2,1,0:T(8,128)(2,1)S(1)}, u32[]{:S(2)}) copy-start(bf16[96,128,256]{2,1,0:T(8,128)(2,1)S(1)} %convert.4) | copy-start | bytes 18874372
  280.4 38.7 %all-to-all-start.1 = ((bf16[8,8,128,172]{2,1,3,0:T(8,128)(2,1)}), bf16[8,8,128,172]{2,1,3,0:T(8,128)(2,1)S(1)}, u32[]{:S(2)}, u32[]{:S(2)}) async-start(bf16[8,8,128,172]{2,1,3,0:T(8,128)(2,1)} %copy.32), calls=%async_computation.1 | async-start | bytes 5636096 | tf_op jit(solution)/shard_map/all_to_all | solution.py:168
  319.1 26.3 %all-to-all-start.2 = ((bf16[16,2,128,172]{2,1,3,0:T(2,128)(2,1)}), bf16[16,2,128,172]{2,1,3,0:T(2,128)(2,1)}, u32[]{:S(2)}, u32[]{:S(2)}) async-start(bf16[16,2,128,172]{2,1,3,0:T(2,128)(2,1)} %copy.34), calls=%async_computation.2 | async-start | bytes 2818048 | tf_op jit(solution)/shard_map/all_to_all | solution.py:172
  328.1 17.4 %copy-start.5 = (s32[1,16,2]{1,2,0:T(2,128)S(1)}, s32[1,16,2]{1,2,0:T(2,128)}, u32[]{:S(2)}) copy-start(s32[1,16,2]{1,2,0:T(2,128)} %param.13) | copy-start | bytes 388
  332.2 15.2 %copy-start.1 = (f32[8,128,256]{2,1,0:T(8,128)S(1)}, f32[8,128,256]{2,1,0:T(8,128)}, u32[]{:S(2)}) copy-start(f32[8,128,256]{2,1,0:T(8,128)} %get-tuple-element.7) | copy-start | bytes 3145732
  332.2 15.2 %copy-start.3 = (bf16[256,172]{0,1:T(8,128)(2,1)S(1)}, bf16[256,172]{0,1:T(8,128)(2,1)}, u32[]{:S(2)}) copy-start(bf16[256,172]{0,1:T(8,128)(2,1)} %param.16) | copy-start | bytes 264196
Sparse Core Ops, SparseCore 0:
  9.7 35.6 all-gather.1
where the time goes:
time: 355 us; the launch traced here: 356 us
  Pallas kernels  136 us (38%)
  blocking collectives  66.6 us (19%)
  waiting for transfers between devices  63.4 us (18%)
  local copies, waits for them, and re-layouts  31.7 us (9%)
  starting transfers between devices  25.3 us (7%)
  between operations  14.2 us (4%)
  other arithmetic  13.4 us (4%)
  matrix products  5.54 us (2%)
    pallas_call x1, Pallas kernels, _fused(): pl.pallas_call(functools.partial(_fused_kernel, classes=classes), grid_sp...  136 us
    all_to_all x1, blocking collectives, per_device(): lax.all_to_all(flat, ('dom', 'sub'), 0, 0, tiled=True)  66.6 us
    all_to_all x1, waiting for transfers between devices, per_device(): lax.all_to_all(local, 'sub', 0, 0, tiled=True).astype(jnp.float32)  25.7 us
    all_to_all x1, waiting for transfers between devices, per_device(): lax.all_to_all(outgoing, 'dom', split_axis=0, concat_axis=0, tiled=True)  23.8 us
    all_to_all x1, waiting for transfers between devices, per_device(): arrived = lax.all_to_all(halo, 'dom', 0, 0, tiled=True).astype(jnp.float32)  13.2 us
    all_to_all x1, starting transfers between devices, per_device(): lax.all_to_all(outgoing, 'dom', split_axis=0, concat_axis=0, tiled=True)  8.72 us
  transfers between devices with their start and end apart: 5, of which 3 were waited for; matrix products, arithmetic and copies ran while one was open for 10% of the time, Pallas kernels for 0%

commit v1 on v0

--- a/solution.py
+++ b/solution.py
@@ -8,6 +8,7 @@
 from jax.sharding import PartitionSpec as P
 
 LANES = 128
+GROUP = 8
 
 
 def _fused_kernel(
@@ -38,12 +39,18 @@
         grads_ref[...] = jnp.zeros_like(grads_ref)
 
     live = live_ref[b]
-
-    def forward(t, acc):
-        s = src_ref[b, t]
-        return acc + jnp.dot(w_ref[0, t], sources_ref[s], preferred_element_type=jnp.float32)
-
-    acc = lax.fori_loop(0, live, forward, jnp.zeros((rows, width), jnp.float32))
+    groups = (live + GROUP - 1) // GROUP
+
+    def tile(t):
+        return jnp.where(t < live, w_ref[0, t], jnp.zeros_like(w_ref[0, t]))
+
+    def forward(g, acc):
+        for k in range(GROUP):
+            t = g * GROUP + k
+            acc = acc + jnp.dot(tile(t), sources_ref[src_ref[b, t]], preferred_element_type=jnp.float32)
+        return acc
+
+    acc = lax.fori_loop(0, groups, forward, jnp.zeros((rows, width), jnp.float32))
     deg = deg_ref[0]
     aggregate = (acc / deg).astype(jnp.bfloat16)
     own = hist_ref[0]
@@ -62,14 +69,16 @@
     grads_ref[0] += lax.dot_general(aggregate, delta, tn, preferred_element_type=jnp.float32)
     grads_ref[1] += lax.dot_general(own, delta, tn, preferred_element_type=jnp.float32)
     selfterm_ref[0] = jnp.dot(delta, swt_ref[...], preferred_element_type=jnp.float32)
-    scaled = (residual / deg).astype(jnp.bfloat16)
-
-    def backward(t, carry):
-        s = src_ref[b, t]
-        term_ref[s] += lax.dot_general(w_ref[0, t], scaled, tn, preferred_element_type=jnp.float32)
+    scaled_t = (residual / deg).astype(jnp.bfloat16).T
+
+    def backward(g, carry):
+        for k in range(GROUP):
+            t = g * GROUP + k
+            s = src_ref[b, t]
+            term_ref[s] += jnp.dot(scaled_t, tile(t), preferred_element_type=jnp.float32)
         return carry
 
-    lax.fori_loop(0, live, backward, 0)
+    lax.fori_loop(0, groups, backward, 0)
 
 
 def _fused(tile_source, tile_live, tile_weight, sources, own_blocks, deg, lab, nw, sw, swt, classes):
@@ -100,7 +109,7 @@
         functools.partial(_fused_kernel, classes=classes),
         grid_spec=grid_spec,
         out_shape=[
-            jax.ShapeDtypeStruct((source_total, rows, padded), jnp.float32),
+            jax.ShapeDtypeStruct((source_total, padded, rows), jnp.float32),
             jax.ShapeDtypeStruct((2, width, padded), jnp.float32),
             jax.ShapeDtypeStruct((block_count, rows, width), jnp.float32),
         ],
@@ -162,21 +171,21 @@
     totals = lax.all_to_all(spread, ("dom", "sub"), 0, 0, tiled=True).reshape(2, width, classes)
     norm_factor = float(nodes_all) ** (-0.5)
 
-    local = term[:part_blocks, :, :classes].astype(jnp.bfloat16)
-    local = local.reshape(sub_count, block_count, block_rows, classes)
+    local = term[:part_blocks, :classes].astype(jnp.bfloat16)
+    local = local.reshape(sub_count, block_count, classes, block_rows)
     local_grad = (
         lax.all_to_all(local, "sub", 0, 0, tiled=True).astype(jnp.float32).sum(axis=0)
     )
-    halo = term[part_blocks:, :, :classes].astype(jnp.bfloat16)
-    halo = halo.reshape(dom_count, slot_count, block_rows, classes)
+    halo = term[part_blocks:, :classes].astype(jnp.bfloat16)
+    halo = halo.reshape(dom_count, slot_count, classes, block_rows)
     arrived = lax.all_to_all(halo, "dom", 0, 0, tiled=True).astype(jnp.float32)
     return_table = send_table.astype(jnp.float32)
-    incoming = jnp.einsum("pks,pkic->sic", return_table, arrived, precision=lax.Precision.HIGHEST)
-    backward_sum = (local_grad + incoming).reshape(-1, classes)
+    incoming = jnp.einsum("pks,pkci->sci", return_table, arrived, precision=lax.Precision.HIGHEST)
+    backward_sum = local_grad + incoming
     neigh_float = neigh_weight.astype(jnp.float32)
-    grad_history = jnp.dot(
-        backward_sum, neigh_float.T, precision=lax.Precision.HIGHEST
-    ) + selfterm.reshape(-1, width)
+    grad_history = jnp.einsum(
+        "sci,fc->sif", backward_sum, neigh_float, precision=lax.Precision.HIGHEST
+    ).reshape(-1, width) + selfterm.reshape(-1, width)
     return (grad_history, totals[0] * norm_factor, totals[1] * norm_factor)
 
 

time: 355 us -> 221 us (0.62); the launches traced: 356 us -> 218 us
  Pallas kernels: 136 us -> 40.9 us
  blocking collectives: 66.6 us -> 28.7 us
  local copies, waits for them, and re-layouts: 31.7 us -> 21.7 us
  waiting for transfers between devices: 63.4 us -> 69.1 us
    pallas_call x1, Pallas kernels: 136 us -> 40.9 us  [_fused(): pl.pallas_call(functools.partial(_fused_kernel, classes=classes), grid_sp...]
    all_to_all x1, blocking collectives: 66.6 us -> 28.7 us  [per_device(): lax.all_to_all(flat, ('dom', 'sub'), 0, 0, tiled=True)]
    reshape x2, local copies, waits for them, and re-layouts: 11.5 us -> 4.52 us  [the longest x1 2.33 us: per_device(): local = local.reshape(sub_count, block_count, classes, block_rows)]
    all_to_all x1, waiting for transfers between devices: 25.7 us -> 30.3 us  [per_device(): lax.all_to_all(local, 'sub', 0, 0, tiled=True).astype(jnp.float32)]
    slice x2, local copies, waits for them, and re-layouts: 5.63 us -> 1.69 us  [the longest x1 1.46 us: per_device(): halo = term[part_blocks:, :classes].astype(jnp.bfloat16)]
  transfers between devices with their start and end apart: 5 -> 5, of which waited for: 3 -> 4; matrix products, arithmetic and copies ran while one was open for 10% -> 12% of each run, Pallas kernels for 0% -> 0%
where the time goes in v1:
time: 221 us; the launch traced here: 218 us
  waiting for transfers between devices  69.1 us (31%)
  Pallas kernels  40.9 us (19%)
  blocking collectives  28.7 us (13%)
  starting transfers between devices  24.2 us (11%)
  local copies, waits for them, and re-layouts  21.7 us (10%)
  between operations  14.2 us (6%)
  other arithmetic  13.8 us (6%)
  matrix products  5.56 us (3%)
    pallas_call x1, Pallas kernels, _fused(): pl.pallas_call(functools.partial(_fused_kernel, classes=classes), grid_sp...  40.9 us
    all_to_all x1, waiting for transfers between devices, per_device(): lax.all_to_all(local, 'sub', 0, 0, tiled=True).astype(jnp.float32)  30.3 us
    all_to_all x1, blocking collectives, per_device(): lax.all_to_all(flat, ('dom', 'sub'), 0, 0, tiled=True)  28.7 us
    all_to_all x1, waiting for transfers between devices, per_device(): lax.all_to_all(outgoing, 'dom', split_axis=0, concat_axis=0, tiled=True)  23.8 us
    all_to_all x1, waiting for transfers between devices, per_device(): arrived = lax.all_to_all(halo, 'dom', 0, 0, tiled=True).astype(jnp.float32)  13.2 us
    all_to_all x1, starting transfers between devices, per_device(): lax.all_to_all(outgoing, 'dom', split_axis=0, concat_axis=0, tiled=True)  8.72 us
    all_to_all x1, starting transfers between devices, per_device(): arrived = lax.all_to_all(halo, 'dom', 0, 0, tiled=True).astype(jnp.float32)  6.31 us
    another operation x1, other arithmetic  5.91 us
  transfers between devices with their start and end apart: 5, of which 4 were waited for; matrix products, arithmetic and copies ran while one was open for 12% of the time, Pallas kernels for 0%

profile of v1, /device:TPU:1, one launch (start us, length us, event | category | flops | bytes accessed | tf_op | source)
XLA Modules:
  0.0 218.2 jit_solution(8426354325189175820)
XLA Ops:
  7.2 0.0 all-gather.2.cloned.1.call-start
  7.2 0.7 all-gather.2.cloned.1.call-update
  7.9 1.8 convolution_convert_fusion
  9.7 2.0 copy.25
  11.7 0.0 copy-start.2
  11.7 0.0 copy-start.4
  11.7 0.0 copy-start.7
  11.8 0.0 copy-start.6
  11.8 8.7 %all-to-all-start = ((bf16[16,2,128,256]{3,2,1,0:T(8,128)(2,1)}), bf16[16,2,128,256]{3,2,1,0:T(8,128)(2,1)S(1)}, u32[]{:S(2)}, u32[]{:S(2)}) async-start(bf16[16,2,128,256]{3,2,1,0:T(8,128)(2,1)} %copy.25), calls=%async_computation | async-start | bytes 4194304 | tf_op jit(solution)/shard_map/all_to_all | solution.py:153
  20.5 0.0 copy-done.2
  20.5 0.1 copy.26
  20.6 0.0 copy-done.4
  20.6 0.1 copy.27
  20.7 0.7 pad.13.swt_ref
  21.4 0.7 pad.11.nw_ref
  22.1 0.7 pad.12.sw_ref
  22.7 0.0 copy-done.7
  22.7 1.0 copy.28.deg_ref
  23.8 0.0 copy-done.6
  23.8 1.0 copy.29.lab_ref
  24.8 23.8 %all-to-all-done = bf16[16,2,128,256]{3,2,1,0:T(8,128)(2,1)S(1)} async-done(((bf16[16,2,128,256]{3,2,1,0:T(8,128)(2,1)}), bf16[16,2,128,256]{3,2,1,0:T(8,128)(2,1)S(1)}, u32[]{:S(2)}, u32[]{:S(2)}) %all-to-all-start) | async-done | bytes 2097184 | tf_op jit(solution)/shard_map/all_to_all | solution.py:153
  48.6 0.0 all-gather.2.cloned.1.call-done
  48.6 5.3 %pad_maximum_fusion.sources_ref = bf16[96,128,256]{2,1,0:T(8,128)(2,1)} fusion(bf16[32,128,256]{2,1,0:T(8,128)(2,1)S(1)} %bitcast.30, bf16[64,128,256]{2,1,0:T(8,128)(2,1)} %all-gather.2.cloned.1.call-done), kind=kLoop, calls=%fused_computation | loop fusion | flops 3145728 | bytes 12582912 | tf_op jit(solution)/shard_map/concatenate | solution.py:155
  54.0 40.9 %shard_map.112 = (f32[96,256,128]{2,1,0:T(8,128)}, f32[2,256,256]{2,1,0:T(8,128)}, f32[8,128,256]{2,1,0:T(8,128)}) custom-call(s32[8,64]{1,0:T(8,128)} %src_ref.1, s32[8]{0:T(128)} %live_ref.1, bf16[8,64,128,128]{3,2,1,0:T(8,128)(2,1)} %w_ref.1, bf16[96,128,256]{2,1,0:T(8,128)(2,1)} %pad_maximum_fusion.sources_ref, bf16[8,128,256]{2,1,0:T(8,128)(2,1)} %bitcast.34, ...), custom_call_target="tpu_custom_call" | custom-call | tf_op jit(solution)/shard_map/pallas_call | solution.py:108
  94.9 1.8 all_to_all.25
  96.7 28.7 %all_to_all.31 = f32[128,1,688]{2,1,0:T(1,128)S(1)} all-to-all(f32[128,1,688]{2,1,0:T(1,128)S(1)} %all_to_all.25), channel_id=1, replica_groups=mesh['dom'=16,'sub'=8] {'dom','sub'}, dimensions={0} | all-to-all | bytes 704512 | tf_op jit(solution)/shard_map/all_to_all | solution.py:169
  125.4 0.3 reduce_sum.19
  125.7 1.0 broadcast_in_dim.2
  126.7 4.6 %all-to-all-start.4 = ((f32[128,1,688]{2,1,0:T(1,128)}), f32[128,1,688]{2,1,0:T(1,128)S(1)}, u32[]{:S(2)}, u32[]{:S(2)}) async-start(f32[128,1,688]{2,1,0:T(1,128)} %broadcast_in_dim.2), calls=%async_computation.4 | async-start | bytes 786432 | tf_op jit(solution)/shard_map/all_to_all | solution.py:171
  131.4 5.9 %convert.4 = bf16[96,256,128]{2,1,0:T(8,128)(2,1)S(1)} convert(f32[96,256,128]{2,1,0:T(8,128)} %get-tuple-element.6) | non-fusion elementwise | flops 3145728 | bytes 18874368 | tf_op jit(solution)/shard_map/convert.1
  137.3 0.0 copy-start
  137.3 2.7 %copy-done = bf16[96,256,128]{2,1,0:T(8,128)(2,1)} copy-done((bf16[96,256,128]{2,1,0:T(8,128)(2,1)}, bf16[96,256,128]{2,1,0:T(8,128)(2,1)S(1)}, u32[]{:S(2)}) %copy-start) | copy-done | bytes 6291480
  139.9 0.2 slice.26
  140.2 2.3 %copy.30 = bf16[8,8,172,128]{3,1,2,0:T(8,128)(2,1)} copy(bf16[8,8,172,128]{3,2,1,0:T(8,128)(2,1)S(1)} %bitcast.29) | data formatting | bytes 5636096 | tf_op jit(solution)/shard_map/reshape | solution.py:175
  142.5 1.0 all-to-all-done.4
  143.6 4.5 %all-to-all-start.1 = ((bf16[8,8,172,128]{3,1,2,0:T(8,128)(2,1)}), bf16[8,8,172,128]{3,1,2,0:T(8,128)(2,1)S(1)}, u32[]{:S(2)}, u32[]{:S(2)}) async-start(bf16[8,8,172,128]{3,1,2,0:T(8,128)(2,1)} %copy.30), calls=%async_computation.1 | async-start | bytes 5636096 | tf_op jit(solution)/shard_map/all_to_all | solution.py:177
  148.1 1.5 slice.27
  149.5 2.2 %copy.31 = bf16[16,2,172,128]{3,1,2,0:T(2,128)(2,1)} copy(bf16[16,2,172,128]{3,2,1,0:T(8,128)(2,1)S(1)} %bitcast.31) | data formatting | bytes 2818048 | tf_op jit(solution)/shard_map/reshape | solution.py:180
  151.7 30.3 %all-to-all-done.1 = bf16[8,8,172,128]{3,1,2,0:T(8,128)(2,1)S(1)} async-done(((bf16[8,8,172,128]{3,1,2,0:T(8,128)(2,1)}), bf16[8,8,172,128]{3,1,2,0:T(8,128)(2,1)S(1)}, u32[]{:S(2)}, u32[]{:S(2)}) %all-to-all-start.1) | async-done | bytes 2818080 | tf_op jit(solution)/shard_map/all_to_all | solution.py:177
  182.0 6.3 %all-to-all-start.2 = ((bf16[16,2,172,128]{3,1,2,0:T(2,128)(2,1)}), bf16[16,2,172,128]{3,1,2,0:T(2,128)(2,1)}, u32[]{:S(2)}, u32[]{:S(2)}) async-start(bf16[16,2,172,128]{3,1,2,0:T(2,128)(2,1)} %copy.31), calls=%async_computation.2 | async-start | bytes 2818048 | tf_op jit(solution)/shard_map/all_to_all | solution.py:181
  188.3 1.8 fusion.11
  190.2 0.0 copy-start.5
  190.2 1.1 mul.15
  191.3 0.8 copy.36
  192.1 1.1 mul.13
  193.1 0.8 copy.35
  193.9 0.4 convert_reduce_fusion
  194.3 0.0 copy-start.1
  194.3 0.0 copy-start.3
  194.4 13.2 %all-to-all-done.2 = bf16[16,2,172,128]{3,1,2,0:T(2,128)(2,1)} async-done(((bf16[16,2,172,128]{3,1,2,0:T(2,128)(2,1)}), bf16[16,2,172,128]{3,1,2,0:T(2,128)(2,1)}, u32[]{:S(2)}, u32[]{:S(2)}) %all-to-all-start.2) | async-done | bytes 1409056 | tf_op jit(solution)/shard_map/all_to_all | solution.py:181
  207.6 0.0 copy-done.5
  207.6 1.7 fusion.5
  209.3 0.0 copy-done.1
  209.3 0.0 copy-done.3
  209.3 2.0 convolution_add_fusion
  (1 shorter events, 0.0 us)
Async XLA Ops:
  7.2 41.5 %all-gather.2.cloned.1.call-start = ((), (), s32[]{:S(2)}) async-start(), calls=%async_computation.5 | async-start | bytes 4718592 | tf_op jit(solution)/shard_map/all_gather | solution.py:143
  11.7 8.7 %copy-start.2 = (bf16[256,172]{0,1:T(8,128)(2,1)S(1)}, bf16[256,172]{0,1:T(8,128)(2,1)}, u32[]{:S(2)}) copy-start(bf16[256,172]{0,1:T(8,128)(2,1)} %param.16) | copy-start | bytes 264196
  11.7 8.9 %copy-start.4 = (bf16[256,172]{0,1:T(8,128)(2,1)S(1)}, bf16[256,172]{0,1:T(8,128)(2,1)}, u32[]{:S(2)}) copy-start(bf16[256,172]{0,1:T(8,128)(2,1)} %param.17) | copy-start | bytes 264196
  11.7 11.0 %copy-start.7 = (s32[1024]{0:T(1024)S(1)}, s32[1024]{0:T(1024)}, u32[]{:S(2)}) copy-start(s32[1024]{0:T(1024)} %param.14) | copy-start | bytes 12292
  11.8 12.0 %copy-start.6 = (s32[1024]{0:T(1024)S(1)}, s32[1024]{0:T(1024)}, u32[]{:S(2)}) copy-start(s32[1024]{0:T(1024)} %param.15) | copy-start | bytes 12292
  11.8 36.9 %all-to-all-start = ((bf16[16,2,128,256]{3,2,1,0:T(8,128)(2,1)}), bf16[16,2,128,256]{3,2,1,0:T(8,128)(2,1)S(1)}, u32[]{:S(2)}, u32[]{:S(2)}) async-start(bf16[16,2,128,256]{3,2,1,0:T(8,128)(2,1)} %copy.25), calls=%async_computation | async-start | bytes 4194304 | tf_op jit(solution)/shard_map/all_to_all | solution.py:153
  126.7 16.9 %all-to-all-start.4 = ((f32[128,1,688]{2,1,0:T(1,128)}), f32[128,1,688]{2,1,0:T(1,128)S(1)}, u32[]{:S(2)}, u32[]{:S(2)}) async-start(f32[128,1,688]{2,1,0:T(1,128)} %broadcast_in_dim.2), calls=%async_computation.4 | async-start | bytes 786432 | tf_op jit(solution)/shard_map/all_to_all | solution.py:171
  137.3 2.7 %copy-start = (bf16[96,256,128]{2,1,0:T(8,128)(2,1)}, bf16[96,256,128]{2,1,0:T(8,128)(2,1)S(1)}, u32[]{:S(2)}) copy-start(bf16[96,256,128]{2,1,0:T(8,128)(2,1)S(1)} %convert.4) | copy-start | bytes 18874372
  143.6 38.5 %all-to-all-start.1 = ((bf16[8,8,172,128]{3,1,2,0:T(8,128)(2,1)}), bf16[8,8,172,128]{3,1,2,0:T(8,128)(2,1)S(1)}, u32[]{:S(2)}, u32[]{:S(2)}) async-start(bf16[8,8,172,128]{3,1,2,0:T(8,128)(2,1)} %copy.30), calls=%async_computation.1 | async-start | bytes 5636096 | tf_op jit(solution)/shard_map/all_to_all | solution.py:177
  182.0 25.6 %all-to-all-start.2 = ((bf16[16,2,172,128]{3,1,2,0:T(2,128)(2,1)}), bf16[16,2,172,128]{3,1,2,0:T(2,128)(2,1)}, u32[]{:S(2)}, u32[]{:S(2)}) async-start(bf16[16,2,172,128]{3,1,2,0:T(2,128)(2,1)} %copy.31), calls=%async_computation.2 | async-start | bytes 2818048 | tf_op jit(solution)/shard_map/all_to_all | solution.py:181
  190.2 17.4 %copy-start.5 = (s32[1,16,2]{1,2,0:T(2,128)S(1)}, s32[1,16,2]{1,2,0:T(2,128)}, u32[]{:S(2)}) copy-start(s32[1,16,2]{1,2,0:T(2,128)} %param.13) | copy-start | bytes 388
  194.3 15.0 %copy-start.1 = (f32[8,128,256]{2,1,0:T(8,128)S(1)}, f32[8,128,256]{2,1,0:T(8,128)}, u32[]{:S(2)}) copy-start(f32[8,128,256]{2,1,0:T(8,128)} %get-tuple-element.7) | copy-start | bytes 3145732
  194.3 15.0 %copy-start.3 = (bf16[256,172]{0,1:T(8,128)(2,1)S(1)}, bf16[256,172]{0,1:T(8,128)(2,1)}, u32[]{:S(2)}) copy-start(bf16[256,172]{0,1:T(8,128)(2,1)} %param.16) | copy-start | bytes 264196
Sparse Core Ops, SparseCore 0:
  9.7 35.6 all-gather.1

commit v2 on v1

--- a/solution.py
+++ b/solution.py
@@ -165,10 +165,10 @@
         tile_source, tile_live, tile_weight, sources, own_blocks, degrees, lab, nw, sw, swt, classes
     )
 
-    flat = grads[:, :, :classes].reshape(devices_all, -1)
-    mine = lax.all_to_all(flat, ("dom", "sub"), 0, 0, tiled=True).sum(axis=0, keepdims=True)
-    spread = jnp.broadcast_to(mine, (devices_all, mine.shape[1]))
-    totals = lax.all_to_all(spread, ("dom", "sub"), 0, 0, tiled=True).reshape(2, width, classes)
+    flat = grads[:, :, :classes].reshape(sub_count, -1)
+    mine = lax.psum_scatter(flat, "sub", scatter_dimension=0, tiled=True)
+    mine = lax.psum(mine, "dom")
+    totals = lax.all_gather(mine, "sub", axis=0, tiled=True).reshape(2, width, classes)
     norm_factor = float(nodes_all) ** (-0.5)
 
     local = term[:part_blocks, :classes].astype(jnp.bfloat16)

time: 221 us -> 294 us (1.33)
  blocking collectives: 28.7 us -> 90.5 us
  waiting for transfers between devices: 69.1 us -> 80.7 us
  starting transfers between devices: 24.2 us -> 30 us
    psum x0 -> x1, blocking collectives: none -> 60.8 us  [per_device(): mine = lax.psum(mine, 'dom')]
    all_gather x0 -> x1, blocking collectives: none -> 29.7 us  [per_device(): lax.all_gather(mine, 'sub', axis=0, tiled=True).reshape(2, width, classes)]
    all_to_all x1 -> x0, blocking collectives: 28.7 us -> none  [per_device(): lax.all_to_all(flat, ('dom', 'sub'), 0, 0, tiled=True)]
    unnamed x1 -> x3, waiting for transfers between devices: 0.68 us -> 26.4 us
    all_to_all x1, waiting for transfers between devices: 13.2 us -> 0.01 us  [per_device(): arrived = lax.all_to_all(halo, 'dom', 0, 0, tiled=True).astype(jnp.float32)]
    all_to_all x1, starting transfers between devices: 4.5 us -> 16.8 us  [per_device(): lax.all_to_all(local, 'sub', 0, 0, tiled=True).astype(jnp.float32)]
    all_to_all x1 -> x0, starting transfers between devices: 4.65 us -> none  [per_device(): lax.all_to_all(spread, ('dom', 'sub'), 0, 0, tiled=True)]
    unnamed x20 -> x26, local copies, waits for them, and re-layouts: 4.46 us -> 6.71 us
  transfers between devices with their start and end apart: 5 -> 5, of which waited for: 4 -> 3; matrix products, arithmetic and copies ran while one was open for 12% -> 6% of each run, Pallas kernels for 0% -> 0%
where the time goes in v2:
time: 294 us
  blocking collectives  90.5 us (31%)
  waiting for transfers between devices  80.7 us (27%)
  Pallas kernels  39.2 us (13%)
  starting transfers between devices  30 us (10%)
  local copies, waits for them, and re-layouts  20.7 us (7%)
  between operations  14.2 us (5%)
  other arithmetic  12.7 us (4%)
  matrix products  5.64 us (2%)
    psum x1, blocking collectives, per_device(): mine = lax.psum(mine, 'dom')  60.8 us
    pallas_call x1, Pallas kernels, _fused(): pl.pallas_call(functools.partial(_fused_kernel, classes=classes), grid_sp...  39.2 us
    all_to_all x1, waiting for transfers between devices, per_device(): lax.all_to_all(local, 'sub', 0, 0, tiled=True).astype(jnp.float32)  30.5 us
    all_gather x1, blocking collectives, per_device(): lax.all_gather(mine, 'sub', axis=0, tiled=True).reshape(2, width, classes)  29.7 us
    unnamed x3, waiting for transfers between devices  26.4 us
    all_to_all x1, waiting for transfers between devices, per_device(): lax.all_to_all(outgoing, 'dom', split_axis=0, concat_axis=0, tiled=True)  23.8 us
    all_to_all x1, starting transfers between devices, per_device(): lax.all_to_all(local, 'sub', 0, 0, tiled=True).astype(jnp.float32)  16.8 us
    all_to_all x1, starting transfers between devices, per_device(): lax.all_to_all(outgoing, 'dom', split_axis=0, concat_axis=0, tiled=True)  8.72 us
  transfers between devices with their start and end apart: 5, of which 3 were waited for; matrix products, arithmetic and copies ran while one was open for 6% of the time, Pallas kernels for 0%

profile of v2, /device:TPU:1, one launch (start us, length us, event | category | flops | bytes accessed | tf_op | source)
XLA Modules:
  0.0 293.8 jit_solution(6571101455695159961)
XLA Ops:
  7.2 0.0 all-gather.3.cloned.1.call-start
  7.2 0.7 all-gather.3.cloned.1.call-update
  7.9 1.8 convolution_convert_fusion
  9.7 2.0 copy.25
  11.7 0.0 copy-start.8
  11.7 0.0 copy-start.7
  11.7 0.0 copy-start.3
  11.8 0.0 copy-start.5
  11.8 8.7 %all-to-all-start = ((bf16[16,2,128,256]{3,2,1,0:T(8,128)(2,1)}), bf16[16,2,128,256]{3,2,1,0:T(8,128)(2,1)S(1)}, u32[]{:S(2)}, u32[]{:S(2)}) async-start(bf16[16,2,128,256]{3,2,1,0:T(8,128)(2,1)} %copy.25), calls=%async_computation | async-start | bytes 4194304 | tf_op jit(solution)/shard_map/all_to_all | solution.py:153
  20.5 0.0 copy-done.8
  20.5 1.0 copy.28.deg_ref
  21.5 0.0 copy-done.7
  21.5 1.0 copy.29.lab_ref
  22.6 0.0 copy-done.3
  22.6 0.1 copy.26
  22.7 0.0 copy-done.5
  22.7 0.1 copy.27
  22.8 0.7 pad.11.nw_ref
  23.5 0.7 pad.12.sw_ref
  24.2 0.7 pad.13.swt_ref
  24.8 23.8 %all-to-all-done = bf16[16,2,128,256]{3,2,1,0:T(8,128)(2,1)S(1)} async-done(((bf16[16,2,128,256]{3,2,1,0:T(8,128)(2,1)}), bf16[16,2,128,256]{3,2,1,0:T(8,128)(2,1)S(1)}, u32[]{:S(2)}, u32[]{:S(2)}) %all-to-all-start) | async-done | bytes 2097184 | tf_op jit(solution)/shard_map/all_to_all | solution.py:153
  48.6 0.0 all-gather.3.cloned.1.call-done
  48.6 5.3 %pad_maximum_fusion.sources_ref = bf16[96,128,256]{2,1,0:T(8,128)(2,1)} fusion(bf16[32,128,256]{2,1,0:T(8,128)(2,1)S(1)} %bitcast.32, bf16[64,128,256]{2,1,0:T(8,128)(2,1)} %all-gather.3.cloned.1.call-done), kind=kLoop, calls=%fused_computation | loop fusion | flops 3145728 | bytes 12582912 | tf_op jit(solution)/shard_map/concatenate | solution.py:155
  54.0 39.2 %shard_map.112 = (f32[96,256,128]{2,1,0:T(8,128)}, f32[2,256,256]{2,1,0:T(8,128)}, f32[8,128,256]{2,1,0:T(8,128)}) custom-call(s32[8,64]{1,0:T(8,128)} %src_ref.1, s32[8]{0:T(128)} %live_ref.1, bf16[8,64,128,128]{3,2,1,0:T(8,128)(2,1)} %w_ref.1, bf16[96,128,256]{2,1,0:T(8,128)(2,1)} %pad_maximum_fusion.sources_ref, bf16[8,128,256]{2,1,0:T(8,128)(2,1)} %bitcast.36, ...), custom_call_target="tpu_custom_call" | custom-call | tf_op jit(solution)/shard_map/pallas_call | solution.py:108
  93.2 5.9 %convert.4 = bf16[96,256,128]{2,1,0:T(8,128)(2,1)S(1)} convert(f32[96,256,128]{2,1,0:T(8,128)} %get-tuple-element.6) | non-fusion elementwise | flops 3145728 | bytes 18874368 | tf_op jit(solution)/shard_map/convert.1
  99.1 0.0 copy-start
  99.1 2.7 copy-done
  101.7 0.2 slice.26
  102.0 2.3 copy.30
  104.3 0.0 copy-start.2
  104.3 0.0 copy-start.9
  104.3 16.8 %all-to-all-start.1 = ((bf16[8,8,172,128]{3,1,2,0:T(8,128)(2,1)}), bf16[8,8,172,128]{3,1,2,0:T(8,128)(2,1)S(1)}, u32[]{:S(2)}, u32[]{:S(2)}) async-start(bf16[8,8,172,128]{3,1,2,0:T(8,128)(2,1)} %copy.30), calls=%async_computation.1 | async-start | bytes 5636096 | tf_op jit(solution)/shard_map/all_to_all | solution.py:177
  121.2 0.0 all-reduce.6.cloned.1.call-start
  121.2 0.0 copy-done.2
  121.2 1.0 reshape.46
  122.2 0.0 all-reduce.6.cloned.1.call-update
  122.2 0.0 copy-done.9
  122.2 0.6 dynamic-slice
  122.8 1.5 slice.27
  124.3 2.2 copy.31
  126.5 30.5 %all-to-all-done.1 = bf16[8,8,172,128]{3,1,2,0:T(8,128)(2,1)S(1)} async-done(((bf16[8,8,172,128]{3,1,2,0:T(8,128)(2,1)}), bf16[8,8,172,128]{3,1,2,0:T(8,128)(2,1)S(1)}, u32[]{:S(2)}, u32[]{:S(2)}) %all-to-all-start.1) | async-done | bytes 2818080 | tf_op jit(solution)/shard_map/all_to_all | solution.py:177
  156.9 4.4 %all-to-all-start.2 = ((bf16[16,2,172,128]{3,1,2,0:T(2,128)(2,1)}), bf16[16,2,172,128]{3,1,2,0:T(2,128)(2,1)}, u32[]{:S(2)}, u32[]{:S(2)}) async-start(bf16[16,2,172,128]{3,1,2,0:T(2,128)(2,1)} %copy.31), calls=%async_computation.2 | async-start | bytes 2818048 | tf_op jit(solution)/shard_map/all_to_all | solution.py:181
  161.3 25.7 %all-reduce.6.cloned.1.call-done = f32[8,11008]{1,0:T(8,128)} async-done(((f32[8,11008]{1,0:T(8,128)}), f32[8,11008]{1,0:T(8,128)}) %all-reduce.6.cloned.1.call-update) | async-done | bytes 352272
  187.0 1.7 constant_dynamic-slice_fusion
  188.7 60.8 %psum.7 = f32[1,11008]{1,0:T(1,128)S(1)} all-reduce(f32[1,11008]{1,0:T(1,128)S(1)} %constant_dynamic-slice_fusion), channel_id=1, replica_groups=mesh['dom'=16,'sub'=8] {'dom'}, use_global_device_ids=true, to_apply=%region_2.3 | all-reduce | flops 11008 | bytes 88064 | tf_op jit(solution)/shard_map/psum | solution.py:170
  249.5 29.7 %all-gather = f32[8,1,11008]{2,1,0:T(1,128)S(1)} all-gather(f32[1,1,11008]{2,1,0:T(1,128)S(1)} %bitcast.40), channel_id=1, replica_groups=mesh['dom'=16,'sub'=8] {'sub'}, dimensions={0}, use_global_device_ids=true | all-gather | bytes 396288 | tf_op jit(solution)/shard_map/all_gather | solution.py:171
  279.2 1.1 fusion.11
  280.3 0.0 copy-start.6
  280.3 0.3 mul.13
  280.7 0.8 copy.34
  281.5 0.3 mul.15
  281.8 0.8 copy.35
  282.6 0.4 convert_reduce_fusion
  283.0 0.0 copy-start.1
  283.0 0.0 copy-start.4
  283.0 0.0 all-to-all-done.2
  283.1 0.0 copy-done.6
  283.1 1.8 fusion.5
  284.9 0.0 copy-done.1
  284.9 0.0 copy-done.4
  284.9 2.0 convolution_add_fusion
  (1 shorter events, 0.0 us)
Async XLA Ops:
  7.2 41.5 %all-gather.3.cloned.1.call-start = ((), (), s32[]{:S(2)}) async-start(), calls=%async_computation.3 | async-start | bytes 4718592 | tf_op jit(solution)/shard_map/all_gather | solution.py:143
  11.7 8.7 %copy-start.8 = (s32[1024]{0:T(1024)S(1)}, s32[1024]{0:T(1024)}, u32[]{:S(2)}) copy-start(s32[1024]{0:T(1024)} %param.14) | copy-start | bytes 12292
  11.7 9.8 %copy-start.7 = (s32[1024]{0:T(1024)S(1)}, s32[1024]{0:T(1024)}, u32[]{:S(2)}) copy-start(s32[1024]{0:T(1024)} %param.15) | copy-start | bytes 12292
  11.7 10.8 %copy-start.3 = (bf16[256,172]{0,1:T(8,128)(2,1)S(1)}, bf16[256,172]{0,1:T(8,128)(2,1)}, u32[]{:S(2)}) copy-start(bf16[256,172]{0,1:T(8,128)(2,1)} %param.16) | copy-start | bytes 264196
  11.8 10.9 %copy-start.5 = (bf16[256,172]{0,1:T(8,128)(2,1)S(1)}, bf16[256,172]{0,1:T(8,128)(2,1)}, u32[]{:S(2)}) copy-start(bf16[256,172]{0,1:T(8,128)(2,1)} %param.17) | copy-start | bytes 264196
  11.8 36.9 %all-to-all-start = ((bf16[16,2,128,256]{3,2,1,0:T(8,128)(2,1)}), bf16[16,2,128,256]{3,2,1,0:T(8,128)(2,1)S(1)}, u32[]{:S(2)}, u32[]{:S(2)}) async-start(bf16[16,2,128,256]{3,2,1,0:T(8,128)(2,1)} %copy.25), calls=%async_computation | async-start | bytes 4194304 | tf_op jit(solution)/shard_map/all_to_all | solution.py:153
  99.1 2.7 copy-start
  104.3 16.9 %copy-start.2 = (f32[2,256,256]{2,1,0:T(8,128)S(1)}, f32[2,256,256]{2,1,0:T(8,128)}, u32[]{:S(2)}) copy-start(f32[2,256,256]{2,1,0:T(8,128)} %get-tuple-element.8) | copy-start | bytes 1572868
  104.3 17.9 %copy-start.9 = (u32[128]{0:T(128)S(1)}, u32[128]{0:T(128)}, u32[]{:S(2)}) copy-start(u32[128]{0:T(128)} %constant.19) | copy-start | bytes 1540
  104.3 52.6 %all-to-all-start.1 = ((bf16[8,8,172,128]{3,1,2,0:T(8,128)(2,1)}), bf16[8,8,172,128]{3,1,2,0:T(8,128)(2,1)S(1)}, u32[]{:S(2)}, u32[]{:S(2)}) async-start(bf16[8,8,172,128]{3,1,2,0:T(8,128)(2,1)} %copy.30), calls=%async_computation.1 | async-start | bytes 5636096 | tf_op jit(solution)/shard_map/all_to_all | solution.py:177
  121.2 65.9 %all-reduce.6.cloned.1.call-start = ((), (), s32[]{:S(2)}) async-start(), calls=%async_computation.4 | async-start | bytes 704512
  156.9 126.1 %all-to-all-start.2 = ((bf16[16,2,172,128]{3,1,2,0:T(2,128)(2,1)}), bf16[16,2,172,128]{3,1,2,0:T(2,128)(2,1)}, u32[]{:S(2)}, u32[]{:S(2)}) async-start(bf16[16,2,172,128]{3,1,2,0:T(2,128)(2,1)} %copy.31), calls=%async_computation.2 | async-start | bytes 2818048 | tf_op jit(solution)/shard_map/all_to_all | solution.py:181
  280.3 2.7 copy-start.6
  283.0 1.9 copy-start.1
  283.0 1.9 copy-start.4
Sparse Core Ops, SparseCore 0:
  9.7 35.6 all-gather.2
  124.3 62.6 all-reduce.5

commit v3 on v1

--- a/solution.py
+++ b/solution.py
@@ -22,9 +22,10 @@
     nw_ref,
     sw_ref,
     swt_ref,
-    term_ref,
+    out_ref,
     grads_ref,
     selfterm_ref,
+    term_ref,
     *,
     classes,
 ):
@@ -45,10 +46,10 @@
         return jnp.where(t < live, w_ref[0, t], jnp.zeros_like(w_ref[0, t]))
 
     def forward(g, acc):
-        for k in range(GROUP):
-            t = g * GROUP + k
-            acc = acc + jnp.dot(tile(t), sources_ref[src_ref[b, t]], preferred_element_type=jnp.float32)
-        return acc
+        ts = [g * GROUP + k for k in range(GROUP)]
+        wcat = jnp.concatenate([tile(t) for t in ts], axis=1)
+        scat = jnp.concatenate([sources_ref[src_ref[b, t]] for t in ts], axis=0)
+        return acc + jnp.dot(wcat, scat, preferred_element_type=jnp.float32)
 
     acc = lax.fori_loop(0, groups, forward, jnp.zeros((rows, width), jnp.float32))
     deg = deg_ref[0]
@@ -80,41 +81,46 @@
 
     lax.fori_loop(0, groups, backward, 0)
 
+    @pl.when(b == pl.num_programs(0) - 1)
+    def _():
+        out_ref[...] = term_ref[:, : out_ref.shape[1], :].astype(out_ref.dtype)
+
 
 def _fused(tile_source, tile_live, tile_weight, sources, own_blocks, deg, lab, nw, sw, swt, classes):
     block_count, tile_slots, rows, _ = tile_weight.shape
     source_total, _, width = sources.shape
     padded = nw.shape[1]
-    vmem = pltpu.MemorySpace.VMEM if hasattr(pltpu, "MemorySpace") else pltpu.VMEM
+    kept = -(-classes // 16) * 16
     grid_spec = pltpu.PrefetchScalarGridSpec(
         num_scalar_prefetch=2,
         grid=(block_count,),
         in_specs=[
             pl.BlockSpec((1, tile_slots, rows, rows), lambda b, *_: (b, 0, 0, 0)),
-            pl.BlockSpec(memory_space=vmem),
+            pl.BlockSpec((source_total, rows, width), lambda b, *_: (0, 0, 0)),
             pl.BlockSpec((1, rows, width), lambda b, *_: (b, 0, 0)),
             pl.BlockSpec((1, rows, 1), lambda b, *_: (b, 0, 0)),
             pl.BlockSpec((1, rows, 1), lambda b, *_: (b, 0, 0)),
-            pl.BlockSpec(memory_space=vmem),
-            pl.BlockSpec(memory_space=vmem),
-            pl.BlockSpec(memory_space=vmem),
+            pl.BlockSpec((width, padded), lambda b, *_: (0, 0)),
+            pl.BlockSpec((width, padded), lambda b, *_: (0, 0)),
+            pl.BlockSpec((padded, width), lambda b, *_: (0, 0)),
         ],
         out_specs=[
-            pl.BlockSpec(memory_space=vmem),
-            pl.BlockSpec(memory_space=vmem),
+            pl.BlockSpec((source_total, kept, rows), lambda b, *_: (0, 0, 0)),
+            pl.BlockSpec((2, width, padded), lambda b, *_: (0, 0, 0)),
             pl.BlockSpec((1, rows, width), lambda b, *_: (b, 0, 0)),
         ],
+        scratch_shapes=[pltpu.VMEM((source_total, padded, rows), jnp.float32)],
     )
     return pl.pallas_call(
         functools.partial(_fused_kernel, classes=classes),
         grid_spec=grid_spec,
         out_shape=[
-            jax.ShapeDtypeStruct((source_total, padded, rows), jnp.float32),
+            jax.ShapeDtypeStruct((source_total, kept, rows), jnp.bfloat16),
             jax.ShapeDtypeStruct((2, width, padded), jnp.float32),
             jax.ShapeDtypeStruct((block_count, rows, width), jnp.float32),
         ],
         compiler_params=pltpu.CompilerParams(
-            dimension_semantics=("arbitrary",), vmem_limit_bytes=56 * 1024 * 1024
+            dimension_semantics=("arbitrary",), vmem_limit_bytes=60 * 1024 * 1024
         ),
     )(tile_source, tile_live, tile_weight, sources, own_blocks, deg, lab, nw, sw, swt)
 
@@ -171,12 +177,12 @@
     totals = lax.all_to_all(spread, ("dom", "sub"), 0, 0, tiled=True).reshape(2, width, classes)
     norm_factor = float(nodes_all) ** (-0.5)
 
-    local = term[:part_blocks, :classes].astype(jnp.bfloat16)
+    local = term[:part_blocks, :classes]
     local = local.reshape(sub_count, block_count, classes, block_rows)
     local_grad = (
         lax.all_to_all(local, "sub", 0, 0, tiled=True).astype(jnp.float32).sum(axis=0)
     )
-    halo = term[part_blocks:, :classes].astype(jnp.bfloat16)
+    halo = term[part_blocks:, :classes]
     halo = halo.reshape(dom_count, slot_count, classes, block_rows)
     arrived = lax.all_to_all(halo, "dom", 0, 0, tiled=True).astype(jnp.float32)
     return_table = send_table.astype(jnp.float32)

time: 221 us -> 214 us (0.968)
  waiting for transfers between devices: 69.1 us -> 76.7 us
  blocking collectives: 28.7 us -> 22.5 us
  other arithmetic: 13.8 us -> 7.93 us
    all_to_all x1, waiting for transfers between devices: 1.05 us -> 7.92 us  [per_device(): lax.all_to_all(spread, ('dom', 'sub'), 0, 0, tiled=True)]
    all_to_all x1, blocking collectives: 28.7 us -> 22.5 us  [per_device(): lax.all_to_all(flat, ('dom', 'sub'), 0, 0, tiled=True)]
    another operation x1 -> x0, other arithmetic: 5.91 us -> none
    unnamed x20 -> x18, local copies, waits for them, and re-layouts: 4.46 us -> 1.8 us
  transfers between devices with their start and end apart: 5 -> 5, of which waited for: 4 -> 4; matrix products, arithmetic and copies ran while one was open for 12% -> 10% of each run, Pallas kernels for 0% -> 0%
where the time goes in v3:
time: 214 us; the launch traced here: 211 us
  waiting for transfers between devices  76.7 us (36%)
  Pallas kernels  41.5 us (19%)
  starting transfers between devices  22.5 us (11%)
  blocking collectives  22.5 us (11%)
  local copies, waits for them, and re-layouts  19.8 us (9%)
  between operations  14.2 us (7%)
  other arithmetic  7.93 us (4%)
  matrix products  5.56 us (3%)
    pallas_call x1, Pallas kernels, _fused(): pl.pallas_call(functools.partial(_fused_kernel, classes=classes), grid_sp...  41.5 us
    all_to_all x1, waiting for transfers between devices, per_device(): lax.all_to_all(local, 'sub', 0, 0, tiled=True).astype(jnp.float32)  30.3 us
    all_to_all x1, waiting for transfers between devices, per_device(): lax.all_to_all(outgoing, 'dom', split_axis=0, concat_axis=0, tiled=True)  23.8 us
    all_to_all x1, blocking collectives, per_device(): lax.all_to_all(flat, ('dom', 'sub'), 0, 0, tiled=True)  22.5 us
    all_to_all x1, waiting for transfers between devices, per_device(): arrived = lax.all_to_all(halo, 'dom', 0, 0, tiled=True).astype(jnp.float32)  14 us
    all_to_all x1, starting transfers between devices, per_device(): lax.all_to_all(outgoing, 'dom', split_axis=0, concat_axis=0, tiled=True)  8.72 us
    all_to_all x1, waiting for transfers between devices, per_device(): lax.all_to_all(spread, ('dom', 'sub'), 0, 0, tiled=True)  7.92 us
    concatenate x1, other arithmetic, per_device(): jnp.concatenate([partition, boundary.reshape(dom_count * slot_count, bloc...  5.4 us
  transfers between devices with their start and end apart: 5, of which 4 were waited for; matrix products, arithmetic and copies ran while one was open for 10% of the time, Pallas kernels for 0%

profile of v3, /device:TPU:1, one launch (start us, length us, event | category | flops | bytes accessed | tf_op | source)
XLA Modules:
  0.0 210.7 jit_solution(7450479422884743957)
XLA Ops:
  7.2 0.0 all-gather.2.cloned.1.call-start
  7.2 0.7 all-gather.2.cloned.1.call-update
  7.9 1.8 convolution_convert_fusion
  9.7 2.1 copy.25
  11.8 0.0 copy-start.6
  11.8 0.0 copy-start.5
  11.8 0.0 copy-start.1
  11.8 0.0 copy-start.3
  11.8 8.7 %all-to-all-start = ((bf16[16,2,128,256]{3,2,1,0:T(8,128)(2,1)}), bf16[16,2,128,256]{3,2,1,0:T(8,128)(2,1)S(1)}, u32[]{:S(2)}, u32[]{:S(2)}) async-start(bf16[16,2,128,256]{3,2,1,0:T(8,128)(2,1)} %copy.25), calls=%async_computation | async-start | bytes 4194304 | tf_op jit(solution)/shard_map/all_to_all | solution.py:159
  20.5 0.0 copy-done.6
  20.5 1.0 copy.28.deg_ref
  21.6 0.0 copy-done.5
  21.6 1.0 copy.29.lab_ref
  22.6 0.0 copy-done.1
  22.6 0.1 copy.26
  22.7 0.0 copy-done.3
  22.7 0.1 copy.27
  22.8 0.7 pad.11.nw_ref
  23.5 0.7 pad.12.sw_ref
  24.2 0.6 pad.13.swt_ref
  24.8 23.8 %all-to-all-done = bf16[16,2,128,256]{3,2,1,0:T(8,128)(2,1)S(1)} async-done(((bf16[16,2,128,256]{3,2,1,0:T(8,128)(2,1)}), bf16[16,2,128,256]{3,2,1,0:T(8,128)(2,1)S(1)}, u32[]{:S(2)}, u32[]{:S(2)}) %all-to-all-start) | async-done | bytes 2097184 | tf_op jit(solution)/shard_map/all_to_all | solution.py:159
  48.7 0.0 all-gather.2.cloned.1.call-done
  48.7 5.4 %pad_maximum_fusion.sources_ref = bf16[96,128,256]{2,1,0:T(8,128)(2,1)} fusion(bf16[32,128,256]{2,1,0:T(8,128)(2,1)S(1)} %bitcast.30, bf16[64,128,256]{2,1,0:T(8,128)(2,1)} %all-gather.2.cloned.1.call-done), kind=kLoop, calls=%fused_computation | loop fusion | flops 3145728 | bytes 12582912 | tf_op jit(solution)/shard_map/concatenate | solution.py:161
  54.1 41.5 %shard_map.112 = (bf16[96,176,128]{2,1,0:T(8,128)(2,1)}, f32[2,256,256]{2,1,0:T(8,128)}, f32[8,128,256]{2,1,0:T(8,128)}) custom-call(s32[8,64]{1,0:T(8,128)} %src_ref.1, s32[8]{0:T(128)} %live_ref.1, bf16[8,64,128,128]{3,2,1,0:T(8,128)(2,1)} %w_ref.1, bf16[96,128,256]{2,1,0:T(8,128)(2,1)} %pad_maximum_fusion.sources_ref, bf16[8,128,256]{2,1,0:T(8,128)(2,1)} %bitcast.34, ...), custom_call_target="tpu_custom_call" | custom-call | tf_op jit(solution)/shard_map/pallas_call | solution.py:114
  95.5 1.8 all_to_all.25
  97.4 22.5 %all_to_all.31 = f32[128,1,688]{2,1,0:T(1,128)S(1)} all-to-all(f32[128,1,688]{2,1,0:T(1,128)S(1)} %all_to_all.25), channel_id=1, replica_groups=mesh['dom'=16,'sub'=8] {'dom','sub'}, dimensions={0} | all-to-all | bytes 704512 | tf_op jit(solution)/shard_map/all_to_all | solution.py:175
  119.9 0.3 reduce_sum.19
  120.2 1.0 broadcast_in_dim.2
  121.1 4.6 %all-to-all-start.4 = ((f32[128,1,688]{2,1,0:T(1,128)}), f32[128,1,688]{2,1,0:T(1,128)S(1)}, u32[]{:S(2)}, u32[]{:S(2)}) async-start(f32[128,1,688]{2,1,0:T(1,128)} %broadcast_in_dim.2), calls=%async_computation.4 | async-start | bytes 786432 | tf_op jit(solution)/shard_map/all_to_all | solution.py:177
  125.8 2.0 slice.19
  127.8 2.3 %copy.30 = bf16[8,8,172,128]{3,1,2,0:T(8,128)(2,1)} copy(bf16[8,8,172,128]{3,2,1,0:T(8,128)(2,1)S(1)} %bitcast.29) | data formatting | bytes 5636096 | tf_op jit(solution)/shard_map/reshape | solution.py:181
  130.1 7.9 %all-to-all-done.4 = f32[128,1,688]{2,1,0:T(1,128)S(1)} async-done(((f32[128,1,688]{2,1,0:T(1,128)}), f32[128,1,688]{2,1,0:T(1,128)S(1)}, u32[]{:S(2)}, u32[]{:S(2)}) %all-to-all-start.4) | async-done | bytes 352288 | tf_op jit(solution)/shard_map/all_to_all | solution.py:177
  138.0 4.5 %all-to-all-start.1 = ((bf16[8,8,172,128]{3,1,2,0:T(8,128)(2,1)}), bf16[8,8,172,128]{3,1,2,0:T(8,128)(2,1)S(1)}, u32[]{:S(2)}, u32[]{:S(2)}) async-start(bf16[8,8,172,128]{3,1,2,0:T(8,128)(2,1)} %copy.30), calls=%async_computation.1 | async-start | bytes 5636096 | tf_op jit(solution)/shard_map/all_to_all | solution.py:183
  142.5 1.5 slice.20
  144.0 2.2 %copy.31 = bf16[16,2,172,128]{3,1,2,0:T(2,128)(2,1)} copy(bf16[16,2,172,128]{3,2,1,0:T(8,128)(2,1)S(1)} %bitcast.31) | data formatting | bytes 2818048 | tf_op jit(solution)/shard_map/reshape | solution.py:186
  146.2 30.3 %all-to-all-done.1 = bf16[8,8,172,128]{3,1,2,0:T(8,128)(2,1)S(1)} async-done(((bf16[8,8,172,128]{3,1,2,0:T(8,128)(2,1)}), bf16[8,8,172,128]{3,1,2,0:T(8,128)(2,1)S(1)}, u32[]{:S(2)}, u32[]{:S(2)}) %all-to-all-start.1) | async-done | bytes 2818080 | tf_op jit(solution)/shard_map/all_to_all | solution.py:183
  176.5 4.6 %all-to-all-start.2 = ((bf16[16,2,172,128]{3,1,2,0:T(2,128)(2,1)}), bf16[16,2,172,128]{3,1,2,0:T(2,128)(2,1)}, u32[]{:S(2)}, u32[]{:S(2)}) async-start(bf16[16,2,172,128]{3,1,2,0:T(2,128)(2,1)} %copy.31), calls=%async_computation.2 | async-start | bytes 2818048 | tf_op jit(solution)/shard_map/all_to_all | solution.py:187
  181.0 1.8 fusion.11
  182.9 0.0 copy-start.4
  182.9 1.1 mul.13
  184.0 0.8 copy.35
  184.8 0.1 mul.15
  184.9 0.8 copy.36
  185.7 0.4 convert_reduce_fusion
  186.1 0.0 copy-start
  186.1 0.0 copy-start.2
  186.1 14.0 %all-to-all-done.2 = bf16[16,2,172,128]{3,1,2,0:T(2,128)(2,1)} async-done(((bf16[16,2,172,128]{3,1,2,0:T(2,128)(2,1)}), bf16[16,2,172,128]{3,1,2,0:T(2,128)(2,1)}, u32[]{:S(2)}, u32[]{:S(2)}) %all-to-all-start.2) | async-done | bytes 1409056 | tf_op jit(solution)/shard_map/all_to_all | solution.py:187
  200.1 0.0 copy-done.4
  200.1 1.7 fusion.5
  201.8 0.0 copy-done
  201.8 0.0 copy-done.2
  201.9 2.0 convolution_add_fusion
  (1 shorter events, 0.0 us)
Async XLA Ops:
  7.2 41.5 %all-gather.2.cloned.1.call-start = ((), (), s32[]{:S(2)}) async-start(), calls=%async_computation.5 | async-start | bytes 4718592 | tf_op jit(solution)/shard_map/all_gather | solution.py:149
  11.8 8.7 %copy-start.6 = (s32[1024]{0:T(1024)S(1)}, s32[1024]{0:T(1024)}, u32[]{:S(2)}) copy-start(s32[1024]{0:T(1024)} %param.14) | copy-start | bytes 12292
  11.8 9.8 %copy-start.5 = (s32[1024]{0:T(1024)S(1)}, s32[1024]{0:T(1024)}, u32[]{:S(2)}) copy-start(s32[1024]{0:T(1024)} %param.15) | copy-start | bytes 12292
  11.8 10.8 %copy-start.1 = (bf16[256,172]{0,1:T(8,128)(2,1)S(1)}, bf16[256,172]{0,1:T(8,128)(2,1)}, u32[]{:S(2)}) copy-start(bf16[256,172]{0,1:T(8,128)(2,1)} %param.16) | copy-start | bytes 264196
  11.8 10.9 %copy-start.3 = (bf16[256,172]{0,1:T(8,128)(2,1)S(1)}, bf16[256,172]{0,1:T(8,128)(2,1)}, u32[]{:S(2)}) copy-start(bf16[256,172]{0,1:T(8,128)(2,1)} %param.17) | copy-start | bytes 264196
  11.8 36.9 %all-to-all-start = ((bf16[16,2,128,256]{3,2,1,0:T(8,128)(2,1)}), bf16[16,2,128,256]{3,2,1,0:T(8,128)(2,1)S(1)}, u32[]{:S(2)}, u32[]{:S(2)}) async-start(bf16[16,2,128,256]{3,2,1,0:T(8,128)(2,1)} %copy.25), calls=%async_computation | async-start | bytes 4194304 | tf_op jit(solution)/shard_map/all_to_all | solution.py:159
  121.1 16.9 %all-to-all-start.4 = ((f32[128,1,688]{2,1,0:T(1,128)}), f32[128,1,688]{2,1,0:T(1,128)S(1)}, u32[]{:S(2)}, u32[]{:S(2)}) async-start(f32[128,1,688]{2,1,0:T(1,128)} %broadcast_in_dim.2), calls=%async_computation.4 | async-start | bytes 786432 | tf_op jit(solution)/shard_map/all_to_all | solution.py:177
  138.0 38.5 %all-to-all-start.1 = ((bf16[8,8,172,128]{3,1,2,0:T(8,128)(2,1)}), bf16[8,8,172,128]{3,1,2,0:T(8,128)(2,1)S(1)}, u32[]{:S(2)}, u32[]{:S(2)}) async-start(bf16[8,8,172,128]{3,1,2,0:T(8,128)(2,1)} %copy.30), calls=%async_computation.1 | async-start | bytes 5636096 | tf_op jit(solution)/shard_map/all_to_all | solution.py:183
  176.5 23.6 %all-to-all-start.2 = ((bf16[16,2,172,128]{3,1,2,0:T(2,128)(2,1)}), bf16[16,2,172,128]{3,1,2,0:T(2,128)(2,1)}, u32[]{:S(2)}, u32[]{:S(2)}) async-start(bf16[16,2,172,128]{3,1,2,0:T(2,128)(2,1)} %copy.31), calls=%async_computation.2 | async-start | bytes 2818048 | tf_op jit(solution)/shard_map/all_to_all | solution.py:187
  182.9 17.2 %copy-start.4 = (s32[1,16,2]{1,2,0:T(2,128)S(1)}, s32[1,16,2]{1,2,0:T(2,128)}, u32[]{:S(2)}) copy-start(s32[1,16,2]{1,2,0:T(2,128)} %param.13) | copy-start | bytes 388
  186.1 15.7 %copy-start = (f32[8,128,256]{2,1,0:T(8,128)S(1)}, f32[8,128,256]{2,1,0:T(8,128)}, u32[]{:S(2)}) copy-start(f32[8,128,256]{2,1,0:T(8,128)} %get-tuple-element.7) | copy-start | bytes 3145732
  186.1 15.7 %copy-start.2 = (bf16[256,172]{0,1:T(8,128)(2,1)S(1)}, bf16[256,172]{0,1:T(8,128)(2,1)}, u32[]{:S(2)}) copy-start(bf16[256,172]{0,1:T(8,128)(2,1)} %param.16) | copy-start | bytes 264196
Sparse Core Ops, SparseCore 0:
  9.7 35.6 all-gather.1

commit v4 on v3

--- a/solution.py
+++ b/solution.py
@@ -171,20 +171,35 @@
         tile_source, tile_live, tile_weight, sources, own_blocks, degrees, lab, nw, sw, swt, classes
     )
 
-    flat = grads[:, :, :classes].reshape(devices_all, -1)
-    mine = lax.all_to_all(flat, ("dom", "sub"), 0, 0, tiled=True).sum(axis=0, keepdims=True)
+    norm_factor = float(nodes_all) ** (-0.5)
+
+    def split(x):
+        hi = x.astype(jnp.bfloat16)
+        return jnp.concatenate([hi, (x - hi.astype(jnp.float32)).astype(jnp.bfloat16)], axis=-1)
+
+    def joined(x):
+        half = x.shape[-1] // 2
+        return x[..., :half].astype(jnp.float32) + x[..., half:].astype(jnp.float32)
+
+    flat = grads[:, :, :classes].reshape(sub_count, -1)
+    local = term[:part_blocks, :classes].reshape(sub_count, -1)
+    local_size = local.shape[1]
+    sent = jnp.concatenate([local, split(flat)], axis=1)
+    got = lax.all_to_all(sent, "sub", 0, 0, tiled=True)
+    local_grad = (
+        got[:, :local_size].astype(jnp.float32).reshape(sub_count, block_count, classes, block_rows).sum(axis=0)
+    )
+    part_sum = joined(got[:, local_size:]).sum(axis=0).reshape(dom_count, -1)
+    halo = term[part_blocks:, :classes].reshape(dom_count, -1)
+    halo_size = halo.shape[1]
+    sent = jnp.concatenate([halo, split(part_sum)], axis=1)
+    got = lax.all_to_all(sent, "dom", 0, 0, tiled=True)
+    arrived = got[:, :halo_size].astype(jnp.float32).reshape(dom_count, slot_count, classes, block_rows)
+    mine = joined(got[:, halo_size:]).sum(axis=0, keepdims=True)
     spread = jnp.broadcast_to(mine, (devices_all, mine.shape[1]))
-    totals = lax.all_to_all(spread, ("dom", "sub"), 0, 0, tiled=True).reshape(2, width, classes)
-    norm_factor = float(nodes_all) ** (-0.5)
-
-    local = term[:part_blocks, :classes]
-    local = local.reshape(sub_count, block_count, classes, block_rows)
-    local_grad = (
-        lax.all_to_all(local, "sub", 0, 0, tiled=True).astype(jnp.float32).sum(axis=0)
-    )
-    halo = term[part_blocks:, :classes]
-    halo = halo.reshape(dom_count, slot_count, classes, block_rows)
-    arrived = lax.all_to_all(halo, "dom", 0, 0, tiled=True).astype(jnp.float32)
+    totals = lax.all_to_all(spread, ("dom", "sub"), 0, 0, tiled=True)
+    totals = totals.reshape(dom_count, sub_count, -1).transpose(1, 0, 2).reshape(2, width, classes)
+
     return_table = send_table.astype(jnp.float32)
     incoming = jnp.einsum("pks,pkci->sci", return_table, arrived, precision=lax.Precision.HIGHEST)
     backward_sum = local_grad + incoming

time: 214 us -> 259 us (1.21); the launches traced: 211 us -> 258 us
  local copies, waits for them, and re-layouts: 19.8 us -> 58.3 us
  blocking collectives: 22.5 us -> 0 us
  other arithmetic: 7.93 us -> 29 us
  starting transfers between devices: 22.5 us -> 32.8 us
    unnamed x18 -> x25, local copies, waits for them, and re-layouts: 1.8 us -> 34.5 us
    all_to_all x1 -> x0, blocking collectives: 22.5 us -> none  [per_device(): lax.all_to_all(flat, ('dom', 'sub'), 0, 0, tiled=True)]
    all_to_all x0 -> x3, other arithmetic: none -> 16 us  [the longest x2 12.2 us: per_device(): got = lax.all_to_all(sent, 'sub', 0, 0, tiled=True)]
    all_to_all x3, starting transfers between devices: 13.7 us -> 24 us  [the longest x1 11.8 us: per_device(): got = lax.all_to_all(sent, 'sub', 0, 0, tiled=True)]
    reduce_sum x2 -> x3, other arithmetic: 0.69 us -> 6.91 us  [the longest x1 6.7 us: per_device(): got[:, :local_size].astype(jnp.float32)]
    reshape x2 -> x6, local copies, waits for them, and re-layouts: 4.48 us -> 7.79 us  [the longest x1 2.8 us: per_device(): local = term[:part_blocks, :classes].reshape(sub_count, -1)]
  transfers between devices with their start and end apart: 5 -> 5, of which waited for: 4 -> 4; matrix products, arithmetic and copies ran while one was open for 10% -> 9% of each run, Pallas kernels for 0% -> 0%
where the time goes in v4:
time: 259 us; the launch traced here: 258 us
  waiting for transfers between devices  79.1 us (31%)
  local copies, waits for them, and re-layouts  58.3 us (23%)
  Pallas kernels  39.3 us (15%)
  starting transfers between devices  32.8 us (13%)
  other arithmetic  29 us (11%)
  between operations  14.3 us (6%)
  matrix products  5.56 us (2%)
    pallas_call x1, Pallas kernels, _fused(): pl.pallas_call(functools.partial(_fused_kernel, classes=classes), grid_sp...  39.3 us
    all_to_all x1, waiting for transfers between devices, per_device(): got = lax.all_to_all(sent, 'sub', 0, 0, tiled=True)  35.2 us
    unnamed x25, local copies, waits for them, and re-layouts  34.5 us
    all_to_all x1, waiting for transfers between devices, per_device(): lax.all_to_all(outgoing, 'dom', split_axis=0, concat_axis=0, tiled=True)  23.8 us
    all_to_all x2, other arithmetic, per_device(): got = lax.all_to_all(sent, 'sub', 0, 0, tiled=True)  12.2 us
    all_to_all x1, starting transfers between devices, per_device(): got = lax.all_to_all(sent, 'sub', 0, 0, tiled=True)  11.8 us
    all_to_all x1, waiting for transfers between devices, per_device(): got = lax.all_to_all(sent, 'dom', 0, 0, tiled=True)  11 us
    all_to_all x1, starting transfers between devices, per_device(): lax.all_to_all(outgoing, 'dom', split_axis=0, concat_axis=0, tiled=True)  8.72 us
  transfers between devices with their start and end apart: 5, of which 4 were waited for; matrix products, arithmetic and copies ran while one was open for 9% of the time, Pallas kernels for 0%

profile of v4, /device:TPU:1, one launch (start us, length us, event | category | flops | bytes accessed | tf_op | source)
XLA Modules:
  0.0 258.3 jit_solution(16736325615213051653)
XLA Ops:
  7.2 0.0 all-gather.2.cloned.1.call-start
  7.2 0.7 all-gather.2.cloned.1.call-update
  7.9 1.8 convolution_convert_fusion
  9.7 2.1 copy.57
  11.8 0.0 copy-start.5
  11.8 8.7 %all-to-all-start = ((bf16[16,2,128,256]{3,2,1,0:T(8,128)(2,1)}), bf16[16,2,128,256]{3,2,1,0:T(8,128)(2,1)S(1)}, u32[]{:S(2)}, u32[]{:S(2)}) async-start(bf16[16,2,128,256]{3,2,1,0:T(8,128)(2,1)} %copy.57), calls=%async_computation | async-start | bytes 4194304 | tf_op jit(solution)/shard_map/all_to_all | solution.py:159
  20.5 0.0 copy-done.5
  20.5 1.0 copy.60.deg_ref
  21.6 0.0 copy-done.4
  21.6 1.0 copy.61.lab_ref
  22.6 0.0 copy-done.1
  22.6 0.1 copy.58
  22.7 0.0 copy-done.2
  22.7 0.1 copy.59
  22.8 0.7 pad.11.nw_ref
  23.5 0.7 pad.12.sw_ref
  24.2 0.7 pad.13.swt_ref
  24.8 23.8 %all-to-all-done = bf16[16,2,128,256]{3,2,1,0:T(8,128)(2,1)S(1)} async-done(((bf16[16,2,128,256]{3,2,1,0:T(8,128)(2,1)}), bf16[16,2,128,256]{3,2,1,0:T(8,128)(2,1)S(1)}, u32[]{:S(2)}, u32[]{:S(2)}) %all-to-all-start) | async-done | bytes 2097184 | tf_op jit(solution)/shard_map/all_to_all | solution.py:159
  48.7 5.4 %pad_maximum_fusion.sources_ref = bf16[96,128,256]{2,1,0:T(8,128)(2,1)} fusion(bf16[32,128,256]{2,1,0:T(8,128)(2,1)S(1)} %bitcast.44, bf16[64,128,256]{2,1,0:T(8,128)(2,1)} %all-gather.2.cloned.1.call-done), kind=kLoop, calls=%fused_computation | loop fusion | flops 3145728 | bytes 12582912 | tf_op jit(solution)/shard_map/concatenate | solution.py:161
  54.1 39.3 %shard_map.112 = (bf16[96,176,128]{2,1,0:T(8,128)(2,1)}, f32[2,256,256]{2,1,0:T(8,128)}, f32[8,128,256]{2,1,0:T(8,128)}) custom-call(s32[8,64]{1,0:T(8,128)} %src_ref.1, s32[8]{0:T(128)} %live_ref.1, bf16[8,64,128,128]{3,2,1,0:T(8,128)(2,1)} %w_ref.1, bf16[96,128,256]{2,1,0:T(8,128)(2,1)} %pad_maximum_fusion.sources_ref, bf16[8,128,256]{2,1,0:T(8,128)(2,1)} %bitcast.50, ...), custom_call_target="tpu_custom_call" | custom-call | tf_op jit(solution)/shard_map/pallas_call | solution.py:114
  93.3 2.6 slice.44
  95.9 2.0 slice.41
  97.9 2.7 %reshape.68 = bf16[16,44032]{1,0:T(8,128)(2,1)} reshape(bf16[32,172,128]{2,1,0:T(8,128)(2,1)} %slice.44) | data formatting | bytes 2818048 | tf_op jit(solution)/shard_map/reshape | solution.py:193
  100.6 1.3 reshape.67
  101.9 0.7 subtract_convert_fusion
  102.6 2.8 %reshape.66 = bf16[8,176128]{1,0:T(8,128)(2,1)} reshape(bf16[64,172,128]{2,1,0:T(8,128)(2,1)S(1)} %slice.41) | data formatting | bytes 5636096 | tf_op jit(solution)/shard_map/reshape | solution.py:185
  105.4 8.3 %maximum_bitcast_fusion = bf16[8,1,198144]{2,0,1:T(8,128)(2,1)S(1)} fusion(bf16[8,11008]{1,0:T(8,128)(2,1)S(1)} %get-tuple-element.23, bf16[8,11008]{1,0:T(8,128)(2,1)} %get-tuple-element.24, bf16[8,176128]{1,0:T(8,128)(2,1)} %reshape.66), kind=kLoop, calls=%fused_computation.2 | loop fusion | flops 9510912 | bytes 6340608 | tf_op jit(solution)/shard_map/all_to_all | solution.py:188
  113.8 0.5 broadcast.18
  114.3 3.8 %reduce.1 = bf16[8,198144]{1,0:T(8,128)(2,1)} reduce(bf16[8,1,198144]{2,0,1:T(8,128)(2,1)S(1)} %maximum_bitcast_fusion, bf16[]{:T(256)} %broadcast.18), dimensions={1}, to_apply=%copy.62.reduce_sub_computation | reduce | bytes 6340610 | tf_op jit(solution)/shard_map/all_to_all | solution.py:188
  118.1 4.3 %reshape.76 = bf16[8,2,99072]{2,1,0:T(2,128)(2,1)} reshape(bf16[8,198144]{1,0:T(8,128)(2,1)} %reduce.1) | data formatting | bytes 6340608
  122.5 11.8 %all-to-all-start.1 = ((bf16[8,2,99072]{2,1,0:T(2,128)(2,1)}), bf16[8,2,99072]{2,1,0:T(2,128)(2,1)S(1)}, u32[]{:S(2)}, u32[]{:S(2)}) async-start(bf16[8,2,99072]{2,1,0:T(2,128)(2,1)} %reshape.76), calls=%async_computation.1 | async-start | bytes 6340608 | tf_op jit(solution)/shard_map/all_to_all | solution.py:188
  134.3 2.5 constant_dynamic-update-slice_fusion
  136.8 35.2 %all-to-all-done.1 = bf16[8,2,99072]{2,1,0:T(2,128)(2,1)S(1)} async-done(((bf16[8,2,99072]{2,1,0:T(2,128)(2,1)}), bf16[8,2,99072]{2,1,0:T(2,128)(2,1)S(1)}, u32[]{:S(2)}, u32[]{:S(2)}) %all-to-all-start.1) | async-done | bytes 3170336 | tf_op jit(solution)/shard_map/all_to_all | solution.py:188
  172.0 7.1 %reshape.77 = bf16[8,1,198144]{2,1,0:T(2,128)(2,1)} reshape(bf16[8,2,99072]{2,1,0:T(2,128)(2,1)S(1)} %all-to-all-done.1) | data formatting | bytes 6340608
  179.1 3.7 %copy.92 = bf16[8,1,198144]{2,0,1:T(8,128)(2,1)S(1)} copy(bf16[8,1,198144]{2,1,0:T(2,128)(2,1)} %reshape.77) | data formatting | bytes 6340608
  182.8 0.1 add_reduce_fusion
  183.0 0.1 reshape.69
  183.1 1.4 dynamic-update-slice.1
  184.5 1.5 dynamic-update-slice.2
  186.0 3.8 %reduce.2 = bf16[16,45408]{1,0:T(8,128)(2,1)} reduce(bf16[16,1,45408]{2,0,1:T(8,128)(2,1)} %bitcast.47, bf16[]{:T(256)} %broadcast.18), dimensions={1}, to_apply=%copy.63.reduce_sub_computation | reduce | bytes 2906114 | tf_op jit(solution)/shard_map/all_to_all | solution.py:196
  189.7 3.4 %reshape.78 = bf16[16,2,22704]{2,1,0:T(2,128)(2,1)} reshape(bf16[16,45408]{1,0:T(8,128)(2,1)} %reduce.2) | data formatting | bytes 2906112
  193.1 4.9 %all-to-all-start.2 = ((bf16[16,2,22704]{2,1,0:T(2,128)(2,1)}), bf16[16,2,22704]{2,1,0:T(2,128)(2,1)}, u32[]{:S(2)}, u32[]{:S(2)}) async-start(bf16[16,2,22704]{2,1,0:T(2,128)(2,1)} %reshape.78), calls=%async_computation.2 | async-start | bytes 2916352 | tf_op jit(solution)/shard_map/all_to_all | solution.py:196
  198.0 6.7 %convert_reduce_fusion = f32[176128]{0:T(1024)} fusion(bf16[8,198144]{1,0:T(8,128)(2,1)S(1)} %bitcast.43), kind=kLoop, calls=%fused_computation.1 | loop fusion | flops 2641920 | bytes 3522560 | tf_op jit(solution)/shard_map/reduce_sum | solution.py:190
  204.7 2.0 reduce_sum.30
  206.7 11.0 %all-to-all-done.2 = bf16[16,2,22704]{2,1,0:T(2,128)(2,1)} async-done(((bf16[16,2,22704]{2,1,0:T(2,128)(2,1)}), bf16[16,2,22704]{2,1,0:T(2,128)(2,1)}, u32[]{:S(2)}, u32[]{:S(2)}) %all-to-all-start.2) | async-done | bytes 1453088 | tf_op jit(solution)/shard_map/all_to_all | solution.py:196
  217.7 10.1 %reshape.79 = bf16[16,1,45408]{2,1,0:T(2,128)(2,1)S(1)} reshape(bf16[16,2,22704]{2,1,0:T(2,128)(2,1)} %all-to-all-done.2) | data formatting | bytes 2906112
  227.8 0.2 copy.93
  227.9 0.0 copy-start.3
  227.9 0.1 slice.55
  228.0 0.1 add_reduce_fusion.1
  228.1 0.7 reshape.70
  228.9 0.0 copy-start
  228.9 1.0 broadcast_in_dim.2
  229.9 7.3 %all-to-all-start.3 = ((f32[128,1,688]{2,1,0:T(1,128)}), f32[128,1,688]{2,1,0:T(1,128)S(1)}, u32[]{:S(2)}, u32[]{:S(2)}) async-start(f32[128,1,688]{2,1,0:T(1,128)} %broadcast_in_dim.2), calls=%async_computation.3 | async-start | bytes 786432 | tf_op jit(solution)/shard_map/all_to_all | solution.py:200
  237.2 0.0 copy-done.3
  237.2 1.7 fusion.5
  238.9 0.0 copy-done
  238.9 2.0 convolution_add_fusion
  241.0 8.4 %all-to-all-done.3 = f32[128,1,688]{2,1,0:T(1,128)S(1)} async-done(((f32[128,1,688]{2,1,0:T(1,128)}), f32[128,1,688]{2,1,0:T(1,128)S(1)}, u32[]{:S(2)}, u32[]{:S(2)}) %all-to-all-start.3) | async-done | bytes 352288 | tf_op jit(solution)/shard_map/all_to_all | solution.py:200
  249.4 0.1 copy.95
  249.6 0.1 mul.13
  249.8 0.8 copy.68
  250.5 0.1 mul.15
  250.7 0.8 copy.69
  (8 shorter events, 0.1 us)
Async XLA Ops:
  7.2 41.5 %all-gather.2.cloned.1.call-start = ((), (), s32[]{:S(2)}) async-start(), calls=%async_computation.4 | async-start | bytes 4718592 | tf_op jit(solution)/shard_map/all_gather | solution.py:149
  11.8 8.7 %copy-start.5 = (s32[1024]{0:T(1024)S(1)}, s32[1024]{0:T(1024)}, u32[]{:S(2)}) copy-start(s32[1024]{0:T(1024)} %param.14) | copy-start | bytes 12292
  11.8 9.8 %copy-start.4 = (s32[1024]{0:T(1024)S(1)}, s32[1024]{0:T(1024)}, u32[]{:S(2)}) copy-start(s32[1024]{0:T(1024)} %param.15) | copy-start | bytes 12292
  11.8 10.8 %copy-start.1 = (bf16[256,172]{0,1:T(8,128)(2,1)S(1)}, bf16[256,172]{0,1:T(8,128)(2,1)}, u32[]{:S(2)}) copy-start(bf16[256,172]{0,1:T(8,128)(2,1)} %param.16) | copy-start | bytes 264196
  11.8 10.9 %copy-start.2 = (bf16[256,172]{0,1:T(8,128)(2,1)S(1)}, bf16[256,172]{0,1:T(8,128)(2,1)}, u32[]{:S(2)}) copy-start(bf16[256,172]{0,1:T(8,128)(2,1)} %param.17) | copy-start | bytes 264196
  11.8 36.9 %all-to-all-start = ((bf16[16,2,128,256]{3,2,1,0:T(8,128)(2,1)}), bf16[16,2,128,256]{3,2,1,0:T(8,128)(2,1)S(1)}, u32[]{:S(2)}, u32[]{:S(2)}) async-start(bf16[16,2,128,256]{3,2,1,0:T(8,128)(2,1)} %copy.57), calls=%async_computation | async-start | bytes 4194304 | tf_op jit(solution)/shard_map/all_to_all | solution.py:159
  122.5 49.5 %all-to-all-start.1 = ((bf16[8,2,99072]{2,1,0:T(2,128)(2,1)}), bf16[8,2,99072]{2,1,0:T(2,128)(2,1)S(1)}, u32[]{:S(2)}, u32[]{:S(2)}) async-start(bf16[8,2,99072]{2,1,0:T(2,128)(2,1)} %reshape.76), calls=%async_computation.1 | async-start | bytes 6340608 | tf_op jit(solution)/shard_map/all_to_all | solution.py:188
  193.1 24.6 %all-to-all-start.2 = ((bf16[16,2,22704]{2,1,0:T(2,128)(2,1)}), bf16[16,2,22704]{2,1,0:T(2,128)(2,1)}, u32[]{:S(2)}, u32[]{:S(2)}) async-start(bf16[16,2,22704]{2,1,0:T(2,128)(2,1)} %reshape.78), calls=%async_computation.2 | async-start | bytes 2916352 | tf_op jit(solution)/shard_map/all_to_all | solution.py:196
  227.9 9.3 %copy-start.3 = (s32[1,16,2]{1,2,0:T(2,128)S(1)}, s32[1,16,2]{1,2,0:T(2,128)}, u32[]{:S(2)}) copy-start(s32[1,16,2]{1,2,0:T(2,128)} %param.13) | copy-start | bytes 388
  228.9 10.0 %copy-start = (f32[8,128,256]{2,1,0:T(8,128)S(1)}, f32[8,128,256]{2,1,0:T(8,128)}, u32[]{:S(2)}) copy-start(f32[8,128,256]{2,1,0:T(8,128)} %get-tuple-element.8) | copy-start | bytes 3145732
  229.9 19.5 %all-to-all-start.3 = ((f32[128,1,688]{2,1,0:T(1,128)}), f32[128,1,688]{2,1,0:T(1,128)S(1)}, u32[]{:S(2)}, u32[]{:S(2)}) async-start(f32[128,1,688]{2,1,0:T(1,128)} %broadcast_in_dim.2), calls=%async_computation.3 | async-start | bytes 786432 | tf_op jit(solution)/shard_map/all_to_all | solution.py:200
Sparse Core Ops, SparseCore 0:
  9.7 35.6 all-gather.1

commit v5 on v3

--- a/solution.py
+++ b/solution.py
@@ -171,23 +171,40 @@
         tile_source, tile_live, tile_weight, sources, own_blocks, degrees, lab, nw, sw, swt, classes
     )
 
-    flat = grads[:, :, :classes].reshape(devices_all, -1)
-    mine = lax.all_to_all(flat, ("dom", "sub"), 0, 0, tiled=True).sum(axis=0, keepdims=True)
-    spread = jnp.broadcast_to(mine, (devices_all, mine.shape[1]))
-    totals = lax.all_to_all(spread, ("dom", "sub"), 0, 0, tiled=True).reshape(2, width, classes)
     norm_factor = float(nodes_all) ** (-0.5)
-
-    local = term[:part_blocks, :classes]
-    local = local.reshape(sub_count, block_count, classes, block_rows)
-    local_grad = (
-        lax.all_to_all(local, "sub", 0, 0, tiled=True).astype(jnp.float32).sum(axis=0)
-    )
-    halo = term[part_blocks:, :classes]
-    halo = halo.reshape(dom_count, slot_count, classes, block_rows)
-    arrived = lax.all_to_all(halo, "dom", 0, 0, tiled=True).astype(jnp.float32)
+    kept = term.shape[1]
+
+    def split(x, size):
+        hi = x.astype(jnp.bfloat16)
+        pair = jnp.concatenate([hi, (x - hi.astype(jnp.float32)).astype(jnp.bfloat16)], axis=-1)
+        return jnp.pad(pair, ((0, 0), (0, size - pair.shape[1])))
+
+    def joined(x, half):
+        return x[:, :half].astype(jnp.float32) + x[:, half : 2 * half].astype(jnp.float32)
+
+    flat = grads[:, :, :classes].reshape(sub_count, -1)
+    chunk = flat.shape[1]
+    extra = split(flat, kept * block_rows).reshape(sub_count, 1, kept, block_rows)
+    local = term[:part_blocks].reshape(sub_count, block_count, kept, block_rows)
+    got = lax.all_to_all(jnp.concatenate([local, extra], axis=1), "sub", 0, 0, tiled=True)
+    local_grad = got[:, :block_count].astype(jnp.float32).sum(axis=0)
+    part_sum = joined(got[:, block_count].reshape(sub_count, -1), chunk).sum(axis=0)
+    part_sum = part_sum.reshape(dom_count, -1)
+    piece = part_sum.shape[1]
+    extra_rows = -(-2 * piece // (16 * block_rows)) * 16
+    extra = split(part_sum, extra_rows * block_rows).reshape(dom_count, extra_rows, block_rows)
+    halo = term[part_blocks:].reshape(dom_count, slot_count * kept, block_rows)
+    got = lax.all_to_all(jnp.concatenate([halo, extra], axis=1), "dom", 0, 0, tiled=True)
+    arrived = got[:, : slot_count * kept].astype(jnp.float32)
+    arrived = arrived.reshape(dom_count, slot_count, kept, block_rows)
+    mine = joined(got[:, slot_count * kept :].reshape(dom_count, -1), piece).sum(axis=0, keepdims=True)
+    spread = jnp.broadcast_to(mine, (devices_all, piece))
+    totals = lax.all_to_all(spread, ("dom", "sub"), 0, 0, tiled=True)
+    totals = totals.reshape(dom_count, sub_count, -1).transpose(1, 0, 2).reshape(2, width, classes)
+
     return_table = send_table.astype(jnp.float32)
     incoming = jnp.einsum("pks,pkci->sci", return_table, arrived, precision=lax.Precision.HIGHEST)
-    backward_sum = local_grad + incoming
+    backward_sum = (local_grad + incoming)[:, :classes]
     neigh_float = neigh_weight.astype(jnp.float32)
     grad_history = jnp.einsum(
         "sci,fc->sif", backward_sum, neigh_float, precision=lax.Precision.HIGHEST

time: 214 us -> 209 us (0.977)
  blocking collectives: 22.5 us -> 0 us
  waiting for transfers between devices: 76.7 us -> 89.3 us
  starting transfers between devices: 22.5 us -> 27.6 us
  other arithmetic: 7.93 us -> 11.8 us
    all_to_all x1 -> x0, blocking collectives: 22.5 us -> none  [per_device(): lax.all_to_all(flat, ('dom', 'sub'), 0, 0, tiled=True)]
    all_to_all x3, waiting for transfers between devices: 52.2 us -> 64.8 us  [the longest x1 35.9 us: per_device(): lax.all_to_all(jnp.concatenate([local, extra], axis=1), 'sub', 0, 0, tile...]
    all_to_all x3, starting transfers between devices: 13.7 us -> 18.9 us  [the longest x1 7.49 us: per_device(): totals = lax.all_to_all(spread, ('dom', 'sub'), 0, 0, tiled=True)]
    concatenate x0 -> x2, other arithmetic: none -> 4.54 us  [the longest x1 2.59 us: per_device(): jnp.concatenate([halo, extra], axis=1)]
    slice x2 -> x4, local copies, waits for them, and re-layouts: 3.46 us -> 6.87 us  [the longest x1 2.56 us: per_device(): halo = term[part_blocks:].reshape(dom_count, slot_count * kept, block_rows)]
    reshape x2 -> x4, local copies, waits for them, and re-layouts: 4.48 us -> 1.61 us  [the longest x1 1.34 us: per_device(): flat = grads[:, :, :classes].reshape(sub_count, -1)]
  transfers between devices with their start and end apart: 5 -> 5, of which waited for: 4 -> 4; matrix products, arithmetic and copies ran while one was open for 10% -> 7% of each run, Pallas kernels for 0% -> 0%
where the time goes in v5:
time: 209 us; the launch traced here: 207 us
  waiting for transfers between devices  89.3 us (43%)
  Pallas kernels  41.9 us (20%)
  starting transfers between devices  27.6 us (13%)
  local copies, waits for them, and re-layouts  17.8 us (9%)
  between operations  14.3 us (7%)
  other arithmetic  11.8 us (6%)
  matrix products  4.35 us (2%)
    pallas_call x1, Pallas kernels, _fused(): pl.pallas_call(functools.partial(_fused_kernel, classes=classes), grid_sp...  41.9 us
    all_to_all x1, waiting for transfers between devices, per_device(): lax.all_to_all(jnp.concatenate([local, extra], axis=1), 'sub', 0, 0, tile...  35.9 us
    all_to_all x1, waiting for transfers between devices, per_device(): lax.all_to_all(outgoing, 'dom', split_axis=0, concat_axis=0, tiled=True)  23.8 us
    all_to_all x1, waiting for transfers between devices, per_device(): lax.all_to_all(jnp.concatenate([halo, extra], axis=1), 'dom', 0, 0, tiled...  18.9 us
    all_to_all x1, waiting for transfers between devices, per_device(): totals = lax.all_to_all(spread, ('dom', 'sub'), 0, 0, tiled=True)  9.91 us
    all_to_all x1, starting transfers between devices, per_device(): lax.all_to_all(outgoing, 'dom', split_axis=0, concat_axis=0, tiled=True)  8.74 us
    all_to_all x1, starting transfers between devices, per_device(): totals = lax.all_to_all(spread, ('dom', 'sub'), 0, 0, tiled=True)  7.49 us
    all_to_all x1, starting transfers between devices, per_device(): lax.all_to_all(jnp.concatenate([local, extra], axis=1), 'sub', 0, 0, tile...  6.56 us
  transfers between devices with their start and end apart: 5, of which 4 were waited for; matrix products, arithmetic and copies ran while one was open for 7% of the time, Pallas kernels for 0%

profile of v5, /device:TPU:1, one launch (start us, length us, event | category | flops | bytes accessed | tf_op | source)
XLA Modules:
  0.0 207.0 jit_solution(6536045306815568241)
XLA Ops:
  7.2 0.0 all-gather.2.cloned.1.call-start
  7.2 0.7 all-gather.2.cloned.1.call-update
  7.9 1.8 convolution_convert_fusion
  9.7 2.0 copy.68
  11.7 0.0 copy-start.6
  11.8 0.0 copy-start.4
  11.8 0.0 copy-start.2
  11.8 0.0 copy-start.3
  11.8 8.7 %all-to-all-start = ((bf16[16,2,128,256]{3,2,1,0:T(8,128)(2,1)}), bf16[16,2,128,256]{3,2,1,0:T(8,128)(2,1)S(1)}, u32[]{:S(2)}, u32[]{:S(2)}) async-start(bf16[16,2,128,256]{3,2,1,0:T(8,128)(2,1)} %copy.68), calls=%async_computation | async-start | bytes 4194304 | tf_op jit(solution)/shard_map/all_to_all | solution.py:159
  20.5 0.0 copy-done.6
  20.5 1.0 copy.71.deg_ref
  21.6 0.0 copy-done.4
  21.6 1.0 copy.72.lab_ref
  22.6 0.0 copy-done.2
  22.6 0.1 copy.69
  22.7 0.0 copy-done.3
  22.7 0.1 copy.70
  22.8 0.7 pad.19.nw_ref
  23.5 0.7 pad.20.sw_ref
  24.2 0.7 pad.21.swt_ref
  24.8 23.8 %all-to-all-done = bf16[16,2,128,256]{3,2,1,0:T(8,128)(2,1)S(1)} async-done(((bf16[16,2,128,256]{3,2,1,0:T(8,128)(2,1)}), bf16[16,2,128,256]{3,2,1,0:T(8,128)(2,1)S(1)}, u32[]{:S(2)}, u32[]{:S(2)}) %all-to-all-start) | async-done | bytes 2097184 | tf_op jit(solution)/shard_map/all_to_all | solution.py:159
  48.7 0.0 all-gather.2.cloned.1.call-done
  48.7 5.4 %pad_maximum_fusion.sources_ref = bf16[96,128,256]{2,1,0:T(8,128)(2,1)} fusion(bf16[32,128,256]{2,1,0:T(8,128)(2,1)S(1)} %bitcast.51, bf16[64,128,256]{2,1,0:T(8,128)(2,1)} %all-gather.2.cloned.1.call-done), kind=kLoop, calls=%fused_computation | loop fusion | flops 3145728 | bytes 12582912 | tf_op jit(solution)/shard_map/concatenate | solution.py:161
  54.0 41.9 %shard_map.112 = (bf16[96,176,128]{2,1,0:T(8,128)(2,1)}, f32[2,256,256]{2,1,0:T(8,128)}, f32[8,128,256]{2,1,0:T(8,128)}) custom-call(s32[8,64]{1,0:T(8,128)} %src_ref.1, s32[8]{0:T(128)} %live_ref.1, bf16[8,64,128,128]{3,2,1,0:T(8,128)(2,1)} %w_ref.1, bf16[96,128,256]{2,1,0:T(8,128)(2,1)} %pad_maximum_fusion.sources_ref, bf16[8,128,256]{2,1,0:T(8,128)(2,1)} %bitcast.56, ...), custom_call_target="tpu_custom_call" | custom-call | tf_op jit(solution)/shard_map/pallas_call | solution.py:114
  96.0 1.3 reshape.70
  97.4 2.0 slice.44
  99.4 2.0 pad_maximum_fusion.1
  101.4 6.6 %all-to-all-start.1 = ((bf16[8,9,176,128]{3,2,1,0:T(8,128)(2,1)}), bf16[8,9,176,128]{3,2,1,0:T(8,128)(2,1)S(1)}, u32[]{:S(2)}, u32[]{:S(2)}) async-start(bf16[8,9,176,128]{3,2,1,0:T(8,128)(2,1)} %pad_maximum_fusion.1), calls=%async_computation.1 | async-start | bytes 6488064 | tf_op jit(solution)/shard_map/all_to_all | solution.py:189
  107.9 2.6 %slice.47 = bf16[32,176,128]{2,1,0:T(8,128)(2,1)} slice(bf16[96,176,128]{2,1,0:T(8,128)(2,1)} %get-tuple-element.6), slice={[64:96], [0:176], [0:128]} | slice | bytes 2883584 | tf_op jit(solution)/shard_map/slice | solution.py:196
  110.5 35.9 %all-to-all-done.1 = bf16[8,9,176,128]{3,2,1,0:T(8,128)(2,1)S(1)} async-done(((bf16[8,9,176,128]{3,2,1,0:T(8,128)(2,1)}), bf16[8,9,176,128]{3,2,1,0:T(8,128)(2,1)S(1)}, u32[]{:S(2)}, u32[]{:S(2)}) %all-to-all-start.1) | async-done | bytes 3244064 | tf_op jit(solution)/shard_map/all_to_all | solution.py:189
  146.5 0.1 copy.104
  146.6 0.1 add_reduce_fusion
  146.7 0.1 reshape.73
  146.8 0.1 fusion.16
  146.9 2.6 %pad_maximum_fusion.2 = bf16[16,368,128]{2,1,0:T(8,128)(2,1)} fusion(bf16[16,16,128]{2,1,0:T(8,128)(2,1)S(1)} %bitcast.64, bf16[16,352,128]{2,1,0:T(8,128)(2,1)} %bitcast.52), kind=kLoop, calls=%fused_computation.4 | loop fusion | flops 3014656 | bytes 3014656 | tf_op jit(solution)/shard_map/concatenate | solution.py:197
  149.5 4.8 %all-to-all-start.2 = ((bf16[16,368,128]{2,1,0:T(8,128)(2,1)}), bf16[16,368,128]{2,1,0:T(8,128)(2,1)}, u32[]{:S(2)}, u32[]{:S(2)}) async-start(bf16[16,368,128]{2,1,0:T(8,128)(2,1)} %pad_maximum_fusion.2), calls=%async_computation.2 | async-start | bytes 3014656 | tf_op jit(solution)/shard_map/all_to_all | solution.py:197
  154.3 0.0 copy-start.5
  154.3 1.2 convert_reduce_fusion
  155.6 0.0 copy-start
  155.6 18.9 %all-to-all-done.2 = bf16[16,368,128]{2,1,0:T(8,128)(2,1)} async-done(((bf16[16,368,128]{2,1,0:T(8,128)(2,1)}), bf16[16,368,128]{2,1,0:T(8,128)(2,1)}, u32[]{:S(2)}, u32[]{:S(2)}) %all-to-all-start.2) | async-done | bytes 1507360 | tf_op jit(solution)/shard_map/all_to_all | solution.py:197
  174.5 1.5 slice.62
  175.9 0.0 copy-start.1
  176.0 0.0 copy-done.5
  176.0 0.5 fusion.2
  176.5 0.8 slice.65
  177.4 0.1 add_reduce_fusion.1
  177.4 0.9 broadcast_in_dim.2
  178.4 7.5 %all-to-all-start.3 = ((f32[128,1,688]{2,1,0:T(1,128)}), f32[128,1,688]{2,1,0:T(1,128)S(1)}, u32[]{:S(2)}, u32[]{:S(2)}) async-start(f32[128,1,688]{2,1,0:T(1,128)} %broadcast_in_dim.2), calls=%async_computation.3 | async-start | bytes 786432 | tf_op jit(solution)/shard_map/all_to_all | solution.py:202
  185.9 0.0 copy-done
  185.9 0.2 copy_add_fusion
  186.1 0.0 copy-done.1
  186.2 2.0 convolution_add_fusion
  188.2 9.9 %all-to-all-done.3 = f32[128,1,688]{2,1,0:T(1,128)S(1)} async-done(((f32[128,1,688]{2,1,0:T(1,128)}), f32[128,1,688]{2,1,0:T(1,128)S(1)}, u32[]{:S(2)}, u32[]{:S(2)}) %all-to-all-start.3) | async-done | bytes 352288 | tf_op jit(solution)/shard_map/all_to_all | solution.py:202
  198.1 0.1 copy.103
  198.3 0.1 mul.13
  198.5 0.8 copy.78
  199.2 0.1 mul.15
  199.4 0.8 copy.79
  (10 shorter events, 0.2 us)
Async XLA Ops:
  7.2 41.5 %all-gather.2.cloned.1.call-start = ((), (), s32[]{:S(2)}) async-start(), calls=%async_computation.4 | async-start | bytes 4718592 | tf_op jit(solution)/shard_map/all_gather | solution.py:149
  11.7 8.8 %copy-start.6 = (s32[1024]{0:T(1024)S(1)}, s32[1024]{0:T(1024)}, u32[]{:S(2)}) copy-start(s32[1024]{0:T(1024)} %param.14) | copy-start | bytes 12292
  11.8 9.8 %copy-start.4 = (s32[1024]{0:T(1024)S(1)}, s32[1024]{0:T(1024)}, u32[]{:S(2)}) copy-start(s32[1024]{0:T(1024)} %param.15) | copy-start | bytes 12292
  11.8 10.8 %copy-start.2 = (bf16[256,172]{0,1:T(8,128)(2,1)S(1)}, bf16[256,172]{0,1:T(8,128)(2,1)}, u32[]{:S(2)}) copy-start(bf16[256,172]{0,1:T(8,128)(2,1)} %param.16) | copy-start | bytes 264196
  11.8 10.9 %copy-start.3 = (bf16[256,172]{0,1:T(8,128)(2,1)S(1)}, bf16[256,172]{0,1:T(8,128)(2,1)}, u32[]{:S(2)}) copy-start(bf16[256,172]{0,1:T(8,128)(2,1)} %param.17) | copy-start | bytes 264196
  11.8 36.9 %all-to-all-start = ((bf16[16,2,128,256]{3,2,1,0:T(8,128)(2,1)}), bf16[16,2,128,256]{3,2,1,0:T(8,128)(2,1)S(1)}, u32[]{:S(2)}, u32[]{:S(2)}) async-start(bf16[16,2,128,256]{3,2,1,0:T(8,128)(2,1)} %copy.68), calls=%async_computation | async-start | bytes 4194304 | tf_op jit(solution)/shard_map/all_to_all | solution.py:159
  101.4 45.1 %all-to-all-start.1 = ((bf16[8,9,176,128]{3,2,1,0:T(8,128)(2,1)}), bf16[8,9,176,128]{3,2,1,0:T(8,128)(2,1)S(1)}, u32[]{:S(2)}, u32[]{:S(2)}) async-start(bf16[8,9,176,128]{3,2,1,0:T(8,128)(2,1)} %pad_maximum_fusion.1), calls=%async_computation.1 | async-start | bytes 6488064 | tf_op jit(solution)/shard_map/all_to_all | solution.py:189
  149.5 25.0 %all-to-all-start.2 = ((bf16[16,368,128]{2,1,0:T(8,128)(2,1)}), bf16[16,368,128]{2,1,0:T(8,128)(2,1)}, u32[]{:S(2)}, u32[]{:S(2)}) async-start(bf16[16,368,128]{2,1,0:T(8,128)(2,1)} %pad_maximum_fusion.2), calls=%async_computation.2 | async-start | bytes 3014656 | tf_op jit(solution)/shard_map/all_to_all | solution.py:197
  154.3 21.7 %copy-start.5 = (s32[1,16,2]{1,2,0:T(2,128)S(1)}, s32[1,16,2]{1,2,0:T(2,128)}, u32[]{:S(2)}) copy-start(s32[1,16,2]{1,2,0:T(2,128)} %param.13) | copy-start | bytes 388
  155.6 30.3 %copy-start = (f32[8,176,128]{2,1,0:T(8,128)S(1)}, f32[8,176,128]{2,1,0:T(8,128)}, u32[]{:S(2)}) copy-start(f32[8,176,128]{2,1,0:T(8,128)} %convert_reduce_fusion) | copy-start | bytes 2162692
  175.9 10.2 %copy-start.1 = (f32[8,128,256]{2,1,0:T(8,128)S(1)}, f32[8,128,256]{2,1,0:T(8,128)}, u32[]{:S(2)}) copy-start(f32[8,128,256]{2,1,0:T(8,128)} %get-tuple-element.8) | copy-start | bytes 3145732
  178.4 19.7 %all-to-all-start.3 = ((f32[128,1,688]{2,1,0:T(1,128)}), f32[128,1,688]{2,1,0:T(1,128)S(1)}, u32[]{:S(2)}, u32[]{:S(2)}) async-start(f32[128,1,688]{2,1,0:T(1,128)} %broadcast_in_dim.2), calls=%async_computation.3 | async-start | bytes 786432 | tf_op jit(solution)/shard_map/all_to_all | solution.py:202
Sparse Core Ops, SparseCore 0:
  9.7 35.6 all-gather.1

commit v6 on v5

--- a/solution.py
+++ b/solution.py
@@ -182,13 +182,11 @@
     def joined(x, half):
         return x[:, :half].astype(jnp.float32) + x[:, half : 2 * half].astype(jnp.float32)
 
+    local_grad = lax.psum_scatter(
+        term[:part_blocks], "sub", scatter_dimension=0, tiled=True
+    ).astype(jnp.float32)
     flat = grads[:, :, :classes].reshape(sub_count, -1)
-    chunk = flat.shape[1]
-    extra = split(flat, kept * block_rows).reshape(sub_count, 1, kept, block_rows)
-    local = term[:part_blocks].reshape(sub_count, block_count, kept, block_rows)
-    got = lax.all_to_all(jnp.concatenate([local, extra], axis=1), "sub", 0, 0, tiled=True)
-    local_grad = got[:, :block_count].astype(jnp.float32).sum(axis=0)
-    part_sum = joined(got[:, block_count].reshape(sub_count, -1), chunk).sum(axis=0)
+    part_sum = lax.all_to_all(flat, "sub", 0, 0, tiled=True).sum(axis=0)
     part_sum = part_sum.reshape(dom_count, -1)
     piece = part_sum.shape[1]
     extra_rows = -(-2 * piece // (16 * block_rows)) * 16

time: 209 us -> 176 us (0.84)
  waiting for transfers between devices: 89.3 us -> 44.2 us
  blocking collectives: 0 us -> 22.7 us
  other arithmetic: 11.8 us -> 5.95 us
  starting transfers between devices: 27.6 us -> 24.4 us
    all_to_all x2 -> x1, waiting for transfers between devices: 54.9 us -> 8.1 us  [per_device(): part_sum = lax.all_to_all(flat, 'sub', 0, 0, tiled=True).sum(axis=0)]
    all_to_all x0 -> x1, blocking collectives: none -> 22.7 us  [per_device(): lax.all_to_all(jnp.concatenate([halo, extra], axis=1), 'dom', 0, 0, tiled...]
    concatenate x1, other arithmetic: 2.59 us -> 0.1 us  [per_device(): jnp.concatenate([halo, extra], axis=1)]
    all_to_all x2 -> x1, starting transfers between devices: 11.4 us -> 9.17 us  [per_device(): part_sum = lax.all_to_all(flat, 'sub', 0, 0, tiled=True).sum(axis=0)]
  transfers between devices with their start and end apart: 5 -> 5, of which waited for: 4 -> 3; matrix products, arithmetic and copies ran while one was open for 7% -> 8% of each run, Pallas kernels for 0% -> 0%
where the time goes in v6:
time: 176 us
  waiting for transfers between devices  44.2 us (25%)
  Pallas kernels  42 us (24%)
  starting transfers between devices  24.4 us (14%)
  blocking collectives  22.7 us (13%)
  local copies, waits for them, and re-layouts  17.2 us (10%)
  between operations  14.2 us (8%)
  other arithmetic  5.95 us (3%)
  matrix products  5.34 us (3%)
    pallas_call x1, Pallas kernels, _fused(): pl.pallas_call(functools.partial(_fused_kernel, classes=classes), grid_sp...  42 us
    all_to_all x1, waiting for transfers between devices, per_device(): lax.all_to_all(outgoing, 'dom', split_axis=0, concat_axis=0, tiled=True)  23.8 us
    all_to_all x1, blocking collectives, per_device(): lax.all_to_all(jnp.concatenate([halo, extra], axis=1), 'dom', 0, 0, tiled...  22.7 us
    all_to_all x1, waiting for transfers between devices, per_device(): totals = lax.all_to_all(spread, ('dom', 'sub'), 0, 0, tiled=True)  11.6 us
    all_to_all x1, starting transfers between devices, per_device(): part_sum = lax.all_to_all(flat, 'sub', 0, 0, tiled=True).sum(axis=0)  9.17 us
    all_to_all x1, starting transfers between devices, per_device(): lax.all_to_all(outgoing, 'dom', split_axis=0, concat_axis=0, tiled=True)  8.74 us
    all_to_all x1, waiting for transfers between devices, per_device(): part_sum = lax.all_to_all(flat, 'sub', 0, 0, tiled=True).sum(axis=0)  8.1 us
    all_to_all x1, starting transfers between devices, per_device(): totals = lax.all_to_all(spread, ('dom', 'sub'), 0, 0, tiled=True)  6.39 us
  transfers between devices with their start and end apart: 5, of which 3 were waited for; matrix products, arithmetic and copies ran while one was open for 8% of the time, Pallas kernels for 0%

profile of v6, /device:TPU:1, one launch (start us, length us, event | category | flops | bytes accessed | tf_op | source)
XLA Modules:
  0.0 176.0 jit_solution(899812930887495280)
XLA Ops:
  7.2 0.0 all-gather.2.cloned.1.call-start
  7.2 0.7 all-gather.2.cloned.1.call-update
  7.9 1.8 %convolution_convert_fusion = bf16[16,2,128,256]{3,0,2,1:T(8,128)(2,1)S(1)} fusion(bf16[8,128,256]{2,1,0:T(8,128)(2,1)} %bitcast.44, s32[16,2]{0,1:T(2,128)} %bitcast.55), kind=kOutput, calls=%fused_computation.1 | convolution fusion | flops 17826048 | bytes 2621568 | tf_op jit(solution)/shard_map/pks,sif->pkif/dot_general | solution.py:153
  9.7 2.0 %copy.52 = bf16[16,2,128,256]{3,2,1,0:T(8,128)(2,1)} copy(bf16[16,2,128,256]{3,0,2,1:T(8,128)(2,1)S(1)} %convolution_convert_fusion) | data formatting | bytes 4194304 | tf_op jit(solution)/shard_map/convert_element_type | solution.py:158
  11.7 0.0 copy-start.6
  11.8 0.0 copy-start.4
  11.8 0.0 copy-start.2
  11.8 0.0 copy-start.3
  11.8 8.7 %all-to-all-start = ((bf16[16,2,128,256]{3,2,1,0:T(8,128)(2,1)}), bf16[16,2,128,256]{3,2,1,0:T(8,128)(2,1)S(1)}, u32[]{:S(2)}, u32[]{:S(2)}) async-start(bf16[16,2,128,256]{3,2,1,0:T(8,128)(2,1)} %copy.52), calls=%async_computation | async-start | bytes 4194304 | tf_op jit(solution)/shard_map/all_to_all | solution.py:159
  20.5 0.0 reduce-scatter.2.cloned.1.call-start
  20.6 0.0 copy-done.6
  20.6 1.0 copy.55.deg_ref
  21.6 0.0 copy-done.4
  21.6 1.0 copy.56.lab_ref
  22.6 0.0 copy-done.2
  22.6 0.1 copy.53
  22.7 0.0 copy-done.3
  22.7 0.1 copy.54
  22.9 0.7 pad.15.nw_ref
  23.5 0.7 pad.16.sw_ref
  24.2 0.7 pad.17.swt_ref
  24.9 23.8 %all-to-all-done = bf16[16,2,128,256]{3,2,1,0:T(8,128)(2,1)S(1)} async-done(((bf16[16,2,128,256]{3,2,1,0:T(8,128)(2,1)}), bf16[16,2,128,256]{3,2,1,0:T(8,128)(2,1)S(1)}, u32[]{:S(2)}, u32[]{:S(2)}) %all-to-all-start) | async-done | bytes 2097184 | tf_op jit(solution)/shard_map/all_to_all | solution.py:159
  48.7 0.0 all-gather.2.cloned.1.call-done
  48.7 5.4 %pad_maximum_fusion.sources_ref = bf16[96,128,256]{2,1,0:T(8,128)(2,1)} fusion(bf16[32,128,256]{2,1,0:T(8,128)(2,1)S(1)} %bitcast.40, bf16[64,128,256]{2,1,0:T(8,128)(2,1)} %all-gather.2.cloned.1.call-done), kind=kLoop, calls=%fused_computation | loop fusion | flops 3145728 | bytes 12582912 | tf_op jit(solution)/shard_map/concatenate | solution.py:161
  54.0 42.0 %shard_map.112 = (bf16[96,176,128]{2,1,0:T(8,128)(2,1)}, f32[2,256,256]{2,1,0:T(8,128)}, f32[8,128,256]{2,1,0:T(8,128)}) custom-call(s32[8,64]{1,0:T(8,128)} %src_ref.1, s32[8]{0:T(128)} %live_ref.1, bf16[8,64,128,128]{3,2,1,0:T(8,128)(2,1)} %w_ref.1, bf16[96,128,256]{2,1,0:T(8,128)(2,1)} %pad_maximum_fusion.sources_ref, bf16[8,128,256]{2,1,0:T(8,128)(2,1)} %bitcast.45, ...), custom_call_target="tpu_custom_call" | custom-call | tf_op jit(solution)/shard_map/pallas_call | solution.py:114
  96.1 3.6 %slice.32 = bf16[64,176,128]{2,1,0:T(8,128)(2,1)} slice(bf16[96,176,128]{2,1,0:T(8,128)(2,1)} %get-tuple-element.6), slice={[0:64], [0:176], [0:128]} | slice | bytes 5767168 | tf_op jit(solution)/shard_map/slice | solution.py:186
  99.6 0.0 copy-start.1
  99.7 0.0 reduce-scatter.2.cloned.1.call-update
  99.7 1.0 copy-done.1
  100.7 1.5 all_to_all.21
  102.2 9.2 %all-to-all-start.1 = ((f32[8,1,11008]{2,1,0:T(1,128)}), f32[8,1,11008]{2,1,0:T(1,128)S(1)}, u32[]{:S(2)}, u32[]{:S(2)}) async-start(f32[8,1,11008]{2,1,0:T(1,128)} %all_to_all.21), calls=%async_computation.2 | async-start | bytes 704512 | tf_op jit(solution)/shard_map/all_to_all | solution.py:189
  111.4 1.5 slice.33
  112.9 8.1 %all-to-all-done.1 = f32[8,1,11008]{2,1,0:T(1,128)S(1)} async-done(((f32[8,1,11008]{2,1,0:T(1,128)}), f32[8,1,11008]{2,1,0:T(1,128)S(1)}, u32[]{:S(2)}, u32[]{:S(2)}) %all-to-all-start.1) | async-done | bytes 352288 | tf_op jit(solution)/shard_map/all_to_all | solution.py:189
  121.0 0.3 reduce_sum.18
  121.3 0.1 reshape.65
  121.4 0.1 fusion.13
  121.5 0.1 pad_maximum_fusion.1
  121.6 22.7 %all_to_all.26 = bf16[16,368,128]{2,1,0:T(8,128)(2,1)S(1)} all-to-all(bf16[16,368,128]{2,1,0:T(8,128)(2,1)S(1)} %pad_maximum_fusion.1), channel_id=1, replica_groups=mesh['dom'=16,'sub'=8] {'dom'}, dimensions={0} | all-to-all | bytes 3014656 | tf_op jit(solution)/shard_map/all_to_all | solution.py:195
  144.3 0.0 copy-start.5
  144.3 0.1 add_reduce_fusion
  144.4 1.0 broadcast_in_dim.2
  145.3 6.4 %all-to-all-start.3 = ((f32[128,1,688]{2,1,0:T(1,128)}), f32[128,1,688]{2,1,0:T(1,128)S(1)}, u32[]{:S(2)}, u32[]{:S(2)}) async-start(f32[128,1,688]{2,1,0:T(1,128)} %broadcast_in_dim.2), calls=%async_computation.4 | async-start | bytes 786432 | tf_op jit(solution)/shard_map/all_to_all | solution.py:200
  151.7 0.1 slice.42
  151.8 0.0 copy-done.5
  151.8 0.5 fusion.2
  152.4 0.0 copy-start
  152.4 11.6 %all-to-all-done.3 = f32[128,1,688]{2,1,0:T(1,128)S(1)} async-done(((f32[128,1,688]{2,1,0:T(1,128)}), f32[128,1,688]{2,1,0:T(1,128)S(1)}, u32[]{:S(2)}, u32[]{:S(2)}) %all-to-all-start.3) | async-done | bytes 352288 | tf_op jit(solution)/shard_map/all_to_all | solution.py:200
  164.1 0.1 copy.83
  164.2 0.1 mul.13
  164.4 0.8 copy.61
  165.2 0.1 mul.15
  165.3 0.8 copy.62
  166.1 0.0 reduce-scatter.2.cloned.1.call-done
  166.1 0.0 copy-done
  166.1 3.0 %convolution_add_fusion = f32[8,128,256]{2,1,0:T(8,128)} fusion(f32[8,128,256]{2,1,0:T(8,128)S(1)} %copy-done, f32[8,172,128]{2,0,1:T(8,128)S(1)} %slice.44, bf16[8,176,128]{2,1,0:T(8,128)(2,1)} %reduce-scatter.2.cloned.1.call-done, bf16[256,172]{0,1:T(8,128)(2,1)S(1)} %copy-done.2), kind=kOutput, calls=%fused_computation.5 | convolution fusion | flops 541679616 | bytes 3250176 | tf_op jit(solution)/shard_map/sci,fc->sif/dot_general | solution.py:207
  (8 shorter events, 0.2 us)
Async XLA Ops:
  7.2 41.5 %all-gather.2.cloned.1.call-start = ((), (), s32[]{:S(2)}) async-start(), calls=%async_computation.5 | async-start | bytes 4718592 | tf_op jit(solution)/shard_map/all_gather | solution.py:149
  11.7 8.8 %copy-start.6 = (s32[1024]{0:T(1024)S(1)}, s32[1024]{0:T(1024)}, u32[]{:S(2)}) copy-start(s32[1024]{0:T(1024)} %param.14) | copy-start | bytes 12292
  11.8 9.9 %copy-start.4 = (s32[1024]{0:T(1024)S(1)}, s32[1024]{0:T(1024)}, u32[]{:S(2)}) copy-start(s32[1024]{0:T(1024)} %param.15) | copy-start | bytes 12292
  11.8 10.9 %copy-start.2 = (bf16[256,172]{0,1:T(8,128)(2,1)S(1)}, bf16[256,172]{0,1:T(8,128)(2,1)}, u32[]{:S(2)}) copy-start(bf16[256,172]{0,1:T(8,128)(2,1)} %param.16) | copy-start | bytes 264196
  11.8 11.0 %copy-start.3 = (bf16[256,172]{0,1:T(8,128)(2,1)S(1)}, bf16[256,172]{0,1:T(8,128)(2,1)}, u32[]{:S(2)}) copy-start(bf16[256,172]{0,1:T(8,128)(2,1)} %param.17) | copy-start | bytes 264196
  11.8 36.9 %all-to-all-start = ((bf16[16,2,128,256]{3,2,1,0:T(8,128)(2,1)}), bf16[16,2,128,256]{3,2,1,0:T(8,128)(2,1)S(1)}, u32[]{:S(2)}, u32[]{:S(2)}) async-start(bf16[16,2,128,256]{3,2,1,0:T(8,128)(2,1)} %copy.52), calls=%async_computation | async-start | bytes 4194304 | tf_op jit(solution)/shard_map/all_to_all | solution.py:159
  20.5 145.6 %reduce-scatter.2.cloned.1.call-start = ((), (), s32[]{:S(2)}) async-start(), calls=%async_computation.6 | async-start | bytes 3244032 | tf_op jit(solution)/shard_map/reduce_scatter | solution.py:185
  99.6 1.0 copy-start.1
  102.2 18.8 %all-to-all-start.1 = ((f32[8,1,11008]{2,1,0:T(1,128)}), f32[8,1,11008]{2,1,0:T(1,128)S(1)}, u32[]{:S(2)}, u32[]{:S(2)}) async-start(f32[8,1,11008]{2,1,0:T(1,128)} %all_to_all.21), calls=%async_computation.2 | async-start | bytes 704512 | tf_op jit(solution)/shard_map/all_to_all | solution.py:189
  144.3 7.6 %copy-start.5 = (s32[1,16,2]{1,2,0:T(2,128)S(1)}, s32[1,16,2]{1,2,0:T(2,128)}, u32[]{:S(2)}) copy-start(s32[1,16,2]{1,2,0:T(2,128)} %param.13) | copy-start | bytes 388
  145.3 18.7 %all-to-all-start.3 = ((f32[128,1,688]{2,1,0:T(1,128)}), f32[128,1,688]{2,1,0:T(1,128)S(1)}, u32[]{:S(2)}, u32[]{:S(2)}) async-start(f32[128,1,688]{2,1,0:T(1,128)} %broadcast_in_dim.2), calls=%async_computation.4 | async-start | bytes 786432 | tf_op jit(solution)/shard_map/all_to_all | solution.py:200
  152.4 13.7 %copy-start = (f32[8,128,256]{2,1,0:T(8,128)S(1)}, f32[8,128,256]{2,1,0:T(8,128)}, u32[]{:S(2)}) copy-start(f32[8,128,256]{2,1,0:T(8,128)} %get-tuple-element.8) | copy-start | bytes 3145732
Sparse Core Ops, SparseCore 0:
  9.7 35.6 all-gather.1
  99.8 38.9 reduce-scatter.1

commit v7 on v6

--- a/solution.py
+++ b/solution.py
@@ -7,11 +7,16 @@
 from jax.experimental.pallas import tpu as pltpu
 from jax.sharding import PartitionSpec as P
 
+
 LANES = 128
 GROUP = 8
 
 
-def _fused_kernel(
+def _tile(w_ref, t, live):
+    return jnp.where(t < live, w_ref[0, t], jnp.zeros_like(w_ref[0, t]))
+
+
+def _forward_kernel(
     src_ref,
     live_ref,
     w_ref,
@@ -22,10 +27,9 @@
     nw_ref,
     sw_ref,
     swt_ref,
-    out_ref,
     grads_ref,
     selfterm_ref,
-    term_ref,
+    scaled_ref,
     *,
     classes,
 ):
@@ -36,18 +40,14 @@
 
     @pl.when(b == 0)
     def _():
-        term_ref[...] = jnp.zeros_like(term_ref)
         grads_ref[...] = jnp.zeros_like(grads_ref)
 
     live = live_ref[b]
     groups = (live + GROUP - 1) // GROUP
 
-    def tile(t):
-        return jnp.where(t < live, w_ref[0, t], jnp.zeros_like(w_ref[0, t]))
-
     def forward(g, acc):
         ts = [g * GROUP + k for k in range(GROUP)]
-        wcat = jnp.concatenate([tile(t) for t in ts], axis=1)
+        wcat = jnp.concatenate([_tile(w_ref, t, live) for t in ts], axis=1)
         scat = jnp.concatenate([sources_ref[src_ref[b, t]] for t in ts], axis=0)
         return acc + jnp.dot(wcat, scat, preferred_element_type=jnp.float32)
 
@@ -70,13 +70,25 @@
     grads_ref[0] += lax.dot_general(aggregate, delta, tn, preferred_element_type=jnp.float32)
     grads_ref[1] += lax.dot_general(own, delta, tn, preferred_element_type=jnp.float32)
     selfterm_ref[0] = jnp.dot(delta, swt_ref[...], preferred_element_type=jnp.float32)
-    scaled_t = (residual / deg).astype(jnp.bfloat16).T
+    scaled_ref[0] = (residual / deg).astype(jnp.bfloat16).T
+
+
+def _backward_kernel(src_ref, live_ref, w_ref, scaled_ref, out_ref, term_ref):
+    b = pl.program_id(0)
+
+    @pl.when(b == 0)
+    def _():
+        term_ref[...] = jnp.zeros_like(term_ref)
+
+    live = live_ref[b]
+    groups = (live + GROUP - 1) // GROUP
+    scaled_t = scaled_ref[0]
 
     def backward(g, carry):
         for k in range(GROUP):
             t = g * GROUP + k
             s = src_ref[b, t]
-            term_ref[s] += jnp.dot(scaled_t, tile(t), preferred_element_type=jnp.float32)
+            term_ref[s] += jnp.dot(scaled_t, _tile(w_ref, t, live), preferred_element_type=jnp.float32)
         return carry
 
     lax.fori_loop(0, groups, backward, 0)
@@ -91,11 +103,14 @@
     source_total, _, width = sources.shape
     padded = nw.shape[1]
     kept = -(-classes // 16) * 16
+    params = pltpu.CompilerParams(dimension_semantics=("arbitrary",), vmem_limit_bytes=60 * 1024 * 1024)
+    w_spec = pl.BlockSpec((1, tile_slots, rows, rows), lambda b, *_: (b, 0, 0, 0))
+    scaled_spec = pl.BlockSpec((1, padded, rows), lambda b, *_: (b, 0, 0))
     grid_spec = pltpu.PrefetchScalarGridSpec(
         num_scalar_prefetch=2,
         grid=(block_count,),
         in_specs=[
-            pl.BlockSpec((1, tile_slots, rows, rows), lambda b, *_: (b, 0, 0, 0)),
+            w_spec,
             pl.BlockSpec((source_total, rows, width), lambda b, *_: (0, 0, 0)),
             pl.BlockSpec((1, rows, width), lambda b, *_: (b, 0, 0)),
             pl.BlockSpec((1, rows, 1), lambda b, *_: (b, 0, 0)),
@@ -105,27 +120,38 @@
             pl.BlockSpec((padded, width), lambda b, *_: (0, 0)),
         ],
         out_specs=[
-            pl.BlockSpec((source_total, kept, rows), lambda b, *_: (0, 0, 0)),
             pl.BlockSpec((2, width, padded), lambda b, *_: (0, 0, 0)),
             pl.BlockSpec((1, rows, width), lambda b, *_: (b, 0, 0)),
+            scaled_spec,
         ],
-        scratch_shapes=[pltpu.VMEM((source_total, padded, rows), jnp.float32)],
-    )
-    return pl.pallas_call(
-        functools.partial(_fused_kernel, classes=classes),
+    )
+    grads, selfterm, scaled = pl.pallas_call(
+        functools.partial(_forward_kernel, classes=classes),
         grid_spec=grid_spec,
         out_shape=[
-            jax.ShapeDtypeStruct((source_total, kept, rows), jnp.bfloat16),
             jax.ShapeDtypeStruct((2, width, padded), jnp.float32),
             jax.ShapeDtypeStruct((block_count, rows, width), jnp.float32),
+            jax.ShapeDtypeStruct((block_count, padded, rows), jnp.bfloat16),
         ],
-        compiler_params=pltpu.CompilerParams(
-            dimension_semantics=("arbitrary",), vmem_limit_bytes=60 * 1024 * 1024
-        ),
+        compiler_params=params,
     )(tile_source, tile_live, tile_weight, sources, own_blocks, deg, lab, nw, sw, swt)
-
-
-def per_device(
+    grid_spec = pltpu.PrefetchScalarGridSpec(
+        num_scalar_prefetch=2,
+        grid=(block_count,),
+        in_specs=[w_spec, scaled_spec],
+        out_specs=[pl.BlockSpec((source_total, kept, rows), lambda b, *_: (0, 0, 0))],
+        scratch_shapes=[pltpu.VMEM((source_total, padded, rows), jnp.float32)],
+    )
+    (term,) = pl.pallas_call(
+        _backward_kernel,
+        grid_spec=grid_spec,
+        out_shape=[jax.ShapeDtypeStruct((source_total, kept, rows), jnp.bfloat16)],
+        compiler_params=params,
+    )(tile_source, tile_live, tile_weight, scaled)
+    return term, grads, selfterm
+
+
+def _per_device(
     history,
     tile_weight,
     tile_source,
@@ -186,7 +212,8 @@
         term[:part_blocks], "sub", scatter_dimension=0, tiled=True
     ).astype(jnp.float32)
     flat = grads[:, :, :classes].reshape(sub_count, -1)
-    part_sum = lax.all_to_all(flat, "sub", 0, 0, tiled=True).sum(axis=0)
+    part_sum = lax.all_to_all(flat, "sub", 0, 0, tiled=True)
+    part_sum = part_sum.sum(axis=0)
     part_sum = part_sum.reshape(dom_count, -1)
     piece = part_sum.shape[1]
     extra_rows = -(-2 * piece // (16 * block_rows)) * 16
@@ -223,7 +250,7 @@
         P(),
     )
     return jax.shard_map(
-        per_device,
+        _per_device,
         mesh=mesh,
         in_specs=placed,
         out_specs=(P(("dom", "sub"), None), P(), P()),

time: 176 us -> 181 us (1.028)
  blocking collectives: 22.7 us -> 28 us
    all_to_all x1, blocking collectives: 22.7 us -> 28 us  [_per_device(): lax.all_to_all(jnp.concatenate([halo, extra], axis=1), 'dom', 0, 0, tiled...]
    slice x5 -> x6, local copies, waits for them, and re-layouts: 5.24 us -> 3.74 us  [the longest x1 3.59 us: _per_device(): term[:part_blocks]]
    pallas_call x1 -> x2, Pallas kernels: 42 us -> 43.1 us  [the longest x1 22.2 us: _fused(): pl.pallas_call(functools.partial(_forward_kernel, classes=classes), grid_...]
  transfers between devices with their start and end apart: 5 -> 5, of which waited for: 3 -> 3; matrix products, arithmetic and copies ran while one was open for 8% -> 7% of each run, Pallas kernels for 0% -> 0%
where the time goes in v7:
time: 181 us; the launch traced here: 180 us
  waiting for transfers between devices  44.1 us (24%)
  Pallas kernels  43.1 us (24%)
  blocking collectives  28 us (15%)
  starting transfers between devices  23.4 us (13%)
  local copies, waits for them, and re-layouts  15.7 us (9%)
  between operations  14.2 us (8%)
  other arithmetic  5.96 us (3%)
  matrix products  5.34 us (3%)
    all_to_all x1, blocking collectives, _per_device(): lax.all_to_all(jnp.concatenate([halo, extra], axis=1), 'dom', 0, 0, tiled...  28 us
    all_to_all x1, waiting for transfers between devices, _per_device(): lax.all_to_all(outgoing, 'dom', split_axis=0, concat_axis=0, tiled=True)  23.8 us
    pallas_call x1, Pallas kernels, _fused(): pl.pallas_call(functools.partial(_forward_kernel, classes=classes), grid_...  22.2 us
    pallas_call x1, Pallas kernels, _fused(): pl.pallas_call(_backward_kernel, grid_spec=grid_spec, out_shape=[jax.Shap...  20.9 us
    all_to_all x1, waiting for transfers between devices, _per_device(): totals = lax.all_to_all(spread, ('dom', 'sub'), 0, 0, tiled=True)  11.5 us
    all_to_all x1, starting transfers between devices, _per_device(): lax.all_to_all(outgoing, 'dom', split_axis=0, concat_axis=0, tiled=True)  8.74 us
    all_to_all x1, waiting for transfers between devices, _per_device(): part_sum = lax.all_to_all(flat, 'sub', 0, 0, tiled=True)  8.1 us
    all_to_all x1, starting transfers between devices, _per_device(): part_sum = lax.all_to_all(flat, 'sub', 0, 0, tiled=True)  8.01 us
  transfers between devices with their start and end apart: 5, of which 3 were waited for; matrix products, arithmetic and copies ran while one was open for 7% of the time, Pallas kernels for 0%

profile of v7, /device:TPU:1, one launch (start us, length us, event | category | flops | bytes accessed | tf_op | source)
XLA Modules:
  0.0 179.8 jit_solution(16938127838658193443)
XLA Ops:
  7.2 0.0 all-gather.2.cloned.1.call-start
  7.2 0.7 all-gather.2.cloned.1.call-update
  7.9 1.8 %convolution_convert_fusion = bf16[16,2,128,256]{3,0,2,1:T(8,128)(2,1)S(1)} fusion(bf16[8,128,256]{2,1,0:T(8,128)(2,1)} %bitcast.44, s32[16,2]{0,1:T(2,128)} %bitcast.55), kind=kOutput, calls=%fused_computation.1 | convolution fusion | flops 17826048 | bytes 2621568 | tf_op jit(solution)/shard_map/pks,sif->pkif/dot_general | solution.py:179
  9.7 2.0 %copy.52 = bf16[16,2,128,256]{3,2,1,0:T(8,128)(2,1)} copy(bf16[16,2,128,256]{3,0,2,1:T(8,128)(2,1)S(1)} %convolution_convert_fusion) | data formatting | bytes 4194304 | tf_op jit(solution)/shard_map/convert_element_type | solution.py:184
  11.8 0.0 copy-start.6
  11.8 0.0 copy-start.4
  11.8 0.0 copy-start.2
  11.8 0.0 copy-start.3
  11.8 8.7 %all-to-all-start = ((bf16[16,2,128,256]{3,2,1,0:T(8,128)(2,1)}), bf16[16,2,128,256]{3,2,1,0:T(8,128)(2,1)S(1)}, u32[]{:S(2)}, u32[]{:S(2)}) async-start(bf16[16,2,128,256]{3,2,1,0:T(8,128)(2,1)} %copy.52), calls=%async_computation | async-start | bytes 4194304 | tf_op jit(solution)/shard_map/all_to_all | solution.py:185
  20.5 0.0 reduce-scatter.2.cloned.1.call-start
  20.6 0.0 copy-done.6
  20.6 1.0 copy.55.deg_ref
  21.6 0.0 copy-done.4
  21.6 1.0 copy.56.lab_ref
  22.6 0.0 copy-done.2
  22.6 0.1 copy.53
  22.8 0.0 copy-done.3
  22.8 0.1 copy.54
  22.9 0.7 pad.15.nw_ref
  23.5 0.7 pad.16.sw_ref
  24.2 0.7 pad.17.swt_ref
  24.9 23.8 %all-to-all-done = bf16[16,2,128,256]{3,2,1,0:T(8,128)(2,1)S(1)} async-done(((bf16[16,2,128,256]{3,2,1,0:T(8,128)(2,1)}), bf16[16,2,128,256]{3,2,1,0:T(8,128)(2,1)S(1)}, u32[]{:S(2)}, u32[]{:S(2)}) %all-to-all-start) | async-done | bytes 2097184 | tf_op jit(solution)/shard_map/all_to_all | solution.py:185
  48.7 0.0 all-gather.2.cloned.1.call-done
  48.7 5.4 %pad_maximum_fusion.sources_ref = bf16[96,128,256]{2,1,0:T(8,128)(2,1)} fusion(bf16[32,128,256]{2,1,0:T(8,128)(2,1)S(1)} %bitcast.41, bf16[64,128,256]{2,1,0:T(8,128)(2,1)} %all-gather.2.cloned.1.call-done), kind=kLoop, calls=%fused_computation | loop fusion | flops 3145728 | bytes 12582912 | tf_op jit(solution)/shard_map/concatenate | solution.py:187
  54.1 22.2 %shard_map.112 = (f32[2,256,256]{2,1,0:T(8,128)}, f32[8,128,256]{2,1,0:T(8,128)}, bf16[8,256,128]{2,1,0:T(8,128)(2,1)}) custom-call(s32[8,64]{1,0:T(8,128)} %src_ref.3, s32[8]{0:T(128)} %live_ref.3, bf16[8,64,128,128]{3,2,1,0:T(8,128)(2,1)} %w_ref.3, bf16[96,128,256]{2,1,0:T(8,128)(2,1)} %pad_maximum_fusion.sources_ref, bf16[8,128,256]{2,1,0:T(8,128)(2,1)} %bitcast.45, ...), custom_call_target="tpu_custom_call" | custom-call | tf_op jit(solution)/shard_map/pallas_call | solution.py:128
  76.3 20.9 %shard_map.113 = bf16[96,176,128]{2,1,0:T(8,128)(2,1)} custom-call(s32[8,64]{1,0:T(8,128)} %src_ref.3, s32[8]{0:T(128)} %live_ref.3, bf16[8,64,128,128]{3,2,1,0:T(8,128)(2,1)} %w_ref.3, bf16[8,256,128]{2,1,0:T(8,128)(2,1)} %get-tuple-element.6.scaled_ref), custom_call_target="tpu_custom_call" | custom-call | tf_op jit(solution)/shard_map/pallas_call | solution.py:145
  97.2 3.6 %slice.42 = bf16[64,176,128]{2,1,0:T(8,128)(2,1)} slice(bf16[96,176,128]{2,1,0:T(8,128)(2,1)} %shard_map.113), slice={[0:64], [0:176], [0:128]} | slice | bytes 5767168 | tf_op jit(solution)/shard_map/slice | solution.py:212
  100.7 0.0 copy-start.1
  100.7 0.0 reduce-scatter.2.cloned.1.call-update
  100.8 1.0 copy-done.1
  101.8 1.5 all_to_all.21
  103.3 0.0 slice-start
  103.3 8.0 %all-to-all-start.1 = ((f32[8,1,11008]{2,1,0:T(1,128)}), f32[8,1,11008]{2,1,0:T(1,128)S(1)}, u32[]{:S(2)}, u32[]{:S(2)}) async-start(f32[8,1,11008]{2,1,0:T(1,128)} %all_to_all.21), calls=%async_computation.2 | async-start | bytes 704512 | tf_op jit(solution)/shard_map/all_to_all | solution.py:215
  111.3 8.1 %all-to-all-done.1 = f32[8,1,11008]{2,1,0:T(1,128)S(1)} async-done(((f32[8,1,11008]{2,1,0:T(1,128)}), f32[8,1,11008]{2,1,0:T(1,128)S(1)}, u32[]{:S(2)}, u32[]{:S(2)}) %all-to-all-start.1) | async-done | bytes 352288 | tf_op jit(solution)/shard_map/all_to_all | solution.py:215
  119.4 0.3 reduce_sum.18
  119.7 0.1 reshape.65
  119.8 0.1 fusion.13
  119.9 0.0 slice-done
  119.9 0.1 pad_maximum_fusion.1
  120.0 28.0 %all_to_all.26 = bf16[16,368,128]{2,1,0:T(8,128)(2,1)S(1)} all-to-all(bf16[16,368,128]{2,1,0:T(8,128)(2,1)S(1)} %pad_maximum_fusion.1), channel_id=1, replica_groups=mesh['dom'=16,'sub'=8] {'dom'}, dimensions={0} | all-to-all | bytes 3014656 | tf_op jit(solution)/shard_map/all_to_all | solution.py:222
  148.0 0.0 copy-start.5
  148.1 0.1 add_reduce_fusion
  148.2 0.9 broadcast_in_dim.2
  149.1 6.6 %all-to-all-start.3 = ((f32[128,1,688]{2,1,0:T(1,128)}), f32[128,1,688]{2,1,0:T(1,128)S(1)}, u32[]{:S(2)}, u32[]{:S(2)}) async-start(f32[128,1,688]{2,1,0:T(1,128)} %broadcast_in_dim.2), calls=%async_computation.4 | async-start | bytes 786432 | tf_op jit(solution)/shard_map/all_to_all | solution.py:227
  155.7 0.1 slice.44
  155.8 0.0 copy-done.5
  155.8 0.5 fusion.2
  156.4 0.0 copy-start
  156.4 11.5 %all-to-all-done.3 = f32[128,1,688]{2,1,0:T(1,128)S(1)} async-done(((f32[128,1,688]{2,1,0:T(1,128)}), f32[128,1,688]{2,1,0:T(1,128)S(1)}, u32[]{:S(2)}, u32[]{:S(2)}) %all-to-all-start.3) | async-done | bytes 352288 | tf_op jit(solution)/shard_map/all_to_all | solution.py:227
  167.9 0.1 copy.83
  168.1 0.1 mul.13
  168.3 0.8 copy.61
  169.1 0.1 mul.15
  169.2 0.8 copy.62
  170.0 0.0 reduce-scatter.2.cloned.1.call-done
  170.0 0.0 copy-done
  170.0 3.0 %convolution_add_fusion = f32[8,128,256]{2,1,0:T(8,128)} fusion(f32[8,128,256]{2,1,0:T(8,128)S(1)} %copy-done, f32[8,172,128]{2,0,1:T(8,128)S(1)} %slice.46, bf16[8,176,128]{2,1,0:T(8,128)(2,1)} %reduce-scatter.2.cloned.1.call-done, bf16[256,172]{0,1:T(8,128)(2,1)S(1)} %copy-done.2), kind=kOutput, calls=%fused_computation.5 | convolution fusion | flops 541679616 | bytes 3250176 | tf_op jit(solution)/shard_map/sci,fc->sif/dot_general | solution.py:234
  (8 shorter events, 0.2 us)
Async XLA Ops:
  7.2 41.5 %all-gather.2.cloned.1.call-start = ((), (), s32[]{:S(2)}) async-start(), calls=%async_computation.5 | async-start | bytes 4718592 | tf_op jit(solution)/shard_map/all_gather | solution.py:175
  11.8 8.8 %copy-start.6 = (s32[1024]{0:T(1024)S(1)}, s32[1024]{0:T(1024)}, u32[]{:S(2)}) copy-start(s32[1024]{0:T(1024)} %param.14) | copy-start | bytes 12292
  11.8 9.9 %copy-start.4 = (s32[1024]{0:T(1024)S(1)}, s32[1024]{0:T(1024)}, u32[]{:S(2)}) copy-start(s32[1024]{0:T(1024)} %param.15) | copy-start | bytes 12292
  11.8 10.9 %copy-start.2 = (bf16[256,172]{0,1:T(8,128)(2,1)S(1)}, bf16[256,172]{0,1:T(8,128)(2,1)}, u32[]{:S(2)}) copy-start(bf16[256,172]{0,1:T(8,128)(2,1)} %param.16) | copy-start | bytes 264196
  11.8 11.0 %copy-start.3 = (bf16[256,172]{0,1:T(8,128)(2,1)S(1)}, bf16[256,172]{0,1:T(8,128)(2,1)}, u32[]{:S(2)}) copy-start(bf16[256,172]{0,1:T(8,128)(2,1)} %param.17) | copy-start | bytes 264196
  11.8 36.9 %all-to-all-start = ((bf16[16,2,128,256]{3,2,1,0:T(8,128)(2,1)}), bf16[16,2,128,256]{3,2,1,0:T(8,128)(2,1)S(1)}, u32[]{:S(2)}, u32[]{:S(2)}) async-start(bf16[16,2,128,256]{3,2,1,0:T(8,128)(2,1)} %copy.52), calls=%async_computation | async-start | bytes 4194304 | tf_op jit(solution)/shard_map/all_to_all | solution.py:185
  20.5 149.5 %reduce-scatter.2.cloned.1.call-start = ((), (), s32[]{:S(2)}) async-start(), calls=%async_computation.6 | async-start | bytes 3244032 | tf_op jit(solution)/shard_map/reduce_scatter | solution.py:211
  100.7 1.0 copy-start.1
  103.3 16.6 %slice-start = ((bf16[96,176,128]{2,1,0:T(8,128)(2,1)}), bf16[32,176,128]{2,1,0:T(8,128)(2,1)S(1)}, s32[]{:S(2)}) async-start(bf16[96,176,128]{2,1,0:T(8,128)(2,1)} %shard_map.113), calls=%async_computation.7 | async-start | bytes 2883584 | tf_op jit(solution)/shard_map/slice | solution.py:221
  103.3 16.1 %all-to-all-start.1 = ((f32[8,1,11008]{2,1,0:T(1,128)}), f32[8,1,11008]{2,1,0:T(1,128)S(1)}, u32[]{:S(2)}, u32[]{:S(2)}) async-start(f32[8,1,11008]{2,1,0:T(1,128)} %all_to_all.21), calls=%async_computation.2 | async-start | bytes 704512 | tf_op jit(solution)/shard_map/all_to_all | solution.py:215
  148.0 7.8 %copy-start.5 = (s32[1,16,2]{1,2,0:T(2,128)S(1)}, s32[1,16,2]{1,2,0:T(2,128)}, u32[]{:S(2)}) copy-start(s32[1,16,2]{1,2,0:T(2,128)} %param.13) | copy-start | bytes 388
  149.1 18.8 %all-to-all-start.3 = ((f32[128,1,688]{2,1,0:T(1,128)}), f32[128,1,688]{2,1,0:T(1,128)S(1)}, u32[]{:S(2)}, u32[]{:S(2)}) async-start(f32[128,1,688]{2,1,0:T(1,128)} %broadcast_in_dim.2), calls=%async_computation.4 | async-start | bytes 786432 | tf_op jit(solution)/shard_map/all_to_all | solution.py:227
  156.4 13.6 %copy-start = (f32[8,128,256]{2,1,0:T(8,128)S(1)}, f32[8,128,256]{2,1,0:T(8,128)}, u32[]{:S(2)}) copy-start(f32[8,128,256]{2,1,0:T(8,128)} %get-tuple-element.8) | copy-start | bytes 3145732
Sparse Core Ops, SparseCore 0:
  9.7 35.6 all-gather.1
  100.9 38.4 reduce-scatter.1

commit v8 on v7

--- a/solution.py
+++ b/solution.py
@@ -20,7 +20,8 @@
     src_ref,
     live_ref,
     w_ref,
-    sources_ref,
+    part_ref,
+    bnd_ref,
     hist_ref,
     deg_ref,
     lab_ref,
@@ -35,20 +36,26 @@
 ):
     b = pl.program_id(0)
     rows = w_ref.shape[2]
-    width = sources_ref.shape[2]
+    width = part_ref.shape[2]
     padded = nw_ref.shape[1]
+    part_total = part_ref.shape[0]
 
     @pl.when(b == 0)
     def _():
         grads_ref[...] = jnp.zeros_like(grads_ref)
 
+    def source(s):
+        inside = part_ref[jnp.minimum(s, part_total - 1)]
+        outside = bnd_ref[jnp.maximum(s - part_total, 0)]
+        return jnp.where(s < part_total, inside, outside)
+
     live = live_ref[b]
     groups = (live + GROUP - 1) // GROUP
 
     def forward(g, acc):
         ts = [g * GROUP + k for k in range(GROUP)]
         wcat = jnp.concatenate([_tile(w_ref, t, live) for t in ts], axis=1)
-        scat = jnp.concatenate([sources_ref[src_ref[b, t]] for t in ts], axis=0)
+        scat = jnp.concatenate([source(src_ref[b, t]) for t in ts], axis=0)
         return acc + jnp.dot(wcat, scat, preferred_element_type=jnp.float32)
 
     acc = lax.fori_loop(0, groups, forward, jnp.zeros((rows, width), jnp.float32))
@@ -98,9 +105,10 @@
         out_ref[...] = term_ref[:, : out_ref.shape[1], :].astype(out_ref.dtype)
 
 
-def _fused(tile_source, tile_live, tile_weight, sources, own_blocks, deg, lab, nw, sw, swt, classes):
+def _fused(tile_source, tile_live, tile_weight, partition, boundary, own_blocks, deg, lab, nw, sw, swt, classes):
     block_count, tile_slots, rows, _ = tile_weight.shape
-    source_total, _, width = sources.shape
+    part_total, _, width = partition.shape
+    source_total = part_total + boundary.shape[0]
     padded = nw.shape[1]
     kept = -(-classes // 16) * 16
     params = pltpu.CompilerParams(dimension_semantics=("arbitrary",), vmem_limit_bytes=60 * 1024 * 1024)
@@ -111,7 +119,8 @@
         grid=(block_count,),
         in_specs=[
             w_spec,
-            pl.BlockSpec((source_total, rows, width), lambda b, *_: (0, 0, 0)),
+            pl.BlockSpec(partition.shape, lambda b, *_: (0, 0, 0)),
+            pl.BlockSpec(boundary.shape, lambda b, *_: (0, 0, 0)),
             pl.BlockSpec((1, rows, width), lambda b, *_: (b, 0, 0)),
             pl.BlockSpec((1, rows, 1), lambda b, *_: (b, 0, 0)),
             pl.BlockSpec((1, rows, 1), lambda b, *_: (b, 0, 0)),
@@ -134,7 +143,7 @@
             jax.ShapeDtypeStruct((block_count, padded, rows), jnp.bfloat16),
         ],
         compiler_params=params,
-    )(tile_source, tile_live, tile_weight, sources, own_blocks, deg, lab, nw, sw, swt)
+    )(tile_source, tile_live, tile_weight, partition, boundary, own_blocks, deg, lab, nw, sw, swt)
     grid_spec = pltpu.PrefetchScalarGridSpec(
         num_scalar_prefetch=2,
         grid=(block_count,),
@@ -176,17 +185,11 @@
     part_blocks = partition.shape[0]
     own_ids = jnp.arange(block_count, dtype=jnp.int32)
     send_table = send_list[0][:, :, None] == own_ids[None, None, :]
-    outgoing = jnp.einsum(
-        "pks,sif->pkif",
-        send_table.astype(jnp.bfloat16),
-        own_blocks,
-        preferred_element_type=jnp.float32,
-    ).astype(jnp.bfloat16)
+    outgoing = jnp.take(own_blocks, send_list[0].reshape(-1), axis=0, mode="clip")
+    outgoing = outgoing.reshape(send_list.shape[1:] + own_blocks.shape[1:])
     boundary = lax.all_to_all(outgoing, "dom", split_axis=0, concat_axis=0, tiled=True)
     slot_count = boundary.shape[1]
-    sources = jnp.concatenate(
-        [partition, boundary.reshape(dom_count * slot_count, block_rows, width)], axis=0
-    )
+    boundary = boundary.reshape(dom_count * slot_count, block_rows, width)
     degrees = degree.astype(jnp.float32).reshape(block_count, block_rows, 1)
     lab = labels.reshape(block_count, block_rows, 1)
     pad_cols = ((0, 0), (0, padded - classes))
@@ -194,7 +197,7 @@
     sw = jnp.pad(self_weight, pad_cols)
     swt = jnp.pad(self_weight.T, ((0, padded - classes), (0, 0)))
     term, grads, selfterm = _fused(
-        tile_source, tile_live, tile_weight, sources, own_blocks, degrees, lab, nw, sw, swt, classes
+        tile_source, tile_live, tile_weight, partition, boundary, own_blocks, degrees, lab, nw, sw, swt, classes
     )
 
     norm_factor = float(nodes_all) ** (-0.5)

time: 181 us -> 178 us (0.983)
  other arithmetic: 5.96 us -> 0.58 us
  local copies, waits for them, and re-layouts: 15.7 us -> 19 us
  matrix products: 5.34 us -> 3.53 us
    concatenate x1 -> x0, other arithmetic: 5.38 us -> none  [_per_device(): jnp.concatenate([partition, boundary.reshape(dom_count * slot_count, bloc...]
    gather x0 -> x1, local copies, waits for them, and re-layouts: none -> 3.08 us  [_per_device(): jnp.take(own_blocks, send_list[0].reshape(-1), axis=0, mode='clip')]
    unnamed x21 -> x24, local copies, waits for them, and re-layouts: 2.87 us -> 4.98 us
    convert_element_type x1 -> x0, local copies, waits for them, and re-layouts: 2.04 us -> none  [_per_device(): outgoing = jnp.einsum('pks,sif->pkif', send_table.astype(jnp.bfloat16), o...]
    dot_general x1 -> x0, matrix products: 1.81 us -> none  [_per_device(): jnp.einsum('pks,sif->pkif', send_table.astype(jnp.bfloat16), own_blocks,...]
where the time goes in v8:
time: 178 us; the launch traced here: 177 us
  waiting for transfers between devices  44 us (25%)
  Pallas kernels  43.8 us (25%)
  blocking collectives  28.2 us (16%)
  starting transfers between devices  23.5 us (13%)
  local copies, waits for them, and re-layouts  19 us (11%)
  between operations  14.2 us (8%)
  matrix products  3.53 us (2%)
    all_to_all x1, blocking collectives, _per_device(): lax.all_to_all(jnp.concatenate([halo, extra], axis=1), 'dom', 0, 0, tiled...  28.2 us
    all_to_all x1, waiting for transfers between devices, _per_device(): lax.all_to_all(outgoing, 'dom', split_axis=0, concat_axis=0, tiled=True)  23.7 us
    pallas_call x1, Pallas kernels, _fused(): pl.pallas_call(functools.partial(_forward_kernel, classes=classes), grid_...  22.9 us
    pallas_call x1, Pallas kernels, _fused(): pl.pallas_call(_backward_kernel, grid_spec=grid_spec, out_shape=[jax.Shap...  20.9 us
    all_to_all x1, waiting for transfers between devices, _per_device(): totals = lax.all_to_all(spread, ('dom', 'sub'), 0, 0, tiled=True)  11.5 us
    all_to_all x1, starting transfers between devices, _per_device(): lax.all_to_all(outgoing, 'dom', split_axis=0, concat_axis=0, tiled=True)  8.73 us
    all_to_all x1, starting transfers between devices, _per_device(): part_sum = lax.all_to_all(flat, 'sub', 0, 0, tiled=True)  8.07 us
    all_to_all x1, waiting for transfers between devices, _per_device(): part_sum = lax.all_to_all(flat, 'sub', 0, 0, tiled=True)  8.04 us
  transfers between devices with their start and end apart: 5, of which 3 were waited for; matrix products, arithmetic and copies ran while one was open for 7% of the time, Pallas kernels for 0%

profile of v8, /device:TPU:1, one launch (start us, length us, event | category | flops | bytes accessed | tf_op | source)
XLA Modules:
  0.0 176.8 jit_solution(4288622577507176368)
XLA Ops:
  7.2 0.0 all-gather.2.cloned.1.call-start
  7.2 0.7 all-gather.2.cloned.1.call-update
  7.9 0.8 copy.49
  8.7 0.1 reshape.77
  8.8 3.1 %gather_fusion = bf16[32,128,256]{2,1,0:T(8,128)(2,1)} fusion(bf16[8,128,256]{2,1,0:T(8,128)(2,1)} %bitcast.35, s32[1024]{0:T(1024)S(1)} %pad_clamp_fusion), kind=kCustom, calls=%fused_computation | custom fusion | bytes 4194432 | tf_op jit(solution)/shard_map/jit(_take)/gather | solution.py:188
  11.8 0.0 copy-start.3
  11.8 0.0 copy-start.4
  11.8 0.0 copy-start.7
  11.8 0.0 copy-start.5
  11.8 8.7 %all-to-all-start = ((bf16[16,2,128,256]{3,2,1,0:T(8,128)(2,1)}), bf16[16,2,128,256]{3,2,1,0:T(8,128)(2,1)S(1)}, u32[]{:S(2)}, u32[]{:S(2)}) async-start(bf16[16,2,128,256]{3,2,1,0:T(8,128)(2,1)} %bitcast.39), calls=%async_computation | async-start | bytes 4194304 | tf_op jit(solution)/shard_map/all_to_all | solution.py:190
  20.6 0.0 reduce-scatter.2.cloned.1.call-start
  20.6 0.0 copy-done.3
  20.6 0.1 copy.50
  20.8 0.0 copy-done.4
  20.8 0.1 copy.51
  20.9 0.7 pad.17.swt_ref
  21.5 0.7 pad.15.nw_ref
  22.2 0.7 pad.16.sw_ref
  22.9 0.0 copy-done.7
  22.9 1.0 copy.52.deg_ref
  23.9 0.0 copy-done.5
  23.9 1.1 copy.53.lab_ref
  25.0 23.7 %all-to-all-done = bf16[16,2,128,256]{3,2,1,0:T(8,128)(2,1)S(1)} async-done(((bf16[16,2,128,256]{3,2,1,0:T(8,128)(2,1)}), bf16[16,2,128,256]{3,2,1,0:T(8,128)(2,1)S(1)}, u32[]{:S(2)}, u32[]{:S(2)}) %all-to-all-start) | async-done | bytes 2097184 | tf_op jit(solution)/shard_map/all_to_all | solution.py:190
  48.8 0.0 copy-start
  48.8 0.0 all-gather.2.cloned.1.call-done.part_ref
  48.8 1.4 copy-done
  50.1 22.9 %shard_map.112 = (f32[2,256,256]{2,1,0:T(8,128)}, f32[8,128,256]{2,1,0:T(8,128)}, bf16[8,256,128]{2,1,0:T(8,128)(2,1)}) custom-call(s32[8,64]{1,0:T(8,128)} %src_ref.3, s32[8]{0:T(128)} %live_ref.3, bf16[8,64,128,128]{3,2,1,0:T(8,128)(2,1)} %w_ref.3, bf16[64,128,256]{2,1,0:T(8,128)(2,1)} %all-gather.2.cloned.1.call-done.part_ref, ...), custom_call_target="tpu_custom_call" | custom-call | tf_op jit(solution)/shard_map/pallas_call | solution.py:137
  73.0 20.9 %shard_map.113 = bf16[96,176,128]{2,1,0:T(8,128)(2,1)} custom-call(s32[8,64]{1,0:T(8,128)} %src_ref.3, s32[8]{0:T(128)} %live_ref.3, bf16[8,64,128,128]{3,2,1,0:T(8,128)(2,1)} %w_ref.3, bf16[8,256,128]{2,1,0:T(8,128)(2,1)} %get-tuple-element.6.scaled_ref), custom_call_target="tpu_custom_call" | custom-call | tf_op jit(solution)/shard_map/pallas_call | solution.py:154
  93.9 3.6 %slice.44 = bf16[64,176,128]{2,1,0:T(8,128)(2,1)} slice(bf16[96,176,128]{2,1,0:T(8,128)(2,1)} %shard_map.113), slice={[0:64], [0:176], [0:128]} | slice | bytes 5767168 | tf_op jit(solution)/shard_map/slice | solution.py:215
  97.5 0.0 copy-start.2
  97.5 0.0 reduce-scatter.2.cloned.1.call-update
  97.5 1.0 copy-done.2
  98.5 1.5 all_to_all.21
  100.0 0.0 slice-start
  100.0 8.1 %all-to-all-start.1 = ((f32[8,1,11008]{2,1,0:T(1,128)}), f32[8,1,11008]{2,1,0:T(1,128)S(1)}, u32[]{:S(2)}, u32[]{:S(2)}) async-start(f32[8,1,11008]{2,1,0:T(1,128)} %all_to_all.21), calls=%async_computation.2 | async-start | bytes 704512 | tf_op jit(solution)/shard_map/all_to_all | solution.py:218
  108.1 8.0 %all-to-all-done.1 = f32[8,1,11008]{2,1,0:T(1,128)S(1)} async-done(((f32[8,1,11008]{2,1,0:T(1,128)}), f32[8,1,11008]{2,1,0:T(1,128)S(1)}, u32[]{:S(2)}, u32[]{:S(2)}) %all-to-all-start.1) | async-done | bytes 352288 | tf_op jit(solution)/shard_map/all_to_all | solution.py:218
  116.1 0.3 reduce_sum.18
  116.4 0.1 reshape.70
  116.5 0.1 fusion.11
  116.6 0.0 slice-done
  116.6 0.1 pad_maximum_fusion
  116.7 28.2 %all_to_all.26 = bf16[16,368,128]{2,1,0:T(8,128)(2,1)S(1)} all-to-all(bf16[16,368,128]{2,1,0:T(8,128)(2,1)S(1)} %pad_maximum_fusion), channel_id=1, replica_groups=mesh['dom'=16,'sub'=8] {'dom'}, dimensions={0} | all-to-all | bytes 3014656 | tf_op jit(solution)/shard_map/all_to_all | solution.py:225
  144.9 0.0 copy-start.6
  145.0 0.1 add_reduce_fusion
  145.1 1.0 broadcast_in_dim.12
  146.0 6.6 %all-to-all-start.3 = ((f32[128,1,688]{2,1,0:T(1,128)}), f32[128,1,688]{2,1,0:T(1,128)S(1)}, u32[]{:S(2)}, u32[]{:S(2)}) async-start(f32[128,1,688]{2,1,0:T(1,128)} %broadcast_in_dim.12), calls=%async_computation.4 | async-start | bytes 786432 | tf_op jit(solution)/shard_map/all_to_all | solution.py:230
  152.6 0.1 slice.46
  152.7 0.0 copy-done.6
  152.7 0.5 fusion.2
  153.3 0.0 copy-start.1
  153.3 11.5 %all-to-all-done.3 = f32[128,1,688]{2,1,0:T(1,128)S(1)} async-done(((f32[128,1,688]{2,1,0:T(1,128)}), f32[128,1,688]{2,1,0:T(1,128)S(1)}, u32[]{:S(2)}, u32[]{:S(2)}) %all-to-all-start.3) | async-done | bytes 352288 | tf_op jit(solution)/shard_map/all_to_all | solution.py:230
  164.8 0.1 copy.75
  165.0 0.1 mul.15
  165.2 0.8 copy.59
  166.0 0.1 mul.13
  166.1 0.8 copy.58
  166.9 0.0 reduce-scatter.2.cloned.1.call-done
  166.9 0.0 copy-done.1
  166.9 3.0 %convolution_add_fusion = f32[8,128,256]{2,1,0:T(8,128)} fusion(f32[8,128,256]{2,1,0:T(8,128)S(1)} %copy-done.1, f32[8,172,128]{2,0,1:T(8,128)S(1)} %slice.48, bf16[8,176,128]{2,1,0:T(8,128)(2,1)} %reduce-scatter.2.cloned.1.call-done, bf16[256,172]{0,1:T(8,128)(2,1)S(1)} %copy-done.3), kind=kOutput, calls=%fused_computation.4 | convolution fusion | flops 541679616 | bytes 3250176 | tf_op jit(solution)/shard_map/sci,fc->sif/dot_general | solution.py:237
  (9 shorter events, 0.2 us)
Async XLA Ops:
  7.2 41.6 %all-gather.2.cloned.1.call-start = ((), (), s32[]{:S(2)}) async-start(), calls=%async_computation.5 | async-start | bytes 4718592 | tf_op jit(solution)/shard_map/all_gather | solution.py:184
  11.8 8.8 %copy-start.3 = (bf16[256,172]{0,1:T(8,128)(2,1)S(1)}, bf16[256,172]{0,1:T(8,128)(2,1)}, u32[]{:S(2)}) copy-start(bf16[256,172]{0,1:T(8,128)(2,1)} %param.16) | copy-start | bytes 264196
  11.8 8.9 %copy-start.4 = (bf16[256,172]{0,1:T(8,128)(2,1)S(1)}, bf16[256,172]{0,1:T(8,128)(2,1)}, u32[]{:S(2)}) copy-start(bf16[256,172]{0,1:T(8,128)(2,1)} %param.17) | copy-start | bytes 264196
  11.8 11.1 %copy-start.7 = (s32[1024]{0:T(1024)S(1)}, s32[1024]{0:T(1024)}, u32[]{:S(2)}) copy-start(s32[1024]{0:T(1024)} %param.14) | copy-start | bytes 12292
  11.8 12.1 %copy-start.5 = (s32[1024]{0:T(1024)S(1)}, s32[1024]{0:T(1024)}, u32[]{:S(2)}) copy-start(s32[1024]{0:T(1024)} %param.15) | copy-start | bytes 12292
  11.8 36.9 %all-to-all-start = ((bf16[16,2,128,256]{3,2,1,0:T(8,128)(2,1)}), bf16[16,2,128,256]{3,2,1,0:T(8,128)(2,1)S(1)}, u32[]{:S(2)}, u32[]{:S(2)}) async-start(bf16[16,2,128,256]{3,2,1,0:T(8,128)(2,1)} %bitcast.39), calls=%async_computation | async-start | bytes 4194304 | tf_op jit(solution)/shard_map/all_to_all | solution.py:190
  20.6 146.3 %reduce-scatter.2.cloned.1.call-start = ((), (), s32[]{:S(2)}) async-start(), calls=%async_computation.6 | async-start | bytes 3244032 | tf_op jit(solution)/shard_map/reduce_scatter | solution.py:214
  48.8 1.4 copy-start
  97.5 1.0 copy-start.2
  100.0 16.6 %slice-start = ((bf16[96,176,128]{2,1,0:T(8,128)(2,1)}), bf16[32,176,128]{2,1,0:T(8,128)(2,1)S(1)}, s32[]{:S(2)}) async-start(bf16[96,176,128]{2,1,0:T(8,128)(2,1)} %shard_map.113), calls=%async_computation.7 | async-start | bytes 2883584 | tf_op jit(solution)/shard_map/slice | solution.py:224
  100.0 16.1 %all-to-all-start.1 = ((f32[8,1,11008]{2,1,0:T(1,128)}), f32[8,1,11008]{2,1,0:T(1,128)S(1)}, u32[]{:S(2)}, u32[]{:S(2)}) async-start(f32[8,1,11008]{2,1,0:T(1,128)} %all_to_all.21), calls=%async_computation.2 | async-start | bytes 704512 | tf_op jit(solution)/shard_map/all_to_all | solution.py:218
  144.9 7.8 %copy-start.6 = (s32[1,16,2]{1,2,0:T(2,128)S(1)}, s32[1,16,2]{1,2,0:T(2,128)}, u32[]{:S(2)}) copy-start(s32[1,16,2]{1,2,0:T(2,128)} %param.13) | copy-start | bytes 388
  146.0 18.8 %all-to-all-start.3 = ((f32[128,1,688]{2,1,0:T(1,128)}), f32[128,1,688]{2,1,0:T(1,128)S(1)}, u32[]{:S(2)}, u32[]{:S(2)}) async-start(f32[128,1,688]{2,1,0:T(1,128)} %broadcast_in_dim.12), calls=%async_computation.4 | async-start | bytes 786432 | tf_op jit(solution)/shard_map/all_to_all | solution.py:230
  153.3 13.6 %copy-start.1 = (f32[8,128,256]{2,1,0:T(8,128)S(1)}, f32[8,128,256]{2,1,0:T(8,128)}, u32[]{:S(2)}) copy-start(f32[8,128,256]{2,1,0:T(8,128)} %get-tuple-element.8) | copy-start | bytes 3145732
Sparse Core Ops, SparseCore 0:
  9.7 35.6 all-gather.1
  97.6 38.6 reduce-scatter.1

commit v9 on v8

--- a/solution.py
+++ b/solution.py
@@ -80,7 +80,7 @@
     scaled_ref[0] = (residual / deg).astype(jnp.bfloat16).T
 
 
-def _backward_kernel(src_ref, live_ref, w_ref, scaled_ref, out_ref, term_ref):
+def _backward_kernel(src_ref, live_ref, w_ref, scaled_ref, local_ref, halo_ref, term_ref, *, spare):
     b = pl.program_id(0)
 
     @pl.when(b == 0)
@@ -102,10 +102,21 @@
 
     @pl.when(b == pl.num_programs(0) - 1)
     def _():
-        out_ref[...] = term_ref[:, : out_ref.shape[1], :].astype(out_ref.dtype)
-
-
-def _fused(tile_source, tile_live, tile_weight, partition, boundary, own_blocks, deg, lab, nw, sw, swt, classes):
+        part_total, kept, rows = local_ref.shape
+        peers = halo_ref.shape[0]
+        slots = (halo_ref.shape[1] - spare) // kept
+        local_ref[...] = term_ref[:part_total, :kept, :].astype(local_ref.dtype)
+        for p in range(peers):
+            for k in range(slots):
+                halo_ref[p, k * kept : (k + 1) * kept, :] = term_ref[
+                    part_total + p * slots + k, :kept, :
+                ].astype(halo_ref.dtype)
+            halo_ref[p, slots * kept :, :] = jnp.zeros((spare, rows), halo_ref.dtype)
+
+
+def _fused(
+    tile_source, tile_live, tile_weight, partition, boundary, own_blocks, deg, lab, nw, sw, swt, classes, peers, spare
+):
     block_count, tile_slots, rows, _ = tile_weight.shape
     part_total, _, width = partition.shape
     source_total = part_total + boundary.shape[0]
@@ -144,20 +155,27 @@
         ],
         compiler_params=params,
     )(tile_source, tile_live, tile_weight, partition, boundary, own_blocks, deg, lab, nw, sw, swt)
+    halo_shape = (peers, (source_total - part_total) // peers * kept + spare, rows)
     grid_spec = pltpu.PrefetchScalarGridSpec(
         num_scalar_prefetch=2,
         grid=(block_count,),
         in_specs=[w_spec, scaled_spec],
-        out_specs=[pl.BlockSpec((source_total, kept, rows), lambda b, *_: (0, 0, 0))],
+        out_specs=[
+            pl.BlockSpec((part_total, kept, rows), lambda b, *_: (0, 0, 0)),
+            pl.BlockSpec(halo_shape, lambda b, *_: (0, 0, 0)),
+        ],
         scratch_shapes=[pltpu.VMEM((source_total, padded, rows), jnp.float32)],
     )
-    (term,) = pl.pallas_call(
-        _backward_kernel,
+    local, halo = pl.pallas_call(
+        functools.partial(_backward_kernel, spare=spare),
         grid_spec=grid_spec,
-        out_shape=[jax.ShapeDtypeStruct((source_total, kept, rows), jnp.bfloat16)],
+        out_shape=[
+            jax.ShapeDtypeStruct((part_total, kept, rows), jnp.bfloat16),
+            jax.ShapeDtypeStruct(halo_shape, jnp.bfloat16),
+        ],
         compiler_params=params,
     )(tile_source, tile_live, tile_weight, scaled)
-    return term, grads, selfterm
+    return local, halo, grads, selfterm
 
 
 def _per_device(
@@ -182,7 +200,6 @@
     padded = -(-classes // LANES) * LANES
     own_blocks = history.reshape(block_count, block_rows, width)
     partition = lax.all_gather(own_blocks, "sub", axis=0, tiled=True)
-    part_blocks = partition.shape[0]
     own_ids = jnp.arange(block_count, dtype=jnp.int32)
     send_table = send_list[0][:, :, None] == own_ids[None, None, :]
     outgoing = jnp.take(own_blocks, send_list[0].reshape(-1), axis=0, mode="clip")
@@ -196,12 +213,15 @@
     nw = jnp.pad(neigh_weight, pad_cols)
     sw = jnp.pad(self_weight, pad_cols)
     swt = jnp.pad(self_weight.T, ((0, padded - classes), (0, 0)))
-    term, grads, selfterm = _fused(
-        tile_source, tile_live, tile_weight, partition, boundary, own_blocks, degrees, lab, nw, sw, swt, classes
+    kept = -(-classes // 16) * 16
+    piece = 2 * width * classes // devices_all
+    spare = -(-2 * piece // (16 * block_rows)) * 16
+    local_term, halo_term, grads, selfterm = _fused(
+        tile_source, tile_live, tile_weight, partition, boundary, own_blocks, degrees, lab, nw, sw, swt, classes,
+        dom_count, spare,
     )
 
     norm_factor = float(nodes_all) ** (-0.5)
-    kept = term.shape[1]
 
     def split(x, size):
         hi = x.astype(jnp.bfloat16)
@@ -211,18 +231,14 @@
     def joined(x, half):
         return x[:, :half].astype(jnp.float32) + x[:, half : 2 * half].astype(jnp.float32)
 
-    local_grad = lax.psum_scatter(
-        term[:part_blocks], "sub", scatter_dimension=0, tiled=True
-    ).astype(jnp.float32)
+    local_grad = lax.psum_scatter(local_term, "sub", scatter_dimension=0, tiled=True).astype(jnp.float32)
     flat = grads[:, :, :classes].reshape(sub_count, -1)
     part_sum = lax.all_to_all(flat, "sub", 0, 0, tiled=True)
     part_sum = part_sum.sum(axis=0)
     part_sum = part_sum.reshape(dom_count, -1)
-    piece = part_sum.shape[1]
-    extra_rows = -(-2 * piece // (16 * block_rows)) * 16
-    extra = split(part_sum, extra_rows * block_rows).reshape(dom_count, extra_rows, block_rows)
-    halo = term[part_blocks:].reshape(dom_count, slot_count * kept, block_rows)
-    got = lax.all_to_all(jnp.concatenate([halo, extra], axis=1), "dom", 0, 0, tiled=True)
+    extra = split(part_sum, spare * block_rows).reshape(dom_count, spare, block_rows)
+    sent = lax.dynamic_update_slice(halo_term, extra, (0, slot_count * kept, 0))
+    got = lax.all_to_all(sent, "dom", 0, 0, tiled=True)
     arrived = got[:, : slot_count * kept].astype(jnp.float32)
     arrived = arrived.reshape(dom_count, slot_count, kept, block_rows)
     mine = joined(got[:, slot_count * kept :].reshape(dom_count, -1), piece).sum(axis=0, keepdims=True)

time: 178 us -> 172 us (0.966)
  blocking collectives: 28.2 us -> 43.9 us
  waiting for transfers between devices: 44 us -> 35.4 us
  starting transfers between devices: 23.5 us -> 15.4 us
  local copies, waits for them, and re-layouts: 19 us -> 14.2 us
    all_to_all x1 -> x2, blocking collectives: 28.2 us -> 43.9 us  [the longest x1 27.9 us: _per_device(): got = lax.all_to_all(sent, 'dom', 0, 0, tiled=True)]
    all_to_all x1 -> x0, starting transfers between devices: 8.07 us -> none  [_per_device(): part_sum = lax.all_to_all(flat, 'sub', 0, 0, tiled=True)]
    all_to_all x1 -> x0, waiting for transfers between devices: 8.04 us -> none  [_per_device(): part_sum = lax.all_to_all(flat, 'sub', 0, 0, tiled=True)]
    slice x3 -> x0, local copies, waits for them, and re-layouts: 3.59 us -> none  [the longest x1 3.59 us: _per_device(): term[:part_blocks]]
    unnamed x24 -> x30, local copies, waits for them, and re-layouts: 4.98 us -> 5.56 us
  transfers between devices with their start and end apart: 5 -> 4, of which waited for: 3 -> 2; matrix products, arithmetic and copies ran while one was open for 7% -> 7% of each run, Pallas kernels for 0% -> 0%
where the time goes in v9:
time: 172 us; the launch traced here: 171 us
  Pallas kernels  43.9 us (26%)
  blocking collectives  43.9 us (26%)
  waiting for transfers between devices  35.4 us (21%)
  starting transfers between devices  15.4 us (9%)
  between operations  14.3 us (8%)
  local copies, waits for them, and re-layouts  14.2 us (8%)
  matrix products  3.53 us (2%)
    all_to_all x1, blocking collectives, _per_device(): got = lax.all_to_all(sent, 'dom', 0, 0, tiled=True)  27.9 us
    all_to_all x1, waiting for transfers between devices, _per_device(): lax.all_to_all(outgoing, 'dom', split_axis=0, concat_axis=0, tiled=True)  23.7 us
    pallas_call x1, Pallas kernels, _fused(): pl.pallas_call(functools.partial(_forward_kernel, classes=classes), grid_...  22.9 us
    pallas_call x1, Pallas kernels, _fused(): pl.pallas_call(functools.partial(_backward_kernel, spare=spare), grid_spe...  21 us
    all_to_all x1, blocking collectives, _per_device(): part_sum = lax.all_to_all(flat, 'sub', 0, 0, tiled=True)  16 us
    all_to_all x1, waiting for transfers between devices, _per_device(): totals = lax.all_to_all(spread, ('dom', 'sub'), 0, 0, tiled=True)  11 us
    all_to_all x1, starting transfers between devices, _per_device(): lax.all_to_all(outgoing, 'dom', split_axis=0, concat_axis=0, tiled=True)  8.73 us
    all_to_all x1, starting transfers between devices, _per_device(): totals = lax.all_to_all(spread, ('dom', 'sub'), 0, 0, tiled=True)  6.62 us
  transfers between devices with their start and end apart: 4, of which 2 were waited for; matrix products, arithmetic and copies ran while one was open for 7% of the time, Pallas kernels for 0%

profile of v9, /device:TPU:1, one launch (start us, length us, event | category | flops | bytes accessed | tf_op | source)
XLA Modules:
  0.0 171.1 jit_solution(14788214858991632099)
XLA Ops:
  7.2 0.0 copy-start
  7.2 0.0 all-gather.2.cloned.1.call-start
  7.2 0.7 all-gather.2.cloned.1.call-update
  7.9 0.8 copy.38
  8.7 0.1 reshape.73
  8.8 0.0 copy-done
  8.8 2.0 %gather_fusion = bf16[32,128,256]{2,1,0:T(8,128)(2,1)} fusion(bf16[8,128,256]{2,1,0:T(8,128)(2,1)S(1)} %bitcast.35, s32[1024]{0:T(1024)S(1)} %pad_clamp_fusion), kind=kCustom, calls=%fused_computation | custom fusion | bytes 4194432 | tf_op jit(solution)/shard_map/jit(_take)/gather | solution.py:205
  10.8 0.0 copy-start.10
  10.8 0.0 copy-start.8
  10.8 0.0 copy-start.6
  10.8 0.0 copy-start.7
  10.8 8.7 %all-to-all-start = ((bf16[16,2,128,256]{3,2,1,0:T(8,128)(2,1)}), bf16[16,2,128,256]{3,2,1,0:T(8,128)(2,1)S(1)}, u32[]{:S(2)}, u32[]{:S(2)}) async-start(bf16[16,2,128,256]{3,2,1,0:T(8,128)(2,1)} %bitcast.37), calls=%async_computation | async-start | bytes 4194304 | tf_op jit(solution)/shard_map/all_to_all | solution.py:207
  19.6 0.0 reduce-scatter.2.cloned.1.call-start
  19.6 0.0 copy-done.10
  19.6 1.0 copy.41.deg_ref
  20.7 0.0 copy-done.8
  20.7 1.1 copy.42.lab_ref
  21.8 0.0 copy-done.6
  21.8 0.1 copy.39
  21.9 0.0 copy-done.7
  21.9 0.1 copy.40
  22.0 0.7 pad.15.nw_ref
  22.7 0.7 pad.16.sw_ref
  23.3 0.7 pad.17.swt_ref
  24.0 23.7 %all-to-all-done = bf16[16,2,128,256]{3,2,1,0:T(8,128)(2,1)S(1)} async-done(((bf16[16,2,128,256]{3,2,1,0:T(8,128)(2,1)}), bf16[16,2,128,256]{3,2,1,0:T(8,128)(2,1)S(1)}, u32[]{:S(2)}, u32[]{:S(2)}) %all-to-all-start) | async-done | bytes 2097184 | tf_op jit(solution)/shard_map/all_to_all | solution.py:207
  47.7 0.0 copy-start.1
  47.7 0.0 all-gather.2.cloned.1.call-done.part_ref
  47.7 1.4 copy-done.1
  49.1 22.9 %shard_map.112 = (f32[2,256,256]{2,1,0:T(8,128)}, f32[8,128,256]{2,1,0:T(8,128)}, bf16[8,256,128]{2,1,0:T(8,128)(2,1)}) custom-call(s32[8,64]{1,0:T(8,128)} %src_ref.3, s32[8]{0:T(128)} %live_ref.3, bf16[8,64,128,128]{3,2,1,0:T(8,128)(2,1)} %w_ref.3, bf16[64,128,256]{2,1,0:T(8,128)(2,1)} %all-gather.2.cloned.1.call-done.part_ref, ...), custom_call_target="tpu_custom_call" | custom-call | tf_op jit(solution)/shard_map/pallas_call | solution.py:148
  72.0 21.0 %shard_map.113 = (bf16[64,176,128]{2,1,0:T(8,128)(2,1)}, bf16[16,368,128]{2,1,0:T(8,128)(2,1)}) custom-call(s32[8,64]{1,0:T(8,128)} %src_ref.3, s32[8]{0:T(128)} %live_ref.3, bf16[8,64,128,128]{3,2,1,0:T(8,128)(2,1)} %w_ref.3, bf16[8,256,128]{2,1,0:T(8,128)(2,1)} %get-tuple-element.8.scaled_ref), custom_call_target="tpu_custom_call" | custom-call | tf_op jit(solution)/shard_map/pallas_call | solution.py:169
  93.0 0.0 copy-start.5
  93.0 0.0 reduce-scatter.2.cloned.1.call-update
  93.0 0.0 copy-start.3
  93.0 1.0 copy-done.5
  94.0 0.8 all_to_all.21
  94.8 16.0 %all_to_all.26 = f32[8,1,11008]{2,1,0:T(1,128)S(1)} all-to-all(f32[8,1,11008]{2,1,0:T(1,128)S(1)} %all_to_all.21), channel_id=1, replica_groups=mesh['dom'=16,'sub'=8] {'sub'}, dimensions={0} | all-to-all | bytes 704512 | tf_op jit(solution)/shard_map/all_to_all | solution.py:236
  110.8 0.3 reduce_sum.18
  111.0 0.1 reshape.66
  111.2 0.1 fusion.11
  111.3 0.0 copy-done.3
  111.3 27.9 %all_to_all.27 = bf16[16,368,128]{2,1,0:T(8,128)(2,1)S(1)} all-to-all(bf16[16,368,128]{2,1,0:T(8,128)(2,1)S(1)} %constant_dynamic-update-slice_fusion), channel_id=1, replica_groups=mesh['dom'=16,'sub'=8] {'dom'}, dimensions={0} | all-to-all | bytes 3014656 | tf_op jit(solution)/shard_map/all_to_all | solution.py:241
  139.3 0.1 add_reduce_fusion
  139.3 1.0 broadcast_in_dim.12
  140.3 6.6 %all-to-all-start.3 = ((f32[128,1,688]{2,1,0:T(1,128)}), f32[128,1,688]{2,1,0:T(1,128)S(1)}, u32[]{:S(2)}, u32[]{:S(2)}) async-start(f32[128,1,688]{2,1,0:T(1,128)} %broadcast_in_dim.12), calls=%async_computation.4 | async-start | bytes 786432 | tf_op jit(solution)/shard_map/all_to_all | solution.py:246
  146.9 0.0 copy-start.9
  146.9 0.1 slice.36
  147.0 0.6 copy-done.9
  147.6 0.5 fusion.2
  148.1 0.0 copy-start.2
  148.1 11.0 %all-to-all-done.3 = f32[128,1,688]{2,1,0:T(1,128)S(1)} async-done(((f32[128,1,688]{2,1,0:T(1,128)}), f32[128,1,688]{2,1,0:T(1,128)S(1)}, u32[]{:S(2)}, u32[]{:S(2)}) %all-to-all-start.3) | async-done | bytes 352288 | tf_op jit(solution)/shard_map/all_to_all | solution.py:246
  159.2 0.0 copy-start.4
  159.2 0.1 copy.64
  159.4 0.0 copy-done.2
  159.4 0.0 slice-start
  159.4 0.1 mul.13
  159.5 0.8 copy.47
  160.3 0.1 mul.15
  160.5 0.8 copy.48
  161.2 0.0 reduce-scatter.2.cloned.1.call-done
  161.2 0.0 copy-done.4
  161.2 0.0 slice-done
  161.2 3.0 %convolution_add_fusion = f32[8,128,256]{2,1,0:T(8,128)} fusion(f32[8,128,256]{2,1,0:T(8,128)S(1)} %copy-done.4, f32[8,172,128]{2,0,1:T(8,128)S(1)} %slice-done, bf16[8,176,128]{2,1,0:T(8,128)(2,1)} %reduce-scatter.2.cloned.1.call-done, bf16[256,172]{0,1:T(8,128)(2,1)S(1)} %copy-done.6), kind=kOutput, calls=%fused_computation.3 | convolution fusion | flops 541679616 | bytes 3250176 | tf_op jit(solution)/shard_map/sci,fc->sif/dot_general | solution.py:253
  (9 shorter events, 0.1 us)
Async XLA Ops:
  7.2 1.6 copy-start
  7.2 40.6 %all-gather.2.cloned.1.call-start = ((), (), s32[]{:S(2)}) async-start(), calls=%async_computation.5 | async-start | bytes 4718592 | tf_op jit(solution)/shard_map/all_gather | solution.py:202
  10.8 8.8 %copy-start.10 = (s32[1024]{0:T(1024)S(1)}, s32[1024]{0:T(1024)}, u32[]{:S(2)}) copy-start(s32[1024]{0:T(1024)} %param.14) | copy-start | bytes 12292
  10.8 9.9 %copy-start.8 = (s32[1024]{0:T(1024)S(1)}, s32[1024]{0:T(1024)}, u32[]{:S(2)}) copy-start(s32[1024]{0:T(1024)} %param.15) | copy-start | bytes 12292
  10.8 10.9 %copy-start.6 = (bf16[256,172]{0,1:T(8,128)(2,1)S(1)}, bf16[256,172]{0,1:T(8,128)(2,1)}, u32[]{:S(2)}) copy-start(bf16[256,172]{0,1:T(8,128)(2,1)} %param.16) | copy-start | bytes 264196
  10.8 11.0 %copy-start.7 = (bf16[256,172]{0,1:T(8,128)(2,1)S(1)}, bf16[256,172]{0,1:T(8,128)(2,1)}, u32[]{:S(2)}) copy-start(bf16[256,172]{0,1:T(8,128)(2,1)} %param.17) | copy-start | bytes 264196
  10.8 36.9 %all-to-all-start = ((bf16[16,2,128,256]{3,2,1,0:T(8,128)(2,1)}), bf16[16,2,128,256]{3,2,1,0:T(8,128)(2,1)S(1)}, u32[]{:S(2)}, u32[]{:S(2)}) async-start(bf16[16,2,128,256]{3,2,1,0:T(8,128)(2,1)} %bitcast.37), calls=%async_computation | async-start | bytes 4194304 | tf_op jit(solution)/shard_map/all_to_all | solution.py:207
  19.6 141.7 %reduce-scatter.2.cloned.1.call-start = ((), (), s32[]{:S(2)}) async-start(), calls=%async_computation.6 | async-start | bytes 3244032 | tf_op jit(solution)/shard_map/reduce_scatter | solution.py:234
  47.7 1.4 copy-start.1
  93.0 1.0 copy-start.5
  93.0 18.2 %copy-start.3 = (bf16[16,368,128]{2,1,0:T(8,128)(2,1)S(1)}, bf16[16,368,128]{2,1,0:T(8,128)(2,1)}, u32[]{:S(2)}) copy-start(bf16[16,368,128]{2,1,0:T(8,128)(2,1)} %get-tuple-element.10) | copy-start | bytes 4521988
  140.3 18.8 %all-to-all-start.3 = ((f32[128,1,688]{2,1,0:T(1,128)}), f32[128,1,688]{2,1,0:T(1,128)S(1)}, u32[]{:S(2)}, u32[]{:S(2)}) async-start(f32[128,1,688]{2,1,0:T(1,128)} %broadcast_in_dim.12), calls=%async_computation.4 | async-start | bytes 786432 | tf_op jit(solution)/shard_map/all_to_all | solution.py:246
  146.9 0.7 copy-start.9
  148.1 11.2 %copy-start.2 = (f32[8,176,128]{2,0,1:T(8,128)}, f32[8,176,128]{2,0,1:T(8,128)S(1)}, u32[]{:S(2)}) copy-start(f32[8,176,128]{2,0,1:T(8,128)S(1)} %fusion.2) | copy-start | bytes 2162692
  159.2 2.1 %copy-start.4 = (f32[8,128,256]{2,1,0:T(8,128)S(1)}, f32[8,128,256]{2,1,0:T(8,128)}, u32[]{:S(2)}) copy-start(f32[8,128,256]{2,1,0:T(8,128)} %get-tuple-element.12) | copy-start | bytes 3145732
  159.4 1.9 %slice-start = ((f32[8,176,128]{2,0,1:T(8,128)}), f32[8,172,128]{2,0,1:T(8,128)S(1)}, s32[]{:S(2)}) async-start(f32[8,176,128]{2,0,1:T(8,128)} %copy-done.2), calls=%async_computation.7 | async-start | bytes 1409024 | tf_op jit(solution)/shard_map/slice | solution.py:251
Sparse Core Ops, SparseCore 0:
  9.7 35.6 all-gather.1
  93.1 38.0 reduce-scatter.1

commit v10 on v9

--- a/solution.py
+++ b/solution.py
@@ -9,7 +9,8 @@
 
 
 LANES = 128
-GROUP = 8
+GROUP = 32
+FORWARD_GROUP = 32
 
 
 def _tile(w_ref, t, live):
@@ -50,10 +51,10 @@
         return jnp.where(s < part_total, inside, outside)
 
     live = live_ref[b]
-    groups = (live + GROUP - 1) // GROUP
+    groups = (live + FORWARD_GROUP - 1) // FORWARD_GROUP
 
     def forward(g, acc):
-        ts = [g * GROUP + k for k in range(GROUP)]
+        ts = [g * FORWARD_GROUP + k for k in range(FORWARD_GROUP)]
         wcat = jnp.concatenate([_tile(w_ref, t, live) for t in ts], axis=1)
         scat = jnp.concatenate([source(src_ref[b, t]) for t in ts], axis=0)
         return acc + jnp.dot(wcat, scat, preferred_element_type=jnp.float32)

time: 172 us -> 160 us (0.930)
  Pallas kernels: 43.9 us -> 36.2 us
  blocking collectives: 43.9 us -> 40.6 us
    pallas_call x1, Pallas kernels: 22.9 us -> 18.4 us  [_fused(): pl.pallas_call(functools.partial(_forward_kernel, classes=classes), grid_...]
    all_to_all x1, blocking collectives: 27.9 us -> 23.5 us  [_per_device(): got = lax.all_to_all(sent, 'dom', 0, 0, tiled=True)]
    pallas_call x1, Pallas kernels: 21 us -> 17.8 us  [_fused(): pl.pallas_call(functools.partial(_backward_kernel, spare=spare), grid_spe...]
where the time goes in v10:
time: 160 us; the launch traced here: 159 us
  blocking collectives  40.6 us (25%)
  Pallas kernels  36.2 us (23%)
  waiting for transfers between devices  35.4 us (22%)
  starting transfers between devices  14.5 us (9%)
  between operations  14.3 us (9%)
  local copies, waits for them, and re-layouts  14.2 us (9%)
  matrix products  3.53 us (2%)
    all_to_all x1, waiting for transfers between devices, _per_device(): lax.all_to_all(outgoing, 'dom', split_axis=0, concat_axis=0, tiled=True)  23.7 us
    all_to_all x1, blocking collectives, _per_device(): got = lax.all_to_all(sent, 'dom', 0, 0, tiled=True)  23.5 us
    pallas_call x1, Pallas kernels, _fused(): pl.pallas_call(functools.partial(_forward_kernel, classes=classes), grid_...  18.4 us
    pallas_call x1, Pallas kernels, _fused(): pl.pallas_call(functools.partial(_backward_kernel, spare=spare), grid_spe...  17.8 us
    all_to_all x1, blocking collectives, _per_device(): part_sum = lax.all_to_all(flat, 'sub', 0, 0, tiled=True)  17.1 us
    all_to_all x1, waiting for transfers between devices, _per_device(): totals = lax.all_to_all(spread, ('dom', 'sub'), 0, 0, tiled=True)  11 us
    all_to_all x1, starting transfers between devices, _per_device(): lax.all_to_all(outgoing, 'dom', split_axis=0, concat_axis=0, tiled=True)  8.73 us
    all_to_all x1, starting transfers between devices, _per_device(): totals = lax.all_to_all(spread, ('dom', 'sub'), 0, 0, tiled=True)  5.72 us
  transfers between devices with their start and end apart: 4, of which 2 were waited for; matrix products, arithmetic and copies ran while one was open for 7% of the time, Pallas kernels for 0%

profile of v10, /device:TPU:1, one launch (start us, length us, event | category | flops | bytes accessed | tf_op | source)
XLA Modules:
  0.0 159.3 jit_solution(16554364107897558817)
XLA Ops:
  7.2 0.0 copy-start
  7.2 0.0 all-gather.2.cloned.1.call-start
  7.2 0.7 all-gather.2.cloned.1.call-update
  7.9 0.8 copy.38
  8.7 0.1 reshape.73
  8.8 0.0 copy-done
  8.8 2.0 %gather_fusion = bf16[32,128,256]{2,1,0:T(8,128)(2,1)} fusion(bf16[8,128,256]{2,1,0:T(8,128)(2,1)S(1)} %bitcast.35, s32[1024]{0:T(1024)S(1)} %pad_clamp_fusion), kind=kCustom, calls=%fused_computation | custom fusion | bytes 4194432 | tf_op jit(solution)/shard_map/jit(_take)/gather | solution.py:206
  10.8 0.0 copy-start.10
  10.8 0.0 copy-start.8
  10.8 0.0 copy-start.6
  10.8 0.0 copy-start.7
  10.8 8.7 %all-to-all-start = ((bf16[16,2,128,256]{3,2,1,0:T(8,128)(2,1)}), bf16[16,2,128,256]{3,2,1,0:T(8,128)(2,1)S(1)}, u32[]{:S(2)}, u32[]{:S(2)}) async-start(bf16[16,2,128,256]{3,2,1,0:T(8,128)(2,1)} %bitcast.37), calls=%async_computation | async-start | bytes 4194304 | tf_op jit(solution)/shard_map/all_to_all | solution.py:208
  19.6 0.0 reduce-scatter.2.cloned.1.call-start
  19.6 0.0 copy-done.10
  19.6 1.0 copy.41.deg_ref
  20.7 0.0 copy-done.8
  20.7 1.1 copy.42.lab_ref
  21.8 0.0 copy-done.6
  21.8 0.1 copy.39
  21.9 0.0 copy-done.7
  21.9 0.1 copy.40
  22.0 0.7 pad.15.nw_ref
  22.7 0.7 pad.16.sw_ref
  23.3 0.7 pad.17.swt_ref
  24.0 23.7 %all-to-all-done = bf16[16,2,128,256]{3,2,1,0:T(8,128)(2,1)S(1)} async-done(((bf16[16,2,128,256]{3,2,1,0:T(8,128)(2,1)}), bf16[16,2,128,256]{3,2,1,0:T(8,128)(2,1)S(1)}, u32[]{:S(2)}, u32[]{:S(2)}) %all-to-all-start) | async-done | bytes 2097184 | tf_op jit(solution)/shard_map/all_to_all | solution.py:208
  47.7 0.0 copy-start.1
  47.7 0.0 all-gather.2.cloned.1.call-done.part_ref
  47.7 1.4 copy-done.1
  49.1 18.4 %shard_map.112 = (f32[2,256,256]{2,1,0:T(8,128)}, f32[8,128,256]{2,1,0:T(8,128)}, bf16[8,256,128]{2,1,0:T(8,128)(2,1)}) custom-call(s32[8,64]{1,0:T(8,128)} %src_ref.3, s32[8]{0:T(128)} %live_ref.3, bf16[8,64,128,128]{3,2,1,0:T(8,128)(2,1)} %w_ref.3, bf16[64,128,256]{2,1,0:T(8,128)(2,1)} %all-gather.2.cloned.1.call-done.part_ref, ...), custom_call_target="tpu_custom_call" | custom-call | tf_op jit(solution)/shard_map/pallas_call | solution.py:149
  67.5 17.8 %shard_map.113 = (bf16[64,176,128]{2,1,0:T(8,128)(2,1)}, bf16[16,368,128]{2,1,0:T(8,128)(2,1)}) custom-call(s32[8,64]{1,0:T(8,128)} %src_ref.3, s32[8]{0:T(128)} %live_ref.3, bf16[8,64,128,128]{3,2,1,0:T(8,128)(2,1)} %w_ref.3, bf16[8,256,128]{2,1,0:T(8,128)(2,1)} %get-tuple-element.8.scaled_ref), custom_call_target="tpu_custom_call" | custom-call | tf_op jit(solution)/shard_map/pallas_call | solution.py:170
  85.3 0.0 copy-start.5
  85.3 0.0 reduce-scatter.2.cloned.1.call-update
  85.3 0.0 copy-start.3
  85.4 1.0 copy-done.5
  86.4 0.8 all_to_all.21
  87.2 17.1 %all_to_all.26 = f32[8,1,11008]{2,1,0:T(1,128)S(1)} all-to-all(f32[8,1,11008]{2,1,0:T(1,128)S(1)} %all_to_all.21), channel_id=1, replica_groups=mesh['dom'=16,'sub'=8] {'sub'}, dimensions={0} | all-to-all | bytes 704512 | tf_op jit(solution)/shard_map/all_to_all | solution.py:237
  104.2 0.3 reduce_sum.18
  104.5 0.1 reshape.66
  104.6 0.1 fusion.11
  104.7 0.0 copy-done.3
  104.7 23.5 %all_to_all.27 = bf16[16,368,128]{2,1,0:T(8,128)(2,1)S(1)} all-to-all(bf16[16,368,128]{2,1,0:T(8,128)(2,1)S(1)} %constant_dynamic-update-slice_fusion), channel_id=1, replica_groups=mesh['dom'=16,'sub'=8] {'dom'}, dimensions={0} | all-to-all | bytes 3014656 | tf_op jit(solution)/shard_map/all_to_all | solution.py:242
  128.3 0.1 add_reduce_fusion
  128.4 1.0 broadcast_in_dim.12
  129.4 5.7 %all-to-all-start.3 = ((f32[128,1,688]{2,1,0:T(1,128)}), f32[128,1,688]{2,1,0:T(1,128)S(1)}, u32[]{:S(2)}, u32[]{:S(2)}) async-start(f32[128,1,688]{2,1,0:T(1,128)} %broadcast_in_dim.12), calls=%async_computation.4 | async-start | bytes 786432 | tf_op jit(solution)/shard_map/all_to_all | solution.py:247
  135.1 0.0 copy-start.9
  135.1 0.1 slice.36
  135.2 0.6 copy-done.9
  135.8 0.5 fusion.2
  136.3 0.0 copy-start.2
  136.3 11.0 %all-to-all-done.3 = f32[128,1,688]{2,1,0:T(1,128)S(1)} async-done(((f32[128,1,688]{2,1,0:T(1,128)}), f32[128,1,688]{2,1,0:T(1,128)S(1)}, u32[]{:S(2)}, u32[]{:S(2)}) %all-to-all-start.3) | async-done | bytes 352288 | tf_op jit(solution)/shard_map/all_to_all | solution.py:247
  147.3 0.0 copy-start.4
  147.3 0.1 copy.64
  147.5 0.0 copy-done.2
  147.5 0.0 slice-start
  147.5 0.1 mul.13
  147.7 0.8 copy.47
  148.5 0.1 mul.15
  148.6 0.8 copy.48
  149.4 0.0 reduce-scatter.2.cloned.1.call-done
  149.4 0.0 copy-done.4
  149.4 0.0 slice-done
  149.4 3.0 %convolution_add_fusion = f32[8,128,256]{2,1,0:T(8,128)} fusion(f32[8,128,256]{2,1,0:T(8,128)S(1)} %copy-done.4, f32[8,172,128]{2,0,1:T(8,128)S(1)} %slice-done, bf16[8,176,128]{2,1,0:T(8,128)(2,1)} %reduce-scatter.2.cloned.1.call-done, bf16[256,172]{0,1:T(8,128)(2,1)S(1)} %copy-done.6), kind=kOutput, calls=%fused_computation.3 | convolution fusion | flops 541679616 | bytes 3250176 | tf_op jit(solution)/shard_map/sci,fc->sif/dot_general | solution.py:254
  (9 shorter events, 0.1 us)
Async XLA Ops:
  7.2 1.6 %copy-start = (bf16[1024,256]{1,0:T(8,128)(2,1)S(1)}, bf16[1024,256]{1,0:T(8,128)(2,1)}, u32[]{:S(2)}) copy-start(bf16[1024,256]{1,0:T(8,128)(2,1)} %param.9) | copy-start | bytes 1572868
  7.2 40.6 %all-gather.2.cloned.1.call-start = ((), (), s32[]{:S(2)}) async-start(), calls=%async_computation.5 | async-start | bytes 4718592 | tf_op jit(solution)/shard_map/all_gather | solution.py:203
  10.8 8.8 %copy-start.10 = (s32[1024]{0:T(1024)S(1)}, s32[1024]{0:T(1024)}, u32[]{:S(2)}) copy-start(s32[1024]{0:T(1024)} %param.14) | copy-start | bytes 12292
  10.8 9.9 %copy-start.8 = (s32[1024]{0:T(1024)S(1)}, s32[1024]{0:T(1024)}, u32[]{:S(2)}) copy-start(s32[1024]{0:T(1024)} %param.15) | copy-start | bytes 12292
  10.8 10.9 %copy-start.6 = (bf16[256,172]{0,1:T(8,128)(2,1)S(1)}, bf16[256,172]{0,1:T(8,128)(2,1)}, u32[]{:S(2)}) copy-start(bf16[256,172]{0,1:T(8,128)(2,1)} %param.16) | copy-start | bytes 264196
  10.8 11.0 %copy-start.7 = (bf16[256,172]{0,1:T(8,128)(2,1)S(1)}, bf16[256,172]{0,1:T(8,128)(2,1)}, u32[]{:S(2)}) copy-start(bf16[256,172]{0,1:T(8,128)(2,1)} %param.17) | copy-start | bytes 264196
  10.8 36.9 %all-to-all-start = ((bf16[16,2,128,256]{3,2,1,0:T(8,128)(2,1)}), bf16[16,2,128,256]{3,2,1,0:T(8,128)(2,1)S(1)}, u32[]{:S(2)}, u32[]{:S(2)}) async-start(bf16[16,2,128,256]{3,2,1,0:T(8,128)(2,1)} %bitcast.37), calls=%async_computation | async-start | bytes 4194304 | tf_op jit(solution)/shard_map/all_to_all | solution.py:208
  19.6 129.8 %reduce-scatter.2.cloned.1.call-start = ((), (), s32[]{:S(2)}) async-start(), calls=%async_computation.6 | async-start | bytes 3244032 | tf_op jit(solution)/shard_map/reduce_scatter | solution.py:235
  47.7 1.4 copy-start.1
  85.3 1.0 copy-start.5
  85.3 19.4 %copy-start.3 = (bf16[16,368,128]{2,1,0:T(8,128)(2,1)S(1)}, bf16[16,368,128]{2,1,0:T(8,128)(2,1)}, u32[]{:S(2)}) copy-start(bf16[16,368,128]{2,1,0:T(8,128)(2,1)} %get-tuple-element.10) | copy-start | bytes 4521988
  129.4 17.9 %all-to-all-start.3 = ((f32[128,1,688]{2,1,0:T(1,128)}), f32[128,1,688]{2,1,0:T(1,128)S(1)}, u32[]{:S(2)}, u32[]{:S(2)}) async-start(f32[128,1,688]{2,1,0:T(1,128)} %broadcast_in_dim.12), calls=%async_computation.4 | async-start | bytes 786432 | tf_op jit(solution)/shard_map/all_to_all | solution.py:247
  135.1 0.7 copy-start.9
  136.3 11.2 %copy-start.2 = (f32[8,176,128]{2,0,1:T(8,128)}, f32[8,176,128]{2,0,1:T(8,128)S(1)}, u32[]{:S(2)}) copy-start(f32[8,176,128]{2,0,1:T(8,128)S(1)} %fusion.2) | copy-start | bytes 2162692
  147.3 2.1 %copy-start.4 = (f32[8,128,256]{2,1,0:T(8,128)S(1)}, f32[8,128,256]{2,1,0:T(8,128)}, u32[]{:S(2)}) copy-start(f32[8,128,256]{2,1,0:T(8,128)} %get-tuple-element.12) | copy-start | bytes 3145732
  147.5 1.9 %slice-start = ((f32[8,176,128]{2,0,1:T(8,128)}), f32[8,172,128]{2,0,1:T(8,128)S(1)}, s32[]{:S(2)}) async-start(f32[8,176,128]{2,0,1:T(8,128)} %copy-done.2), calls=%async_computation.7 | async-start | bytes 1409024 | tf_op jit(solution)/shard_map/slice | solution.py:252
Sparse Core Ops, SparseCore 0:
  9.7 35.6 all-gather.1
  85.5 36.4 reduce-scatter.1
